TPU v7x, 128 devices: a whole 4x4x4 slice. The times are simulated.
128 devices in a mesh: dp: 2 (over z_hi), context: 16 (over z_lo, y, core), tensor: 4 (over x).
Axes of the slice: x: 4, y: 4, z: 4 (z_hi: 2, z_lo: 2; z = z_hi * 2 + z_lo), core: 2. Of those that a mesh axis runs over, the one named last changes fastest.
Arguments:
- streams: bfloat16 [4096, 3, 4096], P(('dp', 'context'), None, 'tensor'), parts along dimension 0, may hold values from -6 to 6
- stream_tail: bfloat16 [4, 3, 4096], P('dp', None, 'tensor'), parts along dimension 0, may hold values from -6 to 6
- short_taps: float32 [3, 3, 4096], P(None, None, 'tensor'), may hold values from -3 to 3
- decay_rates: float32 [16, 4096], P(None, 'tensor'), may hold values from 0.00012207031 to 0.05
- residues: float32 [16, 4096], P(None, 'tensor'), may hold values from -1.5 to 1.5
- hyena_state: float32 [32, 4096], P('dp', 'tensor'), parts along dimension 0, may hold values from -6 to 6
- skip_weight: float32 [4096], P('tensor'), may hold values from -4 to 4
- residual: bfloat16 [4096, 4096], P(('dp', 'context'), 'tensor'), parts along dimension 0, may hold values from -6 to 6
- norm_gain: float32 [4096], replicated, may hold values from 0.1 to 1.9
- qkv_weight: bfloat16 [4096, 3, 4096], P(None, None, 'tensor'), may hold values from -0.09375 to 0.09375
- start_offset: int32 [2], P('dp'), parts along dimension 0, may hold values from 2048 to 65535
- cache_keys: bfloat16 [4096, 4096], P(('dp', 'context'), 'tensor'), parts along dimension 0, may hold values from -300 to 300
- cache_values: bfloat16 [4096, 4096], P(('dp', 'context'), 'tensor'), parts along dimension 0, may hold values from -6 to 6
Outputs:
- attended: bfloat16 [4096, 4096], P(('dp', 'context'), 'tensor'), parts along dimension 0
There are 2 independent parts, one for each index of `dp`. A program takes and returns all parts, laid end to end along the dimension named above; an argument that names none is the same for every part. Nothing has to cross between parts.
All inputs are finite; a program needn't handle non-finite values.
Results may differ from a plain program's by a relative error of at most 0.04.
Values may be sent and summed in bfloat16 or wider, within the bound.
No kernel may reach another device: no remote copies, remote signals or barrier semaphores. Data moves between devices by JAX's collectives and lax.ppermute only.
A program may use at most 128 MiB of HBM per device.

v0:
```python
import math

import jax
import jax.numpy as jnp
from jax import lax
from jax.sharding import PartitionSpec as P

HEAD = 128


ROTARY_BASE = 1000000.0
NORM_EPSILON = 1e-06


def shifted(x, axis, by):
    devices = lax.axis_size(axis)
    pairs = [(i, i + by) for i in range(devices) if 0 <= i + by < devices]
    return lax.ppermute(x, axis, pairs)


def rotate(features, positions):
    half_width = features.shape[-1] // 2
    exponents = jnp.arange(half_width, dtype=jnp.float32) * (2.0 / features.shape[-1])
    frequency = jnp.exp(-math.log(ROTARY_BASE) * exponents)
    angles = positions[:, None] * frequency[None, :]
    cosine = jnp.cos(angles)[:, None, :]
    sine_values = jnp.sin(angles)[:, None, :]
    front = features[..., :half_width]
    back = features[..., half_width:]
    return jnp.concatenate(
        [front * cosine - back * sine_values, back * cosine + front * sine_values], axis=-1
    )


def modal_blocks(signal, incoming, mode_rates, mode_residues):
    length, channels = signal.shape
    mode_count = mode_rates.shape[0]
    block_len = math.gcd(length, 128)
    block_count = length // block_len
    mode_gain = jnp.sqrt(1.0 - jnp.exp(-2.0 * mode_rates))
    mode_decay = jnp.exp(-mode_rates)
    offsets = jnp.arange(block_len, dtype=jnp.float32)[:, None, None]
    falling = jnp.exp(-mode_rates[None] * offsets)
    rising = jnp.exp(mode_rates[None] * offsets)
    lower_ones = (jnp.arange(block_len)[:, None] >= jnp.arange(block_len)[None, :]).astype(
        jnp.float32
    )
    weighted = mode_residues[None] * falling

    def advance(carried, segment):
        scaled_terms = (rising * segment[:, None, :]).reshape(block_len, mode_count * channels)
        prefix_sums = jnp.dot(lower_ones, scaled_terms, precision=lax.Precision.HIGHEST).reshape(
            block_len, mode_count, channels
        )
        inner_state = mode_decay[None] * carried[None] + mode_gain[None] * prefix_sums
        output = jnp.sum(weighted * inner_state, axis=1)
        return (falling[-1] * inner_state[-1], output)

    final_state, outputs = lax.scan(
        advance, incoming, signal.reshape(block_count, block_len, channels)
    )
    return (outputs.reshape(length, channels), final_state)


def shards(
    streams,
    stream_tail,
    short_taps,
    decay_rates,
    residues,
    hyena_state,
    skip_weight,
    residual,
    norm_gain,
    qkv_weight,
    start_offset,
    cache_keys,
    cache_values,
):
    row_count = streams.shape[0]
    tap_count = short_taps.shape[0]
    device_index = lax.axis_index("context")
    before = shifted(streams[row_count - (tap_count - 1) :], "context", 1)
    before = jnp.where(device_index == 0, stream_tail, before)
    extended = jnp.concatenate([before, streams], axis=0).astype(jnp.float32)
    filtered = jnp.zeros(streams.shape, jnp.float32)
    for step_back in range(tap_count):
        begin = tap_count - 1 - step_back
        filtered = filtered + short_taps[step_back][None] * extended[begin : begin + row_count]
    product = (filtered[:, 0] * filtered[:, 2]).astype(jnp.bfloat16)
    spread = lax.all_to_all(product, "context", split_axis=1, concat_axis=0, tiled=True)
    narrow = spread.shape[1]
    first_channel = device_index * narrow
    part_rates = lax.dynamic_slice_in_dim(decay_rates, first_channel, narrow, 1)
    part_residues = lax.dynamic_slice_in_dim(residues, first_channel, narrow, 1)
    part_state = lax.dynamic_slice_in_dim(hyena_state, first_channel, narrow, 1)
    series = modal_blocks(spread.astype(jnp.float32), part_state, part_rates, part_residues)[0]
    long_out = lax.all_to_all(
        series.astype(jnp.bfloat16), "context", split_axis=0, concat_axis=1, tiled=True
    )
    hidden = (
        residual.astype(jnp.float32)
        + filtered[:, 1]
        * (long_out.astype(jnp.float32) + skip_weight[None, :] * product.astype(jnp.float32))
    ).astype(jnp.bfloat16)
    gathered = lax.all_gather(hidden, "tensor", axis=1, tiled=True)
    hidden_float = gathered.astype(jnp.float32)
    mean_square = jnp.mean(hidden_float * hidden_float, axis=1, keepdims=True)
    normed = (hidden_float * lax.rsqrt(mean_square + NORM_EPSILON) * norm_gain[None, :]).astype(
        jnp.bfloat16
    )
    head_width = qkv_weight.shape[2]
    heads_here = head_width // HEAD
    projected = jnp.dot(
        normed,
        qkv_weight.reshape(qkv_weight.shape[0], 3 * head_width),
        preferred_element_type=jnp.float32,
    ).reshape(row_count, 3, heads_here, HEAD)
    query_index = device_index * row_count + jnp.arange(row_count, dtype=jnp.int32)
    positions = (start_offset[0] + query_index).astype(jnp.float32)
    queries = rotate(projected[:, 0], positions).astype(jnp.bfloat16)
    new_keys = rotate(projected[:, 1], positions).astype(jnp.bfloat16)
    new_values = projected[:, 2].astype(jnp.bfloat16)
    cached_keys = cache_keys.reshape(-1, heads_here, HEAD)
    cached_values = cache_values.reshape(-1, heads_here, HEAD)
    hist_rows = cached_keys.shape[0]
    block_keys = jnp.concatenate([cached_keys, new_keys], axis=0)
    block_values = jnp.concatenate([cached_values, new_values], axis=0)
    span_rows = block_keys.shape[0]
    score_scale = 1.0 / math.sqrt(HEAD)
    row_top = jnp.full((heads_here, row_count), -1e30, jnp.float32)
    key_piece = lax.all_gather(block_keys, "context", axis=0, tiled=True)
    value_piece = lax.all_gather(block_values, "context", axis=0, tiled=True)
    piece_rows = key_piece.shape[0]
    key_index = jnp.arange(piece_rows, dtype=jnp.int32)
    owner_device = key_index // span_rows
    within = key_index % span_rows
    visible = (within < hist_rows)[None, :] | (
        (owner_device * row_count + within - hist_rows)[None, :] <= query_index[:, None]
    )
    scores = (
        jnp.einsum("qhd,khd->hqk", queries, key_piece, preferred_element_type=jnp.float32)
        * score_scale
    )
    masked = jnp.where(visible[None], scores, -1e30)
    new_top = jnp.maximum(row_top, jnp.max(masked, axis=2))
    weights = jnp.where(visible[None], jnp.exp(masked - new_top[..., None]), 0.0).astype(
        jnp.bfloat16
    )
    total_sum = jnp.sum(weights.astype(jnp.float32), axis=2)
    accumulated = jnp.einsum(
        "hqk,khd->hqd", weights, value_piece, preferred_element_type=jnp.float32
    )
    row_top, total_sum, accumulated = (new_top, total_sum, accumulated)
    attended = (
        (accumulated / total_sum[..., None])
        .transpose(1, 0, 2)
        .reshape(row_count, head_width)
        .astype(jnp.bfloat16)
    )
    return attended


def solution(mesh):
    placed = (
        P(("dp", "context"), None, "tensor"),
        P("dp", None, "tensor"),
        P(None, None, "tensor"),
        P(None, "tensor"),
        P(None, "tensor"),
        P("dp", "tensor"),
        P("tensor"),
        P(("dp", "context"), "tensor"),
        P(),
        P(None, None, "tensor"),
        P("dp"),
        P(("dp", "context"), "tensor"),
        P(("dp", "context"), "tensor"),
    )
    return jax.shard_map(
        shards,
        mesh=mesh,
        in_specs=placed,
        out_specs=P(("dp", "context"), "tensor"),
        check_vma=False,
    )
```

profile of v0, /device:TPU:1, one launch (start us, length us, event | category | flops | bytes accessed | tf_op | source)
XLA Modules:
  0.0 288.5 jit_solution(10391625576629821818)
XLA Ops:
  6.5 0.8 slice.59
  7.4 4.6 %collective-permute-start = (bf16[2,3,1024]{2,0,1:T(2,128)(2,1)S(1)}, bf16[2,3,1024]{2,0,1:T(2,128)(2,1)S(1)}, u32[]{:S(2)}, u32[]{:S(2)}) collective-permute-start(bf16[2,3,1024]{2,0,1:T(2,128)(2,1)S(1)} %slice.59), channel_id=1, source_target_pairs={{0,4},{4,8},{8,12},{12,16},{16,20},{20,24},{24,28},{28,32},{32,36}... | collective-permute-start | bytes 36872 | tf_op jit(solution)/shard_map/ppermute | solution.py:18
  13.6 1.5 copy.40
  15.1 1.2 copy.38
  17.4 2.4 fusion.14
  19.8 1.2 copy-done.3
  21.7 5.7 %all-to-all-start = ((bf16[128,16,64]{0,2,1:T(8,128)(2,1)}), bf16[128,16,64]{0,2,1:T(8,128)(2,1)S(1)}, u32[]{:S(2)}, u32[]{:S(2)}) async-start(bf16[128,16,64]{0,2,1:T(8,128)(2,1)} %bitcast.4), calls=%async_computation | async-start | bytes 524288 | tf_op jit(solution)/shard_map/all_to_all | solution.py:91
  27.7 6.9 %all-to-all-done = bf16[128,16,64]{0,2,1:T(8,128)(2,1)S(1)} async-done(((bf16[128,16,64]{0,2,1:T(8,128)(2,1)}), bf16[128,16,64]{0,2,1:T(8,128)(2,1)S(1)}, u32[]{:S(2)}, u32[]{:S(2)}) %all-to-all-start) | async-done | bytes 262176 | tf_op jit(solution)/shard_map/all_to_all | solution.py:91
  34.6 48.4 %while.13 = (s32[]{:T(128)}, f32[16,64]{1,0:T(8,128)S(1)}, bf16[16,128,64]{1,2,0:T(8,128)(2,1)}, f32[128,16,64]{0,2,1:T(8,128)S(1)}, f32[16,64]{1,0:T(8,128)S(1)...) while((s32[]{:T(128)}, f32[16,64]{1,0:T(8,128)S(1)}, ...), condition=%wide.region_2.3_spmd.clone, body=%wide.region_0.2_spmd.clone.sunk | while | flops 202401792 | bytes 4944497 | solution.py:59
  83.0 4.1 %all-to-all-start.1 = ((bf16[16,128,64]{1,2,0:T(8,128)(2,1)}), bf16[16,128,64]{1,2,0:T(8,128)(2,1)S(1)}, u32[]{:S(2)}, u32[]{:S(2)}) async-start(bf16[16,128,64]{1,2,0:T(8,128)(2,1)} %get-tuple-element.57), calls=%async_computation.1 | async-start | bytes 524288 | tf_op jit(solution)/shard_map/all_to_all | solution.py:98
  87.3 7.0 %all-to-all-done.1 = bf16[16,128,64]{1,2,0:T(8,128)(2,1)S(1)} async-done(((bf16[16,128,64]{1,2,0:T(8,128)(2,1)}), bf16[16,128,64]{1,2,0:T(8,128)(2,1)S(1)}, u32[]{:S(2)}, u32[]{:S(2)}) %all-to-all-start.1) | async-done | bytes 262176 | tf_op jit(solution)/shard_map/all_to_all | solution.py:98
  94.4 2.3 fusion.26
  96.7 33.6 %copy.42 = bf16[4096,3,1024]{0,2,1:T(8,128)(2,1)} copy(bf16[4096,3,1024]{2,0,1:T(8,128)(2,1)} %param.24) | data formatting | bytes 50331648 | tf_op args[9]
  131.4 1.8 fusion.11
  133.2 12.0 %fusion.19 = f32[128,3,8,128]{0,3,2,1:T(8,128)S(1)} fusion(bf16[3,8,128,4096]{3,2,1,0:T(8,128)(2,1)} %bitcast.75, bf16[128,4096]{0,1:T(8,128)(2,1)} %all-gather.4.cloned.1.call-done, f32[4096]{0:T(1024)S(1)} %copy-done.7, f32[128]{0:T(128)S(1)} %add_rsqrt_fusion), kind=kOutput, calls=%fused_computation.34 | convolution fusion | flops 3223322624 | bytes 27804160 | tf_op jit(solution)/shard_map/dot_general | solution.py:114
  145.5 0.9 maximum_maximum_fusion
  146.9 0.9 pad_maximum_fusion
  148.3 59.5 %all-gather.6.cloned.1.call-done = bf16[4096,8,128]{0,2,1:T(8,128)(2,1)} async-done(((bf16[256,8,128]{0,2,1:T(8,128)(2,1)}), bf16[4096,8,128]{0,2,1:T(8,128)(2,1)}) %all-gather.6.cloned.1.call-update) | async-done | bytes 8388624 | tf_op jit(solution)/shard_map/all_gather | solution.py:132
  207.8 6.3 %fusion.10 = (f32[8,128]{1,0:T(8,128)S(1)}, f32[8,128,4096]{2,1,0:T(8,128)S(1)}) fusion(pred[128,4096]{1,0:T(8,128)(4,1)S(1)} %compare_or_fusion, bf16[4096,8,128]{0,2,1:T(8,128)(2,1)} %all-gather.6.cloned.1.call-done, bf16[128,8,64]{0,2,1:T(8,128)(2,1)S(1)} %get-tuple-element.112, bf16[128,8,64]{0,2,1:T(8,128)(2,1)S(1)} %get-tuple-element.111), kind=kOutput, calls=%fused_computation.17 | convolution fusion | flops 1086848000 | bytes 25956352 | tf_op jit(solution)/shard_map/qhd,khd->hqk/dot_general | solution.py:142
  214.1 5.9 %copy-done.2 = f32[8,128,4096]{2,1,0:T(8,128)} copy-done((f32[8,128,4096]{2,1,0:T(8,128)}, f32[8,128,4096]{2,1,0:T(8,128)S(1)}, u32[]{:S(2)}) %copy-start.2) | copy-done | bytes 16777240
  219.9 5.4 %convert_reduce_fusion = f32[8,128]{1,0:T(8,128)S(1)} fusion(f32[8,128]{1,0:T(8,128)S(1)} %broadcast_maximum_fusion, f32[8,128,4096]{2,1,0:T(8,128)S(1)} %get-tuple-element.125, pred[128,4096]{1,0:T(8,128)(4,1)S(1)} %compare_or_fusion), kind=kLoop, calls=%fused_computation.14 | loop fusion | flops 29359104 | bytes 17309696 | tf_op jit(solution)/shard_map/reduce_sum | solution.py:150
  225.3 44.9 %all-gather.8.cloned.1.call-done = bf16[4096,8,128]{0,2,1:T(8,128)(2,1)} async-done(((bf16[256,8,128]{0,2,1:T(8,128)(2,1)}), bf16[4096,8,128]{0,2,1:T(8,128)(2,1)}) %all-gather.8.cloned.1.call-update) | async-done | bytes 8388624 | tf_op jit(solution)/shard_map/all_gather | solution.py:133
  270.3 10.8 %fusion.17 = bf16[128,8,128]{0,2,1:T(8,128)(2,1)S(1)} fusion(bf16[4096,8,128]{0,2,1:T(8,128)(2,1)} %all-gather.8.cloned.1.call-done, f32[128,8]{0,1:T(8,128)S(1)} %bitcast.82, f32[8,128,4096]{2,1,0:T(8,128)} %copy-done.2, f32[8,128]{1,0:T(8,128)S(1)} %broadcast_maximum_fusion, pred[128,4096]{1,0:T(8,128)(4,1)S(1)} %compare_or_fusion), kind=kOutput, calls=%fused_computation.32 | convolution fusion | flops 1094975488 | bytes 25960448 | tf_op jit(solution)/shard_map/hqk,khd->hqd/dot_general | solution.py:151
  281.1 0.9 copy.48
  (210 shorter events, 52.8 us)
Async XLA Ops:
  6.5 20.8 %copy-start = (f32[16,1024]{1,0:T(8,128)S(1)}, f32[16,1024]{1,0:T(8,128)}, u32[]{:S(2)}) copy-start(f32[16,1024]{1,0:T(8,128)} %param.20) | copy-start | bytes 196612
  7.4 8.9 %collective-permute-start = (bf16[2,3,1024]{2,0,1:T(2,128)(2,1)S(1)}, bf16[2,3,1024]{2,0,1:T(2,128)(2,1)S(1)}, u32[]{:S(2)}, u32[]{:S(2)}) collective-permute-start(bf16[2,3,1024]{2,0,1:T(2,128)(2,1)S(1)} %slice.59), channel_id=1, source_target_pairs={{0,4},{4,8},{8,12},{12,16},{16,20},{20,24},{24,28},{28,32},{32,36}... | collective-permute-start | bytes 36872 | tf_op jit(solution)/shard_map/ppermute | solution.py:18
  19.8 1.2 copy-start.3
  21.7 12.9 %all-to-all-start = ((bf16[128,16,64]{0,2,1:T(8,128)(2,1)}), bf16[128,16,64]{0,2,1:T(8,128)(2,1)S(1)}, u32[]{:S(2)}, u32[]{:S(2)}) async-start(bf16[128,16,64]{0,2,1:T(8,128)(2,1)} %bitcast.4), calls=%async_computation | async-start | bytes 524288 | tf_op jit(solution)/shard_map/all_to_all | solution.py:91
  34.6 52.6 %copy-start.4 = (bf16[128,1024]{1,0:T(8,128)(2,1)S(1)}, bf16[128,1024]{1,0:T(8,128)(2,1)}, u32[]{:S(2)}) copy-start(bf16[128,1024]{1,0:T(8,128)(2,1)} %param.22) | copy-start | bytes 786436
  34.6 59.8 %copy-start.8 = (f32[1024]{0:T(1024)S(1)}, f32[1024]{0:T(1024)}, u32[]{:S(2)}) copy-start(f32[1024]{0:T(1024)} %param.21) | copy-start | bytes 12292
  83.0 11.3 %all-to-all-start.1 = ((bf16[16,128,64]{1,2,0:T(8,128)(2,1)}), bf16[16,128,64]{1,2,0:T(8,128)(2,1)S(1)}, u32[]{:S(2)}, u32[]{:S(2)}) async-start(bf16[16,128,64]{1,2,0:T(8,128)(2,1)} %get-tuple-element.57), calls=%async_computation.1 | async-start | bytes 524288 | tf_op jit(solution)/shard_map/all_to_all | solution.py:98
  87.1 44.3 %all-gather.4.cloned.1.call-start = ((), (), s32[]{:S(2)}) async-start(), calls=%async_computation.2 | async-start | bytes 1310720 | tf_op jit(solution)/shard_map/all_gather | solution.py:106
  96.7 34.3 %copy-start.5 = (bf16[128,1024]{1,0:T(8,128)(2,1)S(1)}, bf16[128,1024]{1,0:T(8,128)(2,1)}, u32[]{:S(2)}) copy-start(bf16[128,1024]{1,0:T(8,128)(2,1)} %param.26) | copy-start | bytes 786436
  96.7 36.5 %copy-start.7 = (f32[4096]{0:T(1024)S(1)}, f32[4096]{0:T(1024)}, u32[]{:S(2)}) copy-start(f32[4096]{0:T(1024)} %param.23) | copy-start | bytes 49156
  96.7 111.1 %all-gather.6.cloned.1.call-start = ((), (), s32[]{:S(2)}) async-start(), calls=%async_computation.3 | async-start | bytes 8912896 | tf_op jit(solution)/shard_map/all_gather | solution.py:132
  133.2 13.5 %copy-start.6 = (bf16[128,1024]{1,0:T(8,128)(2,1)S(1)}, bf16[128,1024]{1,0:T(8,128)(2,1)}, u32[]{:S(2)}) copy-start(bf16[128,1024]{1,0:T(8,128)(2,1)} %param.27) | copy-start | bytes 786436
  146.4 123.9 %all-gather.8.cloned.1.call-start = ((), (), s32[]{:S(2)}) async-start(), calls=%async_computation.4 | async-start | bytes 8912896 | tf_op jit(solution)/shard_map/all_gather | solution.py:133
  214.1 5.9 %copy-start.2 = (f32[8,128,4096]{2,1,0:T(8,128)}, f32[8,128,4096]{2,1,0:T(8,128)S(1)}, u32[]{:S(2)}) copy-start(f32[8,128,4096]{2,1,0:T(8,128)S(1)} %get-tuple-element.125) | copy-start | bytes 50331652
  270.3 11.7 %copy-start.1 = (f32[16,1024]{1,0:T(8,128)S(1)}, f32[16,1024]{1,0:T(8,128)}, u32[]{:S(2)}) copy-start(f32[16,1024]{1,0:T(8,128)} %param.20) | copy-start | bytes 196612
Sparse Core Ops, SparseCore 0:
  96.8 21.6 all-gather.3
  146.6 61.1 all-gather.5
  209.4 60.8 all-gather.7
where the time goes:
time: 290 us; the launch traced here: 288 us
  waiting for transfers between devices  118 us (41%)
  local copies, waits for them, and re-layouts  74.2 us (26%)
  matrix products  38.6 us (13%)
  other arithmetic  27.3 us (9%)
  starting transfers between devices  14.6 us (5%)
  between operations  14.1 us (5%)
    all_gather x1, waiting for transfers between devices, shards(): key_piece = lax.all_gather(block_keys, 'context', axis=0, tiled=True)  59.5 us
    all_gather x1, waiting for transfers between devices, shards(): value_piece = lax.all_gather(block_values, 'context', axis=0, tiled=True)  44.9 us
    unnamed x24, local copies, waits for them, and re-layouts  43.8 us
    dot_general x1, matrix products, shards(): jnp.dot(normed, qkv_weight.reshape(qkv_weight.shape[0], 3 * head_width),...  12 us
    dynamic_update_slice x32, local copies, waits for them, and re-layouts, modal_blocks(): lax.scan(advance, incoming, signal.reshape(block_count, block_len, channe...  11.3 us
    dot_general x1, matrix products, shards(): jnp.einsum('hqk,khd->hqd', weights, value_piece, preferred_element_type=j...  10.8 us
    dot_general x16, matrix products, advance(): jnp.dot(lower_ones, scaled_terms, precision=lax.Precision.HIGHEST)  9.5 us
    reshape x16, local copies, waits for them, and re-layouts, advance(): jnp.dot(lower_ones, scaled_terms, precision=lax.Precision.HIGHEST)  7.93 us
  transfers between devices with their start and end apart: 6, of which 4 were waited for; matrix products, arithmetic and copies ran while one was open for 18% of the time, Pallas kernels for 0%

commit v1 on v0

v1 whole, which is shorter than its diff:
```python
import math

import jax
import jax.numpy as jnp
from jax import lax
from jax.sharding import PartitionSpec as P

HEAD = 128


ROTARY_BASE = 1000000.0
NORM_EPSILON = 1e-06


def shifted(x, axis, by):
    devices = lax.axis_size(axis)
    pairs = [(i, i + by) for i in range(devices) if 0 <= i + by < devices]
    return lax.ppermute(x, axis, pairs)


def rotate(features, positions):
    half_width = features.shape[-1] // 2
    exponents = jnp.arange(half_width, dtype=jnp.float32) * (2.0 / features.shape[-1])
    frequency = jnp.exp(-math.log(ROTARY_BASE) * exponents)
    angles = positions[:, None] * frequency[None, :]
    cosine = jnp.cos(angles)[:, None, :]
    sine_values = jnp.sin(angles)[:, None, :]
    front = features[..., :half_width]
    back = features[..., half_width:]
    return jnp.concatenate(
        [front * cosine - back * sine_values, back * cosine + front * sine_values], axis=-1
    )


def modal_chunk(signal, mode_rates, mode_residues, hyena_state, device_index, devices):
    length, channels = signal.shape
    mode_count = mode_rates.shape[0]
    mode_gain = jnp.sqrt(1.0 - jnp.exp(-2.0 * mode_rates))
    offsets = jnp.arange(length, dtype=jnp.float32)[:, None, None]
    rising = jnp.exp(mode_rates[None] * offsets)
    lower_ones = (jnp.arange(length)[:, None] >= jnp.arange(length)[None, :]).astype(jnp.float32)
    scaled_terms = (rising * signal[:, None, :]).reshape(length, mode_count * channels)
    prefix_sums = jnp.dot(lower_ones, scaled_terms, precision=lax.Precision.HIGH).reshape(
        length, mode_count, channels
    )
    falling = jnp.exp(-mode_rates[None] * offsets)
    local_out = jnp.sum((mode_residues * mode_gain)[None] * falling * prefix_sums, axis=1)
    final_local = mode_gain * jnp.exp(-mode_rates * (length - 1)) * prefix_sums[-1]
    finals = lax.all_gather(final_local, "context", axis=0, tiled=False)
    source = jnp.arange(devices, dtype=jnp.int32)
    steps = (device_index - 1 - source).astype(jnp.float32)
    carry_weight = jnp.where(
        (source < device_index)[:, None, None],
        jnp.exp(-mode_rates[None] * (length * jnp.maximum(steps, 0.0))[:, None, None]),
        0.0,
    )
    incoming = jnp.exp(-mode_rates * (length * device_index.astype(jnp.float32))) * hyena_state
    incoming = incoming + jnp.sum(carry_weight * finals, axis=0)
    carried = jnp.sum(
        (mode_residues * incoming)[None] * jnp.exp(-mode_rates[None] * (offsets + 1.0)), axis=1
    )
    return local_out + carried


def shards(
    streams,
    stream_tail,
    short_taps,
    decay_rates,
    residues,
    hyena_state,
    skip_weight,
    residual,
    norm_gain,
    qkv_weight,
    start_offset,
    cache_keys,
    cache_values,
):
    row_count = streams.shape[0]
    tap_count = short_taps.shape[0]
    devices = lax.axis_size("context")
    device_index = lax.axis_index("context")
    head_width = qkv_weight.shape[2]
    heads_here = head_width // HEAD
    half_rows = row_count // 2

    def by_head(block):
        per_head = block.reshape(row_count, heads_here, HEAD).transpose(1, 0, 2)
        return jnp.repeat(per_head, devices // heads_here, axis=0)

    cache_k = lax.all_to_all(by_head(cache_keys), "context", 0, 0, tiled=True)
    cache_v = lax.all_to_all(by_head(cache_values), "context", 0, 0, tiled=True)

    before = shifted(streams[row_count - (tap_count - 1) :], "context", 1)
    before = jnp.where(device_index == 0, stream_tail, before)
    extended = jnp.concatenate([before, streams], axis=0).astype(jnp.float32)
    filtered = jnp.zeros(streams.shape, jnp.float32)
    for step_back in range(tap_count):
        begin = tap_count - 1 - step_back
        filtered = filtered + short_taps[step_back][None] * extended[begin : begin + row_count]
    product = (filtered[:, 0] * filtered[:, 2]).astype(jnp.bfloat16)
    long_out = modal_chunk(
        product.astype(jnp.float32), decay_rates, residues, hyena_state, device_index, devices
    ).astype(jnp.bfloat16)
    hidden = (
        residual.astype(jnp.float32)
        + filtered[:, 1]
        * (long_out.astype(jnp.float32) + skip_weight[None, :] * product.astype(jnp.float32))
    ).astype(jnp.bfloat16)
    gathered = lax.all_gather(hidden, "tensor", axis=1, tiled=True)
    hidden_float = gathered.astype(jnp.float32)
    mean_square = jnp.mean(hidden_float * hidden_float, axis=1, keepdims=True)
    normed = (hidden_float * lax.rsqrt(mean_square + NORM_EPSILON) * norm_gain[None, :]).astype(
        jnp.bfloat16
    )
    projected = jnp.einsum(
        "pk,kgn->pgn", normed, qkv_weight, preferred_element_type=jnp.float32
    ).reshape(row_count, 3, heads_here, HEAD)
    query_index = device_index * row_count + jnp.arange(row_count, dtype=jnp.int32)
    positions = (start_offset[0] + query_index).astype(jnp.float32)
    queries = rotate(projected[:, 0], positions).astype(jnp.bfloat16)
    new_keys = rotate(projected[:, 1], positions).astype(jnp.bfloat16)
    new_values = projected[:, 2].astype(jnp.bfloat16)

    new_k = lax.all_to_all(by_head(new_keys), "context", 0, 0, tiled=True)
    new_v = lax.all_to_all(by_head(new_values), "context", 0, 0, tiled=True)
    query_parts = (
        queries.reshape(2, half_rows, heads_here, HEAD)
        .transpose(2, 0, 1, 3)
        .reshape(devices, half_rows, HEAD)
    )
    my_queries = lax.all_to_all(query_parts, "context", 0, 0, tiled=True)

    hist_rows = cache_k.shape[0] * cache_k.shape[1]
    all_k = jnp.concatenate([cache_k.reshape(-1, HEAD), new_k.reshape(-1, HEAD)], axis=0)
    all_v = jnp.concatenate([cache_v.reshape(-1, HEAD), new_v.reshape(-1, HEAD)], axis=0)
    q_flat = my_queries.reshape(-1, HEAD)
    key_index = jnp.arange(all_k.shape[0], dtype=jnp.int32)
    key_pos = jnp.where(key_index < hist_rows, -1, key_index - hist_rows)
    src = jnp.arange(devices, dtype=jnp.int32)[:, None]
    row = jnp.arange(half_rows, dtype=jnp.int32)[None, :]
    query_pos = (src * row_count + (device_index % 2) * half_rows + row).reshape(-1)
    visible = key_pos[None, :] <= query_pos[:, None]
    score_scale = 1.0 / math.sqrt(HEAD)
    scores = (
        jnp.einsum("qd,kd->qk", q_flat, all_k, preferred_element_type=jnp.float32) * score_scale
    )
    row_max = jnp.max(jnp.where(visible, scores, -jnp.inf), axis=1, keepdims=True)
    weights = jnp.where(visible, jnp.exp(scores - row_max), 0.0).astype(jnp.bfloat16)
    weight_sum = jnp.sum(weights.astype(jnp.float32), axis=1, keepdims=True)
    numerator = jnp.dot(weights, all_v, preferred_element_type=jnp.float32)
    mine = (numerator / weight_sum).astype(jnp.bfloat16).reshape(devices, half_rows, HEAD)
    back = lax.all_to_all(mine, "context", 0, 0, tiled=True)
    attended = (
        back.reshape(heads_here, 2, half_rows, HEAD)
        .transpose(1, 2, 0, 3)
        .reshape(row_count, head_width)
    )
    return attended


def solution(mesh):
    placed = (
        P(("dp", "context"), None, "tensor"),
        P("dp", None, "tensor"),
        P(None, None, "tensor"),
        P(None, "tensor"),
        P(None, "tensor"),
        P("dp", "tensor"),
        P("tensor"),
        P(("dp", "context"), "tensor"),
        P(),
        P(None, None, "tensor"),
        P("dp"),
        P(("dp", "context"), "tensor"),
        P(("dp", "context"), "tensor"),
    )
    return jax.shard_map(
        shards,
        mesh=mesh,
        in_specs=placed,
        out_specs=P(("dp", "context"), "tensor"),
        check_vma=False,
    )
```

time: 290 us -> 202 us (0.70)
  waiting for transfers between devices: 118 us -> 52.5 us
  local copies, waits for them, and re-layouts: 74.2 us -> 33.3 us
  starting transfers between devices: 14.6 us -> 31.6 us
  blocking collectives: 0 us -> 12.7 us
  matrix products: 38.6 us -> 29.3 us
    all_gather x2 -> x1, waiting for transfers between devices: 104 us -> 20.7 us  [modal_chunk(): finals = lax.all_gather(final_local, 'context', axis=0, tiled=False)]
    unnamed x24 -> x27, local copies, waits for them, and re-layouts: 43.8 us -> 26.2 us
    all_to_all x2 -> x5, starting transfers between devices: 9.74 us -> 26.8 us  [the longest x1 8.05 us: shards(): my_queries = lax.all_to_all(query_parts, 'context', 0, 0, tiled=True)]
    all_gather x1, waiting for transfers between devices: 0.02 us -> 15.4 us  [shards(): gathered = lax.all_gather(hidden, 'tensor', axis=1, tiled=True)]
    all_to_all x0 -> x1, blocking collectives: none -> 12.7 us  [shards(): back = lax.all_to_all(mine, 'context', 0, 0, tiled=True)]
    dynamic_update_slice x32 -> x0, local copies, waits for them, and re-layouts: 11.3 us -> none  [modal_blocks(): lax.scan(advance, incoming, signal.reshape(block_count, block_len, channe...]
    dot_general x19 -> x4, matrix products: 38.6 us -> 29.3 us  [the longest x1 10.3 us: shards(): jnp.einsum('pk,kgn->pgn', normed, qkv_weight, preferred_element_type=jnp....]
    while x16 -> x0, local copies, waits for them, and re-layouts: 7.91 us -> none
  transfers between devices with their start and end apart: 6 -> 8, of which waited for: 4 -> 5; matrix products, arithmetic and copies ran while one was open for 18% -> 25% of each run, Pallas kernels for 0% -> 0%
where the time goes in v1:
time: 202 us; the launch traced here: 201 us
  waiting for transfers between devices  52.5 us (26%)
  local copies, waits for them, and re-layouts  33.3 us (16%)
  starting transfers between devices  31.6 us (16%)
  matrix products  29.3 us (15%)
  other arithmetic  26.7 us (13%)
  between operations  14.4 us (7%)
  blocking collectives  12.7 us (6%)
    unnamed x27, local copies, waits for them, and re-layouts  26.2 us
    all_gather x1, waiting for transfers between devices, modal_chunk(): finals = lax.all_gather(final_local, 'context', axis=0, tiled=False)  20.7 us
    all_gather x1, waiting for transfers between devices, shards(): gathered = lax.all_gather(hidden, 'tensor', axis=1, tiled=True)  15.4 us
    all_to_all x1, blocking collectives, shards(): back = lax.all_to_all(mine, 'context', 0, 0, tiled=True)  12.7 us
    reduce_sum x1, other arithmetic, shards(): weight_sum = jnp.sum(weights.astype(jnp.float32), axis=1, keepdims=True)  10.7 us
    dot_general x1, matrix products, shards(): jnp.einsum('pk,kgn->pgn', normed, qkv_weight, preferred_element_type=jnp....  10.3 us
    dot_general x1, matrix products, shards(): jnp.einsum('qd,kd->qk', q_flat, all_k, preferred_element_type=jnp.float32)  9.44 us
    all_to_all x1, waiting for transfers between devices, shards(): new_k = lax.all_to_all(by_head(new_keys), 'context', 0, 0, tiled=True)  9.26 us
  transfers between devices with their start and end apart: 8, of which 5 were waited for; matrix products, arithmetic and copies ran while one was open for 25% of the time, Pallas kernels for 0%

profile of v1, /device:TPU:1, one launch (start us, length us, event | category | flops | bytes accessed | tf_op | source)
XLA Modules:
  0.0 200.6 jit_solution(16627792065399232558)
XLA Ops:
  7.4 4.6 %collective-permute-start = (bf16[2,3,1024]{2,0,1:T(2,128)(2,1)S(1)}, bf16[2,3,1024]{2,0,1:T(2,128)(2,1)S(1)}, u32[]{:S(2)}, u32[]{:S(2)}) collective-permute-start(bf16[2,3,1024]{2,0,1:T(2,128)(2,1)S(1)} %slice.57), channel_id=1, source_target_pairs={{0,4},{4,8},{8,12},{12,16},{16,20},{20,24},{24,28},{28,32},{32,36}... | collective-permute-start | bytes 36872 | tf_op jit(solution)/shard_map/ppermute | solution.py:18
  13.6 1.4 maximum_convert_fusion
  15.5 1.1 mul.336
  16.6 7.1 %copy.27 = f32[16,8,16,1024]{3,1,2,0:T(8,128)S(1)} copy(f32[16,8,16,1024]{3,2,1,0:T(8,128)S(1)} %bitcast.87) | data formatting | bytes 16777216
  23.8 3.9 %fusion.3 = f32[128,16384]{1,0:T(8,128)S(1)} fusion(f32[128,16384]{1,0:T(8,128)S(1)} %bitcast.86, f32[16384]{0:T(1024)S(1)} %bitcast.103), kind=kOutput, calls=%fused_computation.8 | convolution fusion | flops 1614823424 | bytes 16842752 | tf_op jit(solution)/shard_map/dot_general | solution.py:43
  27.7 3.2 %copy-done = f32[128,16384]{1,0:T(8,128)} copy-done((f32[128,16384]{1,0:T(8,128)}, f32[128,16384]{1,0:T(8,128)S(1)}, u32[]{:S(2)}) %copy-start) | copy-done | bytes 8388632
  32.1 13.8 %copy.28 = f32[16,8,16,1024]{3,2,1,0:T(8,128)} copy(f32[16,8,16,1024]{3,1,2,0:T(8,128)} %bitcast.85) | data formatting | bytes 16777216
  45.9 20.7 %all-gather.6.cloned.1.call-done = f32[256,1024]{1,0:T(8,128)} async-done(((f32[16,1024]{1,0:T(8,128)}), f32[256,1024]{1,0:T(8,128)}) %all-gather.6.cloned.1.call-update) | async-done | bytes 1048592 | tf_op jit(solution)/shard_map/all_gather | solution.py:49
  66.6 1.5 multiply_reduce_fusion.1
  68.2 7.3 %multiply_reduce_fusion = (f32[128,1024]{1,0:T(8,128)S(1)}, f32[128,1024]{1,0:T(8,128)S(1)}) fusion(f32[128]{0:T(128)S(1)} %iota_add_fusion.2, f32[16,1024]{1,0:T(8,128)S(1)} %get-tuple-element.18, f32[16,1024]{1,0:T(8,128)S(1)} %get-tuple-element.19, f32[16,8,16,1024]{3,2,1,0:T(8,128)} %copy.28, f32[16,1024]{1,0:T(8,128)S(1)} %get-tuple-element.17), kind=kLoop, calls=%fused_computation.7 | loop fusion | flops 14417920 | bytes 9634304 | tf_op jit(solution)/shard_map/reduce_sum | solution.py:59
  77.7 4.2 %all-to-all-start.1 = ((bf16[16,128,128]{2,1,0:T(8,128)(2,1)}), bf16[16,128,128]{2,1,0:T(8,128)(2,1)S(1)}, u32[]{:S(2)}, u32[]{:S(2)}) async-start(bf16[16,128,128]{2,1,0:T(8,128)(2,1)} %bitcast.16), calls=%async_computation.1 | async-start | bytes 1048576 | tf_op jit(solution)/shard_map/all_to_all | solution.py:92
  82.8 15.4 %all-gather.4.cloned.1.call-done = bf16[128,4096]{1,0:T(8,128)(2,1)} async-done(((bf16[128,1024]{1,0:T(8,128)(2,1)}), bf16[128,4096]{1,0:T(8,128)(2,1)}) %all-gather.4.cloned.1.call-update) | async-done | bytes 1048592 | tf_op jit(solution)/shard_map/all_gather | solution.py:111
  98.2 1.5 fusion.9
  99.8 10.3 %fusion.16 = f32[128,3,1024]{2,0,1:T(8,128)S(1)} fusion(bf16[4096,3,1024]{2,0,1:T(8,128)(2,1)} %param.22, bf16[128,4096]{1,0:T(8,128)(2,1)} %all-gather.4.cloned.1.call-done, f32[4096]{0:T(1024)S(1)} %copy-done.6, f32[128]{0:T(128)S(1)} %add_rsqrt_fusion), kind=kOutput, calls=%fused_computation.27 | convolution fusion | flops 3223322624 | bytes 27804160 | tf_op jit(solution)/shard_map/pk,kgn->pgn/dot_general | solution.py:117
  112.0 8.0 %all-to-all-start = ((bf16[16,64,128]{2,1,0:T(8,128)(2,1)}), bf16[16,64,128]{2,1,0:T(8,128)(2,1)S(1)}, u32[]{:S(2)}, u32[]{:S(2)}) async-start(bf16[16,64,128]{2,1,0:T(8,128)(2,1)} %bitcast.13), calls=%async_computation | async-start | bytes 524288 | tf_op jit(solution)/shard_map/all_to_all | solution.py:133
  120.2 7.0 %all-to-all-done = bf16[16,64,128]{2,1,0:T(8,128)(2,1)S(1)} async-done(((bf16[16,64,128]{2,1,0:T(8,128)(2,1)}), bf16[16,64,128]{2,1,0:T(8,128)(2,1)S(1)}, u32[]{:S(2)}, u32[]{:S(2)}) %all-to-all-start) | async-done | bytes 262176 | tf_op jit(solution)/shard_map/all_to_all | solution.py:133
  128.1 4.1 %all-to-all-start.2 = ((bf16[16,128,128]{2,1,0:T(8,128)(2,1)}), bf16[16,128,128]{2,1,0:T(8,128)(2,1)S(1)}, u32[]{:S(2)}, u32[]{:S(2)}) async-start(bf16[16,128,128]{2,1,0:T(8,128)(2,1)} %bitcast.20), calls=%async_computation.2 | async-start | bytes 1048576 | tf_op jit(solution)/shard_map/all_to_all | solution.py:126
  132.6 9.3 %all-to-all-done.2 = bf16[16,128,128]{2,1,0:T(8,128)(2,1)S(1)} async-done(((bf16[16,128,128]{2,1,0:T(8,128)(2,1)}), bf16[16,128,128]{2,1,0:T(8,128)(2,1)S(1)}, u32[]{:S(2)}, u32[]{:S(2)}) %all-to-all-start.2) | async-done | bytes 524320 | tf_op jit(solution)/shard_map/all_to_all | solution.py:126
  142.7 4.8 %all-to-all-start.3 = ((bf16[16,128,128]{2,1,0:T(8,128)(2,1)}), bf16[16,128,128]{2,1,0:T(8,128)(2,1)S(1)}, u32[]{:S(2)}, u32[]{:S(2)}) async-start(bf16[16,128,128]{2,1,0:T(8,128)(2,1)} %bitcast.23), calls=%async_computation.3 | async-start | bytes 1048576 | tf_op jit(solution)/shard_map/all_to_all | solution.py:93
  147.5 9.4 %fusion = (f32[1024]{0:T(1024)S(1)}, f32[1024,4096]{1,0:T(8,128)}) fusion(s32[4096]{0:T(1024)S(1)} %fusion.35, s32[1024]{0:T(1024)S(1)} %add.113, bf16[1024,128]{1,0:T(8,128)(2,1)} %bitcast.106, bf16[2048,128]{1,0:T(8,128)(2,1)S(1)} %bitcast.101, bf16[2048,128]{1,0:T(8,128)(2,1)S(1)} %bitcast.99), kind=kOutput, calls=%fused_computation.2 | convolution fusion | flops 1092615168 | bytes 18112512 | tf_op jit(solution)/shard_map/qd,kd->qk/dot_general | solution.py:147
  158.0 5.6 %all-to-all-start.4 = ((bf16[16,128,128]{2,1,0:T(8,128)(2,1)}), bf16[16,128,128]{2,1,0:T(8,128)(2,1)S(1)}, u32[]{:S(2)}, u32[]{:S(2)}) async-start(bf16[16,128,128]{2,1,0:T(8,128)(2,1)} %bitcast.27), calls=%async_computation.4 | async-start | bytes 1048576 | tf_op jit(solution)/shard_map/all_to_all | solution.py:127
  163.7 10.7 %convert_reduce_fusion = (f32[1024]{0:T(1024)S(1)}, bf16[1024,4096]{1,0:T(8,128)(2,1)}) fusion(f32[1024]{0:T(1024)S(1)} %get-tuple-element.26, f32[1024,4096]{1,0:T(8,128)} %get-tuple-element.27, s32[1024]{0:T(1024)S(1)} %add.113, s32[4096]{0:T(1024)S(1)} %fusion.35), kind=kLoop, calls=%fused_computation.4 | loop fusion | flops 29359104 | bytes 25194496 | tf_op jit(solution)/shard_map/reduce_sum | solution.py:151
  174.4 5.7 %fusion.14 = bf16[1024,128]{1,0:T(8,128)(2,1)S(1)} fusion(bf16[1024,4096]{1,0:T(8,128)(2,1)} %get-tuple-element.8, bf16[2048,128]{1,0:T(8,128)(2,1)S(1)} %bitcast.102, bf16[2048,128]{1,0:T(8,128)(2,1)S(1)} %bitcast.100, f32[1024]{0:T(1024)S(1)} %get-tuple-element.7), kind=kOutput, calls=%fused_computation.25 | convolution fusion | flops 1076101120 | bytes 9703424 | tf_op jit(solution)/shard_map/dot_general | solution.py:152
  180.1 12.7 %all_to_all.30 = bf16[16,64,128]{2,1,0:T(8,128)(2,1)S(1)} all-to-all(bf16[16,64,128]{2,1,0:T(8,128)(2,1)S(1)} %bitcast.107), channel_id=1, replica_groups=mesh['dp'=2,'context'=16,'tensor'=4] {'context'}, dimensions={0} | all-to-all | bytes 524288 | tf_op jit(solution)/shard_map/all_to_all | solution.py:154
  (69 shorter events, 12.7 us)
Async XLA Ops:
  6.5 60.1 %all-gather.6.cloned.1.call-start = ((), (), s32[]{:S(2)}) async-start(), calls=%async_computation.7 | async-start | bytes 1114112 | tf_op jit(solution)/shard_map/all_gather | solution.py:49
  7.4 6.2 %collective-permute-start = (bf16[2,3,1024]{2,0,1:T(2,128)(2,1)S(1)}, bf16[2,3,1024]{2,0,1:T(2,128)(2,1)S(1)}, u32[]{:S(2)}, u32[]{:S(2)}) collective-permute-start(bf16[2,3,1024]{2,0,1:T(2,128)(2,1)S(1)} %slice.57), channel_id=1, source_target_pairs={{0,4},{4,8},{8,12},{12,16},{16,20},{20,24},{24,28},{28,32},{32,36}... | collective-permute-start | bytes 36872 | tf_op jit(solution)/shard_map/ppermute | solution.py:18
  23.8 7.3 %copy-start.1 = (f32[16,1024]{1,0:T(8,128)S(1)}, f32[16,1024]{1,0:T(8,128)}, u32[]{:S(2)}) copy-start(f32[16,1024]{1,0:T(8,128)} %param.16) | copy-start | bytes 196612
  27.7 3.2 %copy-start = (f32[128,16384]{1,0:T(8,128)}, f32[128,16384]{1,0:T(8,128)S(1)}, u32[]{:S(2)}) copy-start(f32[128,16384]{1,0:T(8,128)S(1)} %fusion.3) | copy-start | bytes 25165828
  31.8 66.4 %all-gather.4.cloned.1.call-start = ((), (), s32[]{:S(2)}) async-start(), calls=%async_computation.6 | async-start | bytes 1310720 | tf_op jit(solution)/shard_map/all_gather | solution.py:111
  32.1 36.1 %copy-start.7 = (f32[16,1024]{1,0:T(8,128)S(1)}, f32[16,1024]{1,0:T(8,128)}, u32[]{:S(2)}) copy-start(f32[16,1024]{1,0:T(8,128)} %param.17) | copy-start | bytes 196612
  32.1 36.1 %copy-start.8 = (f32[16,1024]{1,0:T(8,128)S(1)}, f32[16,1024]{1,0:T(8,128)}, u32[]{:S(2)}) copy-start(f32[16,1024]{1,0:T(8,128)} %param.18) | copy-start | bytes 196612
  45.9 29.7 %copy-start.2 = (bf16[128,1024]{1,0:T(8,128)(2,1)S(1)}, bf16[128,1024]{1,0:T(8,128)(2,1)}, u32[]{:S(2)}) copy-start(bf16[128,1024]{1,0:T(8,128)(2,1)} %param.20) | copy-start | bytes 786436
  45.9 29.7 %copy-start.9 = (f32[1024]{0:T(1024)S(1)}, f32[1024]{0:T(1024)}, u32[]{:S(2)}) copy-start(f32[1024]{0:T(1024)} %param.19) | copy-start | bytes 12292
  45.9 30.7 %copy-start.3 = (bf16[128,1024]{1,0:T(8,128)(2,1)S(1)}, bf16[128,1024]{1,0:T(8,128)(2,1)}, u32[]{:S(2)}) copy-start(bf16[128,1024]{1,0:T(8,128)(2,1)} %param.24) | copy-start | bytes 786436
  68.2 31.5 %copy-start.6 = (f32[4096]{0:T(1024)S(1)}, f32[4096]{0:T(1024)}, u32[]{:S(2)}) copy-start(f32[4096]{0:T(1024)} %param.21) | copy-start | bytes 49156
  77.7 34.3 %all-to-all-start.1 = ((bf16[16,128,128]{2,1,0:T(8,128)(2,1)}), bf16[16,128,128]{2,1,0:T(8,128)(2,1)S(1)}, u32[]{:S(2)}, u32[]{:S(2)}) async-start(bf16[16,128,128]{2,1,0:T(8,128)(2,1)} %bitcast.16), calls=%async_computation.1 | async-start | bytes 1048576 | tf_op jit(solution)/shard_map/all_to_all | solution.py:92
  110.1 22.3 %copy-start.4 = (bf16[128,1024]{1,0:T(8,128)(2,1)S(1)}, bf16[128,1024]{1,0:T(8,128)(2,1)}, u32[]{:S(2)}) copy-start(bf16[128,1024]{1,0:T(8,128)(2,1)} %param.25) | copy-start | bytes 786436
  112.0 15.2 %all-to-all-start = ((bf16[16,64,128]{2,1,0:T(8,128)(2,1)}), bf16[16,64,128]{2,1,0:T(8,128)(2,1)S(1)}, u32[]{:S(2)}, u32[]{:S(2)}) async-start(bf16[16,64,128]{2,1,0:T(8,128)(2,1)} %bitcast.13), calls=%async_computation | async-start | bytes 524288 | tf_op jit(solution)/shard_map/all_to_all | solution.py:133
  127.2 0.9 copy-start.5
  128.1 13.7 %all-to-all-start.2 = ((bf16[16,128,128]{2,1,0:T(8,128)(2,1)}), bf16[16,128,128]{2,1,0:T(8,128)(2,1)S(1)}, u32[]{:S(2)}, u32[]{:S(2)}) async-start(bf16[16,128,128]{2,1,0:T(8,128)(2,1)} %bitcast.20), calls=%async_computation.2 | async-start | bytes 1048576 | tf_op jit(solution)/shard_map/all_to_all | solution.py:126
  142.7 14.4 %all-to-all-start.3 = ((bf16[16,128,128]{2,1,0:T(8,128)(2,1)}), bf16[16,128,128]{2,1,0:T(8,128)(2,1)S(1)}, u32[]{:S(2)}, u32[]{:S(2)}) async-start(bf16[16,128,128]{2,1,0:T(8,128)(2,1)} %bitcast.23), calls=%async_computation.3 | async-start | bytes 1048576 | tf_op jit(solution)/shard_map/all_to_all | solution.py:93
  158.0 16.4 %all-to-all-start.4 = ((bf16[16,128,128]{2,1,0:T(8,128)(2,1)}), bf16[16,128,128]{2,1,0:T(8,128)(2,1)S(1)}, u32[]{:S(2)}, u32[]{:S(2)}) async-start(bf16[16,128,128]{2,1,0:T(8,128)(2,1)} %bitcast.27), calls=%async_computation.4 | async-start | bytes 1048576 | tf_op jit(solution)/shard_map/all_to_all | solution.py:127
Sparse Core Ops, SparseCore 0:
  31.9 34.6 all-gather.5
  76.7 21.4 all-gather.3

commit v2 on v1

--- a/solution.py
+++ b/solution.py
@@ -1,8 +1,11 @@
+import functools
 import math
 
 import jax
 import jax.numpy as jnp
 from jax import lax
+from jax.experimental import pallas as pl
+from jax.experimental.pallas import tpu as pltpu
 from jax.sharding import PartitionSpec as P
 
 HEAD = 128
@@ -32,20 +35,65 @@
     )
 
 
+def local_modes_kernel(x_ref, rate_ref, rg_ref, g_ref, out_ref, final_ref):
+    length = x_ref.shape[0]
+    mode_count = rate_ref.shape[0]
+    x = x_ref[...]
+    rows = lax.broadcasted_iota(jnp.int32, (length, length), 0)
+    cols = lax.broadcasted_iota(jnp.int32, (length, length), 1)
+    lower = (rows >= cols).astype(jnp.bfloat16)
+    offsets = lax.broadcasted_iota(jnp.int32, (length, 1), 0).astype(jnp.float32)
+    total = jnp.zeros(x.shape, jnp.float32)
+    for m in range(mode_count):
+        rate = rate_ref[m : m + 1, :]
+        terms = jnp.exp(rate * offsets) * x
+        high = terms.astype(jnp.bfloat16)
+        low = (terms - high.astype(jnp.float32)).astype(jnp.bfloat16)
+        prefix = jnp.dot(lower, high, preferred_element_type=jnp.float32) + jnp.dot(
+            lower, low, preferred_element_type=jnp.float32
+        )
+        total = total + rg_ref[m : m + 1, :] * jnp.exp(-rate * offsets) * prefix
+        final_ref[m : m + 1, :] = (
+            g_ref[m : m + 1, :] * jnp.exp(-rate * (length - 1.0)) * prefix[length - 1 : length, :]
+        )
+    out_ref[...] = total
+
+
+def carried_kernel(local_ref, rate_ref, weight_ref, out_ref):
+    length = local_ref.shape[0]
+    mode_count = rate_ref.shape[0]
+    steps = lax.broadcasted_iota(jnp.int32, (length, 1), 0).astype(jnp.float32) + 1.0
+    total = local_ref[...]
+    for m in range(mode_count):
+        total = total + weight_ref[m : m + 1, :] * jnp.exp(-rate_ref[m : m + 1, :] * steps)
+    out_ref[...] = total.astype(out_ref.dtype)
+
+
+def channel_blocks(kernel, inputs, outputs, block):
+    channels = inputs[0].shape[1]
+    specs = [pl.BlockSpec((a.shape[0], block), lambda j: (0, j)) for a in inputs]
+    out_specs = [pl.BlockSpec((o.shape[0], block), lambda j: (0, j)) for o in outputs]
+    return pl.pallas_call(
+        kernel,
+        grid=(channels // block,),
+        in_specs=specs,
+        out_specs=out_specs,
+        out_shape=outputs,
+    )(*inputs)
+
+
 def modal_chunk(signal, mode_rates, mode_residues, hyena_state, device_index, devices):
     length, channels = signal.shape
-    mode_count = mode_rates.shape[0]
     mode_gain = jnp.sqrt(1.0 - jnp.exp(-2.0 * mode_rates))
-    offsets = jnp.arange(length, dtype=jnp.float32)[:, None, None]
-    rising = jnp.exp(mode_rates[None] * offsets)
-    lower_ones = (jnp.arange(length)[:, None] >= jnp.arange(length)[None, :]).astype(jnp.float32)
-    scaled_terms = (rising * signal[:, None, :]).reshape(length, mode_count * channels)
-    prefix_sums = jnp.dot(lower_ones, scaled_terms, precision=lax.Precision.HIGH).reshape(
-        length, mode_count, channels
-    )
-    falling = jnp.exp(-mode_rates[None] * offsets)
-    local_out = jnp.sum((mode_residues * mode_gain)[None] * falling * prefix_sums, axis=1)
-    final_local = mode_gain * jnp.exp(-mode_rates * (length - 1)) * prefix_sums[-1]
+    local_out, final_local = channel_blocks(
+        local_modes_kernel,
+        [signal, mode_rates, mode_residues * mode_gain, mode_gain],
+        [
+            jax.ShapeDtypeStruct((length, channels), jnp.float32),
+            jax.ShapeDtypeStruct(mode_rates.shape, jnp.float32),
+        ],
+        256,
+    )
     finals = lax.all_gather(final_local, "context", axis=0, tiled=False)
     source = jnp.arange(devices, dtype=jnp.int32)
     steps = (device_index - 1 - source).astype(jnp.float32)
@@ -56,10 +104,47 @@
     )
     incoming = jnp.exp(-mode_rates * (length * device_index.astype(jnp.float32))) * hyena_state
     incoming = incoming + jnp.sum(carry_weight * finals, axis=0)
-    carried = jnp.sum(
-        (mode_residues * incoming)[None] * jnp.exp(-mode_rates[None] * (offsets + 1.0)), axis=1
-    )
-    return local_out + carried
+    (long_out,) = channel_blocks(
+        carried_kernel,
+        [local_out, mode_rates, mode_residues * incoming],
+        [jax.ShapeDtypeStruct((length, channels), jnp.bfloat16)],
+        256,
+    )
+    return long_out
+
+
+def attention_kernel(scale, q_ref, k_ref, v_ref, qpos_ref, kpos_ref, out_ref):
+    scores = (
+        lax.dot_general(
+            q_ref[...], k_ref[...], (((1,), (1,)), ((), ())), preferred_element_type=jnp.float32
+        )
+        * scale
+    )
+    visible = kpos_ref[...] <= qpos_ref[...]
+    row_max = jnp.max(jnp.where(visible, scores, -jnp.inf), axis=1, keepdims=True)
+    weights = jnp.where(visible, jnp.exp(scores - row_max), 0.0).astype(jnp.bfloat16)
+    weight_sum = jnp.sum(weights.astype(jnp.float32), axis=1, keepdims=True)
+    numerator = jnp.dot(weights, v_ref[...], preferred_element_type=jnp.float32)
+    out_ref[...] = (numerator / weight_sum).astype(out_ref.dtype)
+
+
+def attend(queries, keys, values, query_pos, key_pos, block=256):
+    rows, width = queries.shape
+    key_rows = keys.shape[0]
+    return pl.pallas_call(
+        functools.partial(attention_kernel, 1.0 / math.sqrt(width)),
+        grid=(rows // block,),
+        in_specs=[
+            pl.BlockSpec((block, width), lambda i: (i, 0)),
+            pl.BlockSpec((key_rows, width), lambda i: (0, 0)),
+            pl.BlockSpec((key_rows, width), lambda i: (0, 0)),
+            pl.BlockSpec((block, 1), lambda i: (i, 0)),
+            pl.BlockSpec((1, key_rows), lambda i: (0, 0)),
+        ],
+        out_specs=pl.BlockSpec((block, width), lambda i: (i, 0)),
+        out_shape=jax.ShapeDtypeStruct((rows, width), jnp.bfloat16),
+        compiler_params=pltpu.CompilerParams(vmem_limit_bytes=48 * 1024 * 1024),
+    )(queries, keys, values, query_pos.reshape(rows, 1), key_pos.reshape(1, key_rows))
 
 
 def shards(
@@ -89,8 +174,11 @@
         per_head = block.reshape(row_count, heads_here, HEAD).transpose(1, 0, 2)
         return jnp.repeat(per_head, devices // heads_here, axis=0)
 
-    cache_k = lax.all_to_all(by_head(cache_keys), "context", 0, 0, tiled=True)
-    cache_v = lax.all_to_all(by_head(cache_values), "context", 0, 0, tiled=True)
+    cache_kv = lax.all_to_all(
+        jnp.concatenate([by_head(cache_keys), by_head(cache_values)], axis=1),
+        "context", 0, 0, tiled=True,
+    )
+    cache_k, cache_v = cache_kv[:, :row_count], cache_kv[:, row_count:]
 
     before = shifted(streams[row_count - (tap_count - 1) :], "context", 1)
     before = jnp.where(device_index == 0, stream_tail, before)
@@ -102,7 +190,7 @@
     product = (filtered[:, 0] * filtered[:, 2]).astype(jnp.bfloat16)
     long_out = modal_chunk(
         product.astype(jnp.float32), decay_rates, residues, hyena_state, device_index, devices
-    ).astype(jnp.bfloat16)
+    )
     hidden = (
         residual.astype(jnp.float32)
         + filtered[:, 1]
@@ -123,14 +211,18 @@
     new_keys = rotate(projected[:, 1], positions).astype(jnp.bfloat16)
     new_values = projected[:, 2].astype(jnp.bfloat16)
 
-    new_k = lax.all_to_all(by_head(new_keys), "context", 0, 0, tiled=True)
-    new_v = lax.all_to_all(by_head(new_values), "context", 0, 0, tiled=True)
     query_parts = (
         queries.reshape(2, half_rows, heads_here, HEAD)
         .transpose(2, 0, 1, 3)
         .reshape(devices, half_rows, HEAD)
     )
-    my_queries = lax.all_to_all(query_parts, "context", 0, 0, tiled=True)
+    sent = lax.all_to_all(
+        jnp.concatenate([query_parts, by_head(new_keys), by_head(new_values)], axis=1),
+        "context", 0, 0, tiled=True,
+    )
+    my_queries = sent[:, :half_rows]
+    new_k = sent[:, half_rows : half_rows + row_count]
+    new_v = sent[:, half_rows + row_count :]
 
     hist_rows = cache_k.shape[0] * cache_k.shape[1]
     all_k = jnp.concatenate([cache_k.reshape(-1, HEAD), new_k.reshape(-1, HEAD)], axis=0)
@@ -141,16 +233,7 @@
     src = jnp.arange(devices, dtype=jnp.int32)[:, None]
     row = jnp.arange(half_rows, dtype=jnp.int32)[None, :]
     query_pos = (src * row_count + (device_index % 2) * half_rows + row).reshape(-1)
-    visible = key_pos[None, :] <= query_pos[:, None]
-    score_scale = 1.0 / math.sqrt(HEAD)
-    scores = (
-        jnp.einsum("qd,kd->qk", q_flat, all_k, preferred_element_type=jnp.float32) * score_scale
-    )
-    row_max = jnp.max(jnp.where(visible, scores, -jnp.inf), axis=1, keepdims=True)
-    weights = jnp.where(visible, jnp.exp(scores - row_max), 0.0).astype(jnp.bfloat16)
-    weight_sum = jnp.sum(weights.astype(jnp.float32), axis=1, keepdims=True)
-    numerator = jnp.dot(weights, all_v, preferred_element_type=jnp.float32)
-    mine = (numerator / weight_sum).astype(jnp.bfloat16).reshape(devices, half_rows, HEAD)
+    mine = attend(q_flat, all_k, all_v, query_pos, key_pos).reshape(devices, half_rows, HEAD)
     back = lax.all_to_all(mine, "context", 0, 0, tiled=True)
     attended = (
         back.reshape(heads_here, 2, half_rows, HEAD)

time: 202 us -> 159 us (0.79)
  local copies, waits for them, and re-layouts: 33.3 us -> 5.15 us
  Pallas kernels: 0 us -> 21 us
  matrix products: 29.3 us -> 10 us
  starting transfers between devices: 31.6 us -> 16.8 us
  waiting for transfers between devices: 52.5 us -> 66.5 us
  other arithmetic: 26.7 us -> 13.5 us
  blocking collectives: 12.7 us -> 10.5 us
    unnamed x27 -> x24, local copies, waits for them, and re-layouts: 26.2 us -> 1.22 us
    pallas_call x0 -> x3, Pallas kernels: none -> 21 us  [the longest x1 10.8 us: attend(): pl.pallas_call(functools.partial(attention_kernel, 1.0 / math.sqrt(width)...]
    dot_general x3 -> x0, matrix products: 19 us -> none  [the longest x1 9.44 us: shards(): jnp.einsum('qd,kd->qk', q_flat, all_k, preferred_element_type=jnp.float32)]
    reduce_sum x2 -> x0, other arithmetic: 18.1 us -> none  [the longest x1 10.7 us: shards(): weight_sum = jnp.sum(weights.astype(jnp.float32), axis=1, keepdims=True)]
    all_to_all x5 -> x2, starting transfers between devices: 26.8 us -> 12.2 us  [the longest x1 7.86 us: shards(): lax.all_to_all(jnp.concatenate([query_parts, by_head(new_keys), by_head(n...]
    all_gather x1, waiting for transfers between devices: 20.7 us -> 34.3 us  [modal_chunk(): finals = lax.all_gather(final_local, 'context', axis=0, tiled=False)]
    broadcast_in_dim x4, local copies, waits for them, and re-layouts: 3.65 us -> 0.38 us  [by_head(): return jnp.repeat(per_head, devices // heads_here, axis=0)]
    concatenate x0 -> x3, other arithmetic: none -> 2.36 us  [the longest x1 1.15 us: shards(): jnp.concatenate([query_parts, by_head(new_keys), by_head(new_values)], ax...]
  transfers between devices with their start and end apart: 8 -> 5, of which waited for: 5 -> 3; matrix products, arithmetic and copies ran while one was open for 25% -> 13% of each run, Pallas kernels for 0% -> 0%
where the time goes in v2:
time: 159 us; the launch traced here: 158 us
  waiting for transfers between devices  66.5 us (42%)
  Pallas kernels  21 us (13%)
  starting transfers between devices  16.8 us (11%)
  between operations  14.4 us (9%)
  other arithmetic  13.5 us (8%)
  blocking collectives  10.5 us (7%)
  matrix products  10 us (6%)
  local copies, waits for them, and re-layouts  5.15 us (3%)
    all_gather x1, waiting for transfers between devices, modal_chunk(): finals = lax.all_gather(final_local, 'context', axis=0, tiled=False)  34.3 us
    all_to_all x1, waiting for transfers between devices, shards(): lax.all_to_all(jnp.concatenate([query_parts, by_head(new_keys), by_head(n...  17.1 us
    all_gather x1, waiting for transfers between devices, shards(): gathered = lax.all_gather(hidden, 'tensor', axis=1, tiled=True)  15 us
    pallas_call x1, Pallas kernels, attend(): pl.pallas_call(functools.partial(attention_kernel, 1.0 / math.sqrt(width)...  10.8 us
    all_to_all x1, blocking collectives, shards(): back = lax.all_to_all(mine, 'context', 0, 0, tiled=True)  10.5 us
    pallas_call x2, Pallas kernels, channel_blocks(): pl.pallas_call(kernel, grid=(channels // block,), in_specs=specs, out_spe...  10.2 us
    dot_general x1, matrix products, shards(): jnp.einsum('pk,kgn->pgn', normed, qkv_weight, preferred_element_type=jnp....  10 us
    all_to_all x1, starting transfers between devices, shards(): lax.all_to_all(jnp.concatenate([query_parts, by_head(new_keys), by_head(n...  7.86 us
  transfers between devices with their start and end apart: 5, of which 3 were waited for; matrix products, arithmetic and copies ran while one was open for 13% of the time, Pallas kernels for 0%

profile of v2, /device:TPU:1, one launch (start us, length us, event | category | flops | bytes accessed | tf_op | source)
XLA Modules:
  0.0 157.8 jit_solution(3613483250348897932)
XLA Ops:
  6.5 0.8 slice.68
  7.4 4.6 %collective-permute-start = (bf16[2,3,1024]{2,0,1:T(2,128)(2,1)S(1)}, bf16[2,3,1024]{2,0,1:T(2,128)(2,1)S(1)}, u32[]{:S(2)}, u32[]{:S(2)}) collective-permute-start(bf16[2,3,1024]{2,0,1:T(2,128)(2,1)S(1)} %slice.68), channel_id=1, source_target_pairs={{0,4},{4,8},{8,12},{12,16},{16,20},{20,24},{24,28},{28,32},{32,36}... | collective-permute-start | bytes 36872 | tf_op jit(solution)/shard_map/ppermute | solution.py:21
  11.9 1.6 fusion.20
  13.5 0.8 slice_bitcast_fusion.5
  14.3 1.4 maximum_convert_fusion
  16.2 0.9 fusion.15.x_ref
  17.1 6.3 %shard_map.127 = (f32[128,1024]{1,0:T(8,128)}, f32[16,1024]{1,0:T(8,128)}) custom-call(f32[128,1024]{1,0:T(8,128)} %fusion.15.x_ref, f32[16,1024]{1,0:T(8,128)} %rate_ref.3, f32[16,1024]{1,0:T(8,128)} %get-tuple-element.22.rg_ref, f32[16,1024]{1,0:T(8,128)} %get-tuple-element.23.g_ref), custom_call_target="tpu_custom_call" | custom-call | tf_op jit(solution)/shard_map/pallas_call | solution.py:76
  23.4 34.3 %all-gather.6.cloned.1.call-done = f32[256,1024]{1,0:T(8,128)} async-done(((f32[16,1024]{1,0:T(8,128)}), f32[256,1024]{1,0:T(8,128)}) %all-gather.6.cloned.1.call-update) | async-done | bytes 1048592 | tf_op jit(solution)/shard_map/all_gather | solution.py:97
  57.8 1.5 multiply_reduce_fusion
  59.3 0.6 add_multiply_fusion.weight_ref
  60.0 3.9 %shard_map.128 = bf16[128,1024]{1,0:T(8,128)(2,1)} custom-call(f32[128,1024]{1,0:T(8,128)} %get-tuple-element.7.local_ref, f32[16,1024]{1,0:T(8,128)} %rate_ref.3, f32[16,1024]{1,0:T(8,128)} %add_multiply_fusion.weight_ref), custom_call_target="tpu_custom_call" | custom-call | tf_op jit(solution)/shard_map/pallas_call | solution.py:76
  63.9 1.9 %fusion.13 = bf16[128,1024]{1,0:T(8,128)(2,1)} fusion(f32[128,3,1024]{2,0,1:T(8,128)S(1)} %fusion.3, bf16[128,1024]{1,0:T(8,128)(2,1)} %shard_map.128, bf16[128,1024]{1,0:T(8,128)(2,1)S(1)} %copy-done.3, f32[1024]{0:T(1024)S(1)} %copy-done.9), kind=kLoop, calls=%fused_computation.28 | loop fusion | flops 1310720 | bytes 2363392 | tf_op jit(solution)/shard_map/convert_element_type | solution.py:198
  66.3 1.1 pad_maximum_fusion.1
  67.3 4.3 %all-to-all-start.1 = ((bf16[16,256,128]{2,1,0:T(8,128)(2,1)}), bf16[16,256,128]{2,1,0:T(8,128)(2,1)S(1)}, u32[]{:S(2)}, u32[]{:S(2)}) async-start(bf16[16,256,128]{2,1,0:T(8,128)(2,1)} %pad_maximum_fusion.1), calls=%async_computation.1 | async-start | bytes 2097152 | tf_op jit(solution)/shard_map/all_to_all | solution.py:177
  72.7 15.0 %all-gather.4.cloned.1.call-done = bf16[128,4096]{1,0:T(8,128)(2,1)} async-done(((bf16[128,1024]{1,0:T(8,128)(2,1)}), bf16[128,4096]{1,0:T(8,128)(2,1)}) %all-gather.4.cloned.1.call-update) | async-done | bytes 1048592 | tf_op jit(solution)/shard_map/all_gather | solution.py:199
  87.7 1.6 %fusion = f32[128]{0:T(128)S(1)} fusion(bf16[128,4096]{1,0:T(8,128)(2,1)} %all-gather.4.cloned.1.call-done), kind=kLoop, calls=%fused_computation.2 | loop fusion | flops 1572736 | bytes 1049088 | tf_op jit(solution)/shard_map/reduce_sum | solution.py:201
  89.3 10.0 %fusion.6 = f32[128,3,1024]{2,0,1:T(8,128)S(1)} fusion(bf16[4096,3,1024]{2,0,1:T(8,128)(2,1)} %param.22, bf16[128,4096]{1,0:T(8,128)(2,1)S(1)} %copy-done, f32[4096]{0:T(1024)S(1)} %copy-done.7, f32[128]{0:T(128)S(1)} %add_rsqrt_fusion), kind=kOutput, calls=%fused_computation.12 | convolution fusion | flops 3223322624 | bytes 27804160 | tf_op jit(solution)/shard_map/pk,kgn->pgn/dot_general | solution.py:205
  101.0 1.2 pad_maximum_fusion
  102.1 7.9 %all-to-all-start = ((bf16[16,320,128]{2,1,0:T(8,128)(2,1)}), bf16[16,320,128]{2,1,0:T(8,128)(2,1)S(1)}, u32[]{:S(2)}, u32[]{:S(2)}) async-start(bf16[16,320,128]{2,1,0:T(8,128)(2,1)} %pad_maximum_fusion), calls=%async_computation | async-start | bytes 2621440 | tf_op jit(solution)/shard_map/all_to_all | solution.py:219
  110.6 0.9 fusion.19
  111.5 17.1 %all-to-all-done = bf16[16,320,128]{2,1,0:T(8,128)(2,1)S(1)} async-done(((bf16[16,320,128]{2,1,0:T(8,128)(2,1)}), bf16[16,320,128]{2,1,0:T(8,128)(2,1)S(1)}, u32[]{:S(2)}, u32[]{:S(2)}) %all-to-all-start) | async-done | bytes 1310752 | tf_op jit(solution)/shard_map/all_to_all | solution.py:219
  128.8 10.8 %shard_map.129 = bf16[1024,128]{1,0:T(8,128)(2,1)S(1)} custom-call(bf16[1024,128]{1,0:T(8,128)(2,1)S(1)} %bitcast.74, bf16[4096,128]{1,0:T(8,128)(2,1)S(1)} %get-tuple-element.29.k_ref, bf16[4096,128]{1,0:T(8,128)(2,1)S(1)} %get-tuple-element.30.v_ref, s32[1024,1]{1,0:T(8,128)S(1)} %add.119.qpos_ref, s32[1,4096]{1,0:T(1,128)S(1)} %compare_select_fusion.kpos_ref), custom_call_target="tpu_custom_call" | custom-call | tf_op jit(solution)/shard_map/pallas_call | solution.py:134
  139.6 10.5 %all_to_all.15 = bf16[16,64,128]{2,1,0:T(8,128)(2,1)S(1)} all-to-all(bf16[16,64,128]{2,1,0:T(8,128)(2,1)S(1)} %bitcast.75), channel_id=1, replica_groups=mesh['dp'=2,'context'=16,'tensor'=4] {'context'}, dimensions={0} | all-to-all | bytes 524288 | tf_op jit(solution)/shard_map/all_to_all | solution.py:237
  150.2 0.8 copy.34
  (60 shorter events, 3.8 us)
Async XLA Ops:
  6.5 51.2 %all-gather.6.cloned.1.call-start = ((), (), s32[]{:S(2)}) async-start(), calls=%async_computation.4 | async-start | bytes 1114112 | tf_op jit(solution)/shard_map/all_gather | solution.py:97
  7.4 6.9 %collective-permute-start = (bf16[2,3,1024]{2,0,1:T(2,128)(2,1)S(1)}, bf16[2,3,1024]{2,0,1:T(2,128)(2,1)S(1)}, u32[]{:S(2)}, u32[]{:S(2)}) collective-permute-start(bf16[2,3,1024]{2,0,1:T(2,128)(2,1)S(1)} %slice.68), channel_id=1, source_target_pairs={{0,4},{4,8},{8,12},{12,16},{16,20},{20,24},{24,28},{28,32},{32,36}... | collective-permute-start | bytes 36872 | tf_op jit(solution)/shard_map/ppermute | solution.py:21
  16.2 43.1 %copy-start.2 = (f32[16,1024]{1,0:T(8,128)S(1)}, f32[16,1024]{1,0:T(8,128)}, u32[]{:S(2)}) copy-start(f32[16,1024]{1,0:T(8,128)} %rate_ref.3) | copy-start | bytes 196612
  16.2 43.1 %copy-start.4 = (f32[16,1024]{1,0:T(8,128)S(1)}, f32[16,1024]{1,0:T(8,128)}, u32[]{:S(2)}) copy-start(f32[16,1024]{1,0:T(8,128)} %param.17) | copy-start | bytes 196612
  16.2 43.1 %copy-start.8 = (f32[16,1024]{1,0:T(8,128)S(1)}, f32[16,1024]{1,0:T(8,128)}, u32[]{:S(2)}) copy-start(f32[16,1024]{1,0:T(8,128)} %param.18) | copy-start | bytes 196612
  17.1 46.9 %copy-start.3 = (bf16[128,1024]{1,0:T(8,128)(2,1)S(1)}, bf16[128,1024]{1,0:T(8,128)(2,1)}, u32[]{:S(2)}) copy-start(bf16[128,1024]{1,0:T(8,128)(2,1)} %param.20) | copy-start | bytes 786436
  17.1 46.9 %copy-start.9 = (f32[1024]{0:T(1024)S(1)}, f32[1024]{0:T(1024)}, u32[]{:S(2)}) copy-start(f32[1024]{0:T(1024)} %param.19) | copy-start | bytes 12292
  23.4 64.3 %all-gather.4.cloned.1.call-start = ((), (), s32[]{:S(2)}) async-start(), calls=%async_computation.3 | async-start | bytes 1310720 | tf_op jit(solution)/shard_map/all_gather | solution.py:199
  60.0 5.9 %copy-start.5 = (bf16[128,1024]{1,0:T(8,128)(2,1)S(1)}, bf16[128,1024]{1,0:T(8,128)(2,1)}, u32[]{:S(2)}) copy-start(bf16[128,1024]{1,0:T(8,128)(2,1)} %param.25) | copy-start | bytes 786436
  63.9 2.0 %copy-start.6 = (bf16[128,1024]{1,0:T(8,128)(2,1)S(1)}, bf16[128,1024]{1,0:T(8,128)(2,1)}, u32[]{:S(2)}) copy-start(bf16[128,1024]{1,0:T(8,128)(2,1)} %param.24) | copy-start | bytes 786436
  67.3 21.9 %copy-start.7 = (f32[4096]{0:T(1024)S(1)}, f32[4096]{0:T(1024)}, u32[]{:S(2)}) copy-start(f32[4096]{0:T(1024)} %param.21) | copy-start | bytes 49156
  67.3 34.8 %all-to-all-start.1 = ((bf16[16,256,128]{2,1,0:T(8,128)(2,1)}), bf16[16,256,128]{2,1,0:T(8,128)(2,1)S(1)}, u32[]{:S(2)}, u32[]{:S(2)}) async-start(bf16[16,256,128]{2,1,0:T(8,128)(2,1)} %pad_maximum_fusion.1), calls=%async_computation.1 | async-start | bytes 2097152 | tf_op jit(solution)/shard_map/all_to_all | solution.py:177
  87.7 1.6 %copy-start = (bf16[128,4096]{1,0:T(8,128)(2,1)S(1)}, bf16[128,4096]{1,0:T(8,128)(2,1)}, u32[]{:S(2)}) copy-start(bf16[128,4096]{1,0:T(8,128)(2,1)} %all-gather.4.cloned.1.call-done) | copy-start | bytes 3145732
  102.1 26.4 %all-to-all-start = ((bf16[16,320,128]{2,1,0:T(8,128)(2,1)}), bf16[16,320,128]{2,1,0:T(8,128)(2,1)S(1)}, u32[]{:S(2)}, u32[]{:S(2)}) async-start(bf16[16,320,128]{2,1,0:T(8,128)(2,1)} %pad_maximum_fusion), calls=%async_computation | async-start | bytes 2621440 | tf_op jit(solution)/shard_map/all_to_all | solution.py:219
  111.5 17.2 %copy-start.1 = (bf16[16,128,128]{2,1,0:T(8,128)(2,1)S(1)}, bf16[16,128,128]{2,1,0:T(8,128)(2,1)}, u32[]{:S(2)}) copy-start(bf16[16,128,128]{2,1,0:T(8,128)(2,1)} %get-tuple-element.14) | copy-start | bytes 1572868
Sparse Core Ops, SparseCore 0:
  23.5 34.2 all-gather.5
  66.0 21.6 all-gather.3

commit v3 on v2

--- a/solution.py
+++ b/solution.py
@@ -94,7 +94,10 @@
         ],
         256,
     )
-    finals = lax.all_gather(final_local, "context", axis=0, tiled=False)
+    finals = lax.all_to_all(
+        jnp.broadcast_to(final_local[None], (devices,) + final_local.shape),
+        "context", 0, 0, tiled=True,
+    )
     source = jnp.arange(devices, dtype=jnp.int32)
     steps = (device_index - 1 - source).astype(jnp.float32)
     carry_weight = jnp.where(
@@ -145,6 +148,31 @@
         out_shape=jax.ShapeDtypeStruct((rows, width), jnp.bfloat16),
         compiler_params=pltpu.CompilerParams(vmem_limit_bytes=48 * 1024 * 1024),
     )(queries, keys, values, query_pos.reshape(rows, 1), key_pos.reshape(1, key_rows))
+
+
+def project_kernel(x_ref, w_ref, out_ref):
+    out_ref[...] = jnp.dot(x_ref[...], w_ref[...], preferred_element_type=jnp.float32)
+
+
+def project(x, w, block=512):
+    rows, depth = x.shape
+    groups, _, width = w.shape
+    return pl.pallas_call(
+        project_kernel,
+        grid=(groups, width // block),
+        in_specs=[
+            pl.BlockSpec((rows, depth), lambda g, j: (0, 0)),
+            pl.BlockSpec((None, depth, block), lambda g, j: (g, 0, j)),
+        ],
+        out_specs=pl.BlockSpec((None, rows, block), lambda g, j: (g, 0, j)),
+        out_shape=jax.ShapeDtypeStruct((groups, rows, width), jnp.float32),
+        compiler_params=pltpu.CompilerParams(vmem_limit_bytes=48 * 1024 * 1024),
+        cost_estimate=pl.CostEstimate(
+            flops=2 * rows * depth * width * groups,
+            bytes_accessed=2 * (rows * depth + groups * depth * width) + 4 * groups * rows * width,
+            transcendentals=0,
+        ),
+    )(x, w)
 
 
 def shards(
@@ -196,15 +224,21 @@
         + filtered[:, 1]
         * (long_out.astype(jnp.float32) + skip_weight[None, :] * product.astype(jnp.float32))
     ).astype(jnp.bfloat16)
-    gathered = lax.all_gather(hidden, "tensor", axis=1, tiled=True)
+    ways = lax.axis_size("tensor")
+    gathered = lax.all_to_all(
+        jnp.broadcast_to(hidden[None], (ways,) + hidden.shape), "tensor", 0, 0, tiled=True
+    )
+    gathered = gathered.transpose(1, 0, 2).reshape(row_count, ways * hidden.shape[1])
     hidden_float = gathered.astype(jnp.float32)
     mean_square = jnp.mean(hidden_float * hidden_float, axis=1, keepdims=True)
     normed = (hidden_float * lax.rsqrt(mean_square + NORM_EPSILON) * norm_gain[None, :]).astype(
         jnp.bfloat16
     )
-    projected = jnp.einsum(
-        "pk,kgn->pgn", normed, qkv_weight, preferred_element_type=jnp.float32
-    ).reshape(row_count, 3, heads_here, HEAD)
+    projected = (
+        project(normed, qkv_weight.transpose(1, 0, 2))
+        .transpose(1, 0, 2)
+        .reshape(row_count, 3, heads_here, HEAD)
+    )
     query_index = device_index * row_count + jnp.arange(row_count, dtype=jnp.int32)
     positions = (start_offset[0] + query_index).astype(jnp.float32)
     queries = rotate(projected[:, 0], positions).astype(jnp.bfloat16)

time: 159 us -> 134 us (0.84)
  waiting for transfers between devices: 66.5 us -> 45.7 us
  between operations: 14.4 us -> 1.06 us
  Pallas kernels: 21 us -> 31.5 us
  matrix products: 10 us -> 0 us
  starting transfers between devices: 16.8 us -> 24.5 us
  local copies, waits for them, and re-layouts: 5.15 us -> 8.55 us
  other arithmetic: 13.5 us -> 10.8 us
    all_gather x2 -> x0, waiting for transfers between devices: 49.3 us -> none  [the longest x1 34.3 us: modal_chunk(): finals = lax.all_gather(final_local, 'context', axis=0, tiled=False)]
    all_to_all x0 -> x2, waiting for transfers between devices: none -> 27.4 us  [the longest x1 15.7 us: modal_chunk(): lax.all_to_all(jnp.broadcast_to(final_local[None], (devices,) + final_loc...]
    pallas_call x0 -> x1, Pallas kernels: none -> 10.6 us  [project(): pl.pallas_call(project_kernel, grid=(groups, width // block), in_specs=[p...]
    dot_general x1 -> x0, matrix products: 10 us -> none  [shards(): jnp.einsum('pk,kgn->pgn', normed, qkv_weight, preferred_element_type=jnp....]
    all_to_all x0 -> x2, starting transfers between devices: none -> 9.94 us  [the longest x1 5.79 us: modal_chunk(): lax.all_to_all(jnp.broadcast_to(final_local[None], (devices,) + final_loc...]
    all_to_all x1, starting transfers between devices: 7.86 us -> 4.62 us  [shards(): lax.all_to_all(jnp.concatenate([query_parts, by_head(new_keys), by_head(n...]
    broadcast_in_dim x0 -> x2, local copies, waits for them, and re-layouts: none -> 3.06 us  [the longest x1 1.94 us: modal_chunk(): jnp.broadcast_to(final_local[None], (devices,) + final_local.shape)]
  transfers between devices with their start and end apart: 5 -> 5, of which waited for: 3 -> 4; matrix products, arithmetic and copies ran while one was open for 13% -> 7% of each run, Pallas kernels for 0% -> 8%
where the time goes in v3:
time: 134 us; the launch traced here: 132 us
  waiting for transfers between devices  45.7 us (34%)
  Pallas kernels  31.5 us (24%)
  starting transfers between devices  24.5 us (18%)
  other arithmetic  10.8 us (8%)
  blocking collectives  10.5 us (8%)
  local copies, waits for them, and re-layouts  8.55 us (6%)
    all_to_all x1, waiting for transfers between devices, shards(): lax.all_to_all(jnp.concatenate([query_parts, by_head(new_keys), by_head(n...  17.1 us
    all_to_all x1, waiting for transfers between devices, modal_chunk(): lax.all_to_all(jnp.broadcast_to(final_local[None], (devices,) + final_loc...  15.7 us
    all_to_all x1, waiting for transfers between devices, shards(): lax.all_to_all(jnp.broadcast_to(hidden[None], (ways,) + hidden.shape), 't...  11.7 us
    pallas_call x1, Pallas kernels, attend(): pl.pallas_call(functools.partial(attention_kernel, 1.0 / math.sqrt(width)...  10.8 us
    pallas_call x1, Pallas kernels, project(): pl.pallas_call(project_kernel, grid=(groups, width // block), in_specs=[p...  10.6 us
    all_to_all x1, blocking collectives, shards(): back = lax.all_to_all(mine, 'context', 0, 0, tiled=True)  10.5 us
    pallas_call x2, Pallas kernels, channel_blocks(): pl.pallas_call(kernel, grid=(channels // block,), in_specs=specs, out_spe...  10.1 us
    all_to_all x1, starting transfers between devices, modal_chunk(): lax.all_to_all(jnp.broadcast_to(final_local[None], (devices,) + final_loc...  5.79 us
  transfers between devices with their start and end apart: 5, of which 4 were waited for; matrix products, arithmetic and copies ran while one was open for 7% of the time, Pallas kernels for 8%

profile of v3, /device:TPU:1, one launch (start us, length us, event | category | flops | bytes accessed | tf_op | source)
XLA Modules:
  0.0 132.5 jit_solution(10848756028381276338)
XLA Ops:
  0.0 0.8 slice.68
  0.8 4.6 %collective-permute-start = (bf16[2,3,1024]{2,0,1:T(2,128)(2,1)S(1)}, bf16[2,3,1024]{2,0,1:T(2,128)(2,1)S(1)}, u32[]{:S(2)}, u32[]{:S(2)}) collective-permute-start(bf16[2,3,1024]{2,0,1:T(2,128)(2,1)S(1)} %slice.68), channel_id=1, source_target_pairs={{0,4},{4,8},{8,12},{12,16},{16,20},{20,24},{24,28},{28,32},{32,36}... | collective-permute-start | bytes 36872 | tf_op jit(solution)/shard_map/ppermute | solution.py:21
  5.4 1.6 %fusion.13 = (f32[16,1024]{1,0:T(8,128)S(1)}, f32[16,1024]{1,0:T(8,128)}, f32[16,1024]{1,0:T(8,128)}) fusion(f32[16,1024]{1,0:T(8,128)} %rate_ref.3, f32[16,1024]{1,0:T(8,128)} %param.17), kind=kLoop, calls=%fused_computation.54 | loop fusion | flops 65536 | bytes 327680 | tf_op jit(solution)/shard_map/neg | solution.py:108
  7.8 1.4 %maximum_convert_fusion = f32[130,3,1024]{2,0,1:T(8,128)S(1)} fusion(bf16[128,3,1024]{2,0,1:T(8,128)(2,1)} %param.13, bf16[2,3,1024]{2,0,1:T(2,128)(2,1)S(1)} %broadcast_select_fusion), kind=kLoop, calls=%fused_computation.14 | loop fusion | flops 1597440 | bytes 2396160 | tf_op jit(solution)/shard_map/convert_element_type | solution.py:213
  9.6 0.9 fusion.8.x_ref
  10.5 6.2 %shard_map.127 = (f32[128,1024]{1,0:T(8,128)}, f32[16,1024]{1,0:T(8,128)}) custom-call(f32[128,1024]{1,0:T(8,128)} %fusion.8.x_ref, f32[16,1024]{1,0:T(8,128)} %rate_ref.3, f32[16,1024]{1,0:T(8,128)} %get-tuple-element.22.rg_ref, f32[16,1024]{1,0:T(8,128)} %get-tuple-element.23.g_ref), custom_call_target="tpu_custom_call" | custom-call | tf_op jit(solution)/shard_map/pallas_call | solution.py:76
  16.7 1.9 %broadcast_in_dim.29 = f32[16,16,1024]{2,1,0:T(8,128)} broadcast(f32[16,1024]{1,0:T(8,128)} %get-tuple-element.8), dimensions={1,2} | broadcast | bytes 1114112 | tf_op jit(solution)/shard_map/broadcast_in_dim | solution.py:98
  18.7 5.8 %all-to-all-start = ((f32[16,16,1024]{2,1,0:T(8,128)}), f32[16,16,1024]{2,1,0:T(8,128)S(1)}, u32[]{:S(2)}, u32[]{:S(2)}) async-start(f32[16,16,1024]{2,1,0:T(8,128)} %broadcast_in_dim.29), calls=%async_computation | async-start | bytes 2097152 | tf_op jit(solution)/shard_map/all_to_all | solution.py:97
  24.5 15.7 %all-to-all-done = f32[16,16,1024]{2,1,0:T(8,128)S(1)} async-done(((f32[16,16,1024]{2,1,0:T(8,128)}), f32[16,16,1024]{2,1,0:T(8,128)S(1)}, u32[]{:S(2)}, u32[]{:S(2)}) %all-to-all-start) | async-done | bytes 1048608 | tf_op jit(solution)/shard_map/all_to_all | solution.py:97
  41.2 3.9 %shard_map.128 = bf16[128,1024]{1,0:T(8,128)(2,1)} custom-call(f32[128,1024]{1,0:T(8,128)} %get-tuple-element.7.local_ref, f32[16,1024]{1,0:T(8,128)} %rate_ref.3, f32[16,1024]{1,0:T(8,128)} %add_multiply_fusion.weight_ref), custom_call_target="tpu_custom_call" | custom-call | tf_op jit(solution)/shard_map/pallas_call | solution.py:76
  45.1 1.1 fusion.6
  46.3 1.1 broadcast_in_dim.30
  47.4 4.1 %all-to-all-start.1 = ((bf16[4,128,1024]{2,1,0:T(8,128)(2,1)}), bf16[4,128,1024]{2,1,0:T(8,128)(2,1)S(1)}, u32[]{:S(2)}, u32[]{:S(2)}) async-start(bf16[4,128,1024]{2,1,0:T(8,128)(2,1)} %broadcast_in_dim.30), calls=%async_computation.1 | async-start | bytes 2097152 | tf_op jit(solution)/shard_map/all_to_all | solution.py:228
  52.6 1.1 pad_maximum_fusion.1
  54.0 11.7 %all-to-all-done.1 = bf16[4,128,1024]{2,1,0:T(8,128)(2,1)S(1)} async-done(((bf16[4,128,1024]{2,1,0:T(8,128)(2,1)}), bf16[4,128,1024]{2,1,0:T(8,128)(2,1)S(1)}, u32[]{:S(2)}, u32[]{:S(2)}) %all-to-all-start.1) | async-done | bytes 1048608 | tf_op jit(solution)/shard_map/all_to_all | solution.py:228
  65.6 5.4 %all-to-all-start.3 = ((bf16[16,256,128]{2,1,0:T(8,128)(2,1)}), bf16[16,256,128]{2,1,0:T(8,128)(2,1)S(1)}, u32[]{:S(2)}, u32[]{:S(2)}) async-start(bf16[16,256,128]{2,1,0:T(8,128)(2,1)} %pad_maximum_fusion.1), calls=%async_computation.3 | async-start | bytes 2097152 | tf_op jit(solution)/shard_map/all_to_all | solution.py:205
  72.3 10.6 %shard_map.129 = f32[3,128,1024]{2,1,0:T(8,128)S(1)} custom-call(bf16[128,4096]{1,0:T(8,128)(2,1)S(1)} %multiply_convert_fusion.x_ref, bf16[3,4096,1024]{2,1,0:T(8,128)(2,1)} %bitcast.78), custom_call_target="tpu_custom_call" | custom-call | flops 3221225472 | bytes 27787264 | tf_op jit(solution)/shard_map/pallas_call | solution.py:160
  84.5 1.2 pad_maximum_fusion
  85.7 1.2 all-to-all-done.3
  86.9 4.6 %all-to-all-start.2 = ((bf16[16,320,128]{2,1,0:T(8,128)(2,1)}), bf16[16,320,128]{2,1,0:T(8,128)(2,1)S(1)}, u32[]{:S(2)}, u32[]{:S(2)}) async-start(bf16[16,320,128]{2,1,0:T(8,128)(2,1)} %pad_maximum_fusion), calls=%async_computation.2 | async-start | bytes 2621440 | tf_op jit(solution)/shard_map/all_to_all | solution.py:253
  92.1 0.9 fusion.12
  92.9 17.1 %all-to-all-done.2 = bf16[16,320,128]{2,1,0:T(8,128)(2,1)S(1)} async-done(((bf16[16,320,128]{2,1,0:T(8,128)(2,1)}), bf16[16,320,128]{2,1,0:T(8,128)(2,1)S(1)}, u32[]{:S(2)}, u32[]{:S(2)}) %all-to-all-start.2) | async-done | bytes 1310752 | tf_op jit(solution)/shard_map/all_to_all | solution.py:253
  110.3 10.8 %shard_map.130 = bf16[1024,128]{1,0:T(8,128)(2,1)S(1)} custom-call(bf16[1024,128]{1,0:T(8,128)(2,1)S(1)} %bitcast.76, bf16[4096,128]{1,0:T(8,128)(2,1)S(1)} %get-tuple-element.29.k_ref, bf16[4096,128]{1,0:T(8,128)(2,1)S(1)} %get-tuple-element.30.v_ref, s32[1024,1]{1,0:T(8,128)S(1)} %add.119.qpos_ref, s32[1,4096]{1,0:T(1,128)S(1)} %compare_select_fusion.kpos_ref), custom_call_target="tpu_custom_call" | custom-call | tf_op jit(solution)/shard_map/pallas_call | solution.py:137
  121.1 10.5 %all_to_all.25 = bf16[16,64,128]{2,1,0:T(8,128)(2,1)S(1)} all-to-all(bf16[16,64,128]{2,1,0:T(8,128)(2,1)S(1)} %bitcast.77), channel_id=1, replica_groups=mesh['dp'=2,'context'=16,'tensor'=4] {'context'}, dimensions={0} | all-to-all | bytes 524288 | tf_op jit(solution)/shard_map/all_to_all | solution.py:271
  (61 shorter events, 7.4 us)
Async XLA Ops:
  0.8 6.9 %collective-permute-start = (bf16[2,3,1024]{2,0,1:T(2,128)(2,1)S(1)}, bf16[2,3,1024]{2,0,1:T(2,128)(2,1)S(1)}, u32[]{:S(2)}, u32[]{:S(2)}) collective-permute-start(bf16[2,3,1024]{2,0,1:T(2,128)(2,1)S(1)} %slice.68), channel_id=1, source_target_pairs={{0,4},{4,8},{8,12},{12,16},{16,20},{20,24},{24,28},{28,32},{32,36}... | collective-permute-start | bytes 36872 | tf_op jit(solution)/shard_map/ppermute | solution.py:21
  18.7 21.9 %copy-start.1 = (f32[16,1024]{1,0:T(8,128)S(1)}, f32[16,1024]{1,0:T(8,128)}, u32[]{:S(2)}) copy-start(f32[16,1024]{1,0:T(8,128)} %rate_ref.3) | copy-start | bytes 196612
  18.7 21.9 %copy-start.3 = (f32[16,1024]{1,0:T(8,128)S(1)}, f32[16,1024]{1,0:T(8,128)}, u32[]{:S(2)}) copy-start(f32[16,1024]{1,0:T(8,128)} %param.17) | copy-start | bytes 196612
  18.7 21.9 %copy-start.6 = (f32[16,1024]{1,0:T(8,128)S(1)}, f32[16,1024]{1,0:T(8,128)}, u32[]{:S(2)}) copy-start(f32[16,1024]{1,0:T(8,128)} %param.18) | copy-start | bytes 196612
  18.7 21.6 %all-to-all-start = ((f32[16,16,1024]{2,1,0:T(8,128)}), f32[16,16,1024]{2,1,0:T(8,128)S(1)}, u32[]{:S(2)}, u32[]{:S(2)}) async-start(f32[16,16,1024]{2,1,0:T(8,128)} %broadcast_in_dim.29), calls=%async_computation | async-start | bytes 2097152 | tf_op jit(solution)/shard_map/all_to_all | solution.py:97
  24.5 20.6 %copy-start.2 = (bf16[128,1024]{1,0:T(8,128)(2,1)S(1)}, bf16[128,1024]{1,0:T(8,128)(2,1)}, u32[]{:S(2)}) copy-start(bf16[128,1024]{1,0:T(8,128)(2,1)} %param.20) | copy-start | bytes 786436
  24.5 20.6 %copy-start.8 = (f32[1024]{0:T(1024)S(1)}, f32[1024]{0:T(1024)}, u32[]{:S(2)}) copy-start(f32[1024]{0:T(1024)} %param.19) | copy-start | bytes 12292
  46.2 5.9 %copy-start.4 = (bf16[128,1024]{1,0:T(8,128)(2,1)S(1)}, bf16[128,1024]{1,0:T(8,128)(2,1)}, u32[]{:S(2)}) copy-start(bf16[128,1024]{1,0:T(8,128)(2,1)} %param.25) | copy-start | bytes 786436
  47.4 4.9 %copy-start.5 = (bf16[128,1024]{1,0:T(8,128)(2,1)S(1)}, bf16[128,1024]{1,0:T(8,128)(2,1)}, u32[]{:S(2)}) copy-start(bf16[128,1024]{1,0:T(8,128)(2,1)} %param.24) | copy-start | bytes 786436
  47.4 18.3 %all-to-all-start.1 = ((bf16[4,128,1024]{2,1,0:T(8,128)(2,1)}), bf16[4,128,1024]{2,1,0:T(8,128)(2,1)S(1)}, u32[]{:S(2)}, u32[]{:S(2)}) async-start(bf16[4,128,1024]{2,1,0:T(8,128)(2,1)} %broadcast_in_dim.30), calls=%async_computation.1 | async-start | bytes 2097152 | tf_op jit(solution)/shard_map/all_to_all | solution.py:228
  65.6 21.2 %all-to-all-start.3 = ((bf16[16,256,128]{2,1,0:T(8,128)(2,1)}), bf16[16,256,128]{2,1,0:T(8,128)(2,1)S(1)}, u32[]{:S(2)}, u32[]{:S(2)}) async-start(bf16[16,256,128]{2,1,0:T(8,128)(2,1)} %pad_maximum_fusion.1), calls=%async_computation.3 | async-start | bytes 2097152 | tf_op jit(solution)/shard_map/all_to_all | solution.py:205
  71.3 0.7 copy-start.7
  86.9 23.2 %all-to-all-start.2 = ((bf16[16,320,128]{2,1,0:T(8,128)(2,1)}), bf16[16,320,128]{2,1,0:T(8,128)(2,1)S(1)}, u32[]{:S(2)}, u32[]{:S(2)}) async-start(bf16[16,320,128]{2,1,0:T(8,128)(2,1)} %pad_maximum_fusion), calls=%async_computation.2 | async-start | bytes 2621440 | tf_op jit(solution)/shard_map/all_to_all | solution.py:253
  92.9 17.2 %copy-start = (bf16[16,128,128]{2,1,0:T(8,128)(2,1)S(1)}, bf16[16,128,128]{2,1,0:T(8,128)(2,1)}, u32[]{:S(2)}) copy-start(bf16[16,128,128]{2,1,0:T(8,128)(2,1)} %get-tuple-element.14) | copy-start | bytes 1572868

commit v4 on v3

--- a/solution.py
+++ b/solution.py
@@ -95,9 +95,9 @@
         256,
     )
     finals = lax.all_to_all(
-        jnp.broadcast_to(final_local[None], (devices,) + final_local.shape),
+        jnp.broadcast_to(final_local.astype(jnp.bfloat16)[None], (devices,) + final_local.shape),
         "context", 0, 0, tiled=True,
-    )
+    ).astype(jnp.float32)
     source = jnp.arange(devices, dtype=jnp.int32)
     steps = (device_index - 1 - source).astype(jnp.float32)
     carry_weight = jnp.where(
@@ -267,8 +267,16 @@
     src = jnp.arange(devices, dtype=jnp.int32)[:, None]
     row = jnp.arange(half_rows, dtype=jnp.int32)[None, :]
     query_pos = (src * row_count + (device_index % 2) * half_rows + row).reshape(-1)
-    mine = attend(q_flat, all_k, all_v, query_pos, key_pos).reshape(devices, half_rows, HEAD)
-    back = lax.all_to_all(mine, "context", 0, 0, tiled=True)
+    quarter = half_rows // 2
+    q_split = q_flat.reshape(devices, 2, quarter, HEAD)
+    pos_split = query_pos.reshape(devices, 2, quarter)
+    halves = []
+    for h in range(2):
+        mine = attend(
+            q_split[:, h].reshape(-1, HEAD), all_k, all_v, pos_split[:, h].reshape(-1), key_pos
+        ).reshape(devices, quarter, HEAD)
+        halves.append(lax.all_to_all(mine, "context", 0, 0, tiled=True))
+    back = jnp.stack(halves, axis=1).reshape(devices, half_rows, HEAD)
     attended = (
         back.reshape(heads_here, 2, half_rows, HEAD)
         .transpose(1, 2, 0, 3)

time: 134 us -> 134 us (level)
  waiting for transfers between devices: 45.7 us -> 39.2 us
  starting transfers between devices: 24.5 us -> 29.2 us
    all_to_all x1 -> x2, waiting for transfers between devices: 15.7 us -> 9.93 us  [the longest x1 9.47 us: modal_chunk(): lax.all_to_all(jnp.broadcast_to(final_local.astype(jnp.bfloat16)[None], (...]
    all_to_all x1 -> x2, starting transfers between devices: 5.79 us -> 9.75 us  [the longest x1 5.66 us: modal_chunk(): lax.all_to_all(jnp.broadcast_to(final_local.astype(jnp.bfloat16)[None], (...]
    pallas_call x1 -> x2, Pallas kernels: 10.8 us -> 11.4 us  [attend(): pl.pallas_call(functools.partial(attention_kernel, 1.0 / math.sqrt(width)...]
  transfers between devices with their start and end apart: 5 -> 6, of which waited for: 4 -> 5; matrix products, arithmetic and copies ran while one was open for 7% -> 7% of each run, Pallas kernels for 8% -> 12%
where the time goes in v4:
time: 134 us; the launch traced here: 133 us
  waiting for transfers between devices  39.2 us (29%)
  Pallas kernels  32.2 us (24%)
  starting transfers between devices  29.2 us (22%)
  other arithmetic  11.7 us (9%)
  blocking collectives  11.2 us (8%)
  local copies, waits for them, and re-layouts  8.66 us (6%)
    all_to_all x1, waiting for transfers between devices, shards(): lax.all_to_all(jnp.concatenate([query_parts, by_head(new_keys), by_head(n...  17.1 us
    pallas_call x2, Pallas kernels, attend(): pl.pallas_call(functools.partial(attention_kernel, 1.0 / math.sqrt(width)...  11.4 us
    all_to_all x1, blocking collectives, shards(): halves.append(lax.all_to_all(mine, 'context', 0, 0, tiled=True))  11.2 us
    all_to_all x1, waiting for transfers between devices, shards(): lax.all_to_all(jnp.broadcast_to(hidden[None], (ways,) + hidden.shape), 't...  11 us
    pallas_call x1, Pallas kernels, project(): pl.pallas_call(project_kernel, grid=(groups, width // block), in_specs=[p...  10.6 us
    pallas_call x2, Pallas kernels, channel_blocks(): pl.pallas_call(kernel, grid=(channels // block,), in_specs=specs, out_spe...  10.1 us
    all_to_all x1, waiting for transfers between devices, modal_chunk(): lax.all_to_all(jnp.broadcast_to(final_local.astype(jnp.bfloat16)[None], (...  9.47 us
    all_to_all x1, starting transfers between devices, shards(): lax.all_to_all(jnp.concatenate([by_head(cache_keys), by_head(cache_values...  6.07 us
  transfers between devices with their start and end apart: 6, of which 5 were waited for; matrix products, arithmetic and copies ran while one was open for 7% of the time, Pallas kernels for 12%

profile of v4, /device:TPU:1, one launch (start us, length us, event | category | flops | bytes accessed | tf_op | source)
XLA Modules:
  0.0 133.1 jit_solution(4179385144345789534)
XLA Ops:
  0.8 4.6 %collective-permute-start = (bf16[2,3,1024]{2,0,1:T(2,128)(2,1)S(1)}, bf16[2,3,1024]{2,0,1:T(2,128)(2,1)S(1)}, u32[]{:S(2)}, u32[]{:S(2)}) collective-permute-start(bf16[2,3,1024]{2,0,1:T(2,128)(2,1)S(1)} %slice.80), channel_id=1, source_target_pairs={{0,4},{4,8},{8,12},{12,16},{16,20},{20,24},{24,28},{28,32},{32,36}... | collective-permute-start | bytes 36872 | tf_op jit(solution)/shard_map/ppermute | solution.py:21
  5.4 1.6 %fusion.14 = (f32[16,1024]{1,0:T(8,128)S(1)}, f32[16,1024]{1,0:T(8,128)}, f32[16,1024]{1,0:T(8,128)}) fusion(f32[16,1024]{1,0:T(8,128)} %rate_ref.3, f32[16,1024]{1,0:T(8,128)} %param.17), kind=kLoop, calls=%fused_computation.57 | loop fusion | flops 65536 | bytes 327680 | tf_op jit(solution)/shard_map/neg | solution.py:108
  7.8 1.4 %maximum_convert_fusion = f32[130,3,1024]{2,0,1:T(8,128)S(1)} fusion(bf16[128,3,1024]{2,0,1:T(8,128)(2,1)} %param.13, bf16[2,3,1024]{2,0,1:T(2,128)(2,1)S(1)} %broadcast_select_fusion), kind=kLoop, calls=%fused_computation.14 | loop fusion | flops 1597440 | bytes 2396160 | tf_op jit(solution)/shard_map/convert_element_type | solution.py:213
  10.5 6.2 %shard_map.127 = (f32[128,1024]{1,0:T(8,128)}, f32[16,1024]{1,0:T(8,128)}) custom-call(f32[128,1024]{1,0:T(8,128)} %fusion.8.x_ref, f32[16,1024]{1,0:T(8,128)} %rate_ref.3, f32[16,1024]{1,0:T(8,128)} %get-tuple-element.24.rg_ref, f32[16,1024]{1,0:T(8,128)} %get-tuple-element.25.g_ref), custom_call_target="tpu_custom_call" | custom-call | tf_op jit(solution)/shard_map/pallas_call | solution.py:76
  18.5 5.7 %all-to-all-start = ((bf16[16,16,1024]{2,1,0:T(8,128)(2,1)}), bf16[16,16,1024]{2,1,0:T(8,128)(2,1)S(1)}, u32[]{:S(2)}, u32[]{:S(2)}) async-start(bf16[16,16,1024]{2,1,0:T(8,128)(2,1)} %broadcast_in_dim.29), calls=%async_computation | async-start | bytes 1048576 | tf_op jit(solution)/shard_map/all_to_all | solution.py:97
  24.1 9.5 %all-to-all-done = bf16[16,16,1024]{2,1,0:T(8,128)(2,1)S(1)} async-done(((bf16[16,16,1024]{2,1,0:T(8,128)(2,1)}), bf16[16,16,1024]{2,1,0:T(8,128)(2,1)S(1)}, u32[]{:S(2)}, u32[]{:S(2)}) %all-to-all-start) | async-done | bytes 524320 | tf_op jit(solution)/shard_map/all_to_all | solution.py:97
  34.6 3.9 %shard_map.128 = bf16[128,1024]{1,0:T(8,128)(2,1)} custom-call(f32[128,1024]{1,0:T(8,128)} %get-tuple-element.7.local_ref, f32[16,1024]{1,0:T(8,128)} %rate_ref.3, f32[16,1024]{1,0:T(8,128)} %add_multiply_fusion.weight_ref), custom_call_target="tpu_custom_call" | custom-call | tf_op jit(solution)/shard_map/pallas_call | solution.py:76
  38.5 1.1 fusion.6
  39.7 1.1 broadcast_in_dim.30
  40.8 4.1 %all-to-all-start.1 = ((bf16[4,128,1024]{2,1,0:T(8,128)(2,1)}), bf16[4,128,1024]{2,1,0:T(8,128)(2,1)S(1)}, u32[]{:S(2)}, u32[]{:S(2)}) async-start(bf16[4,128,1024]{2,1,0:T(8,128)(2,1)} %broadcast_in_dim.30), calls=%async_computation.1 | async-start | bytes 2097152 | tf_op jit(solution)/shard_map/all_to_all | solution.py:228
  46.1 1.1 pad_maximum_fusion.1
  47.5 11.0 %all-to-all-done.1 = bf16[4,128,1024]{2,1,0:T(8,128)(2,1)S(1)} async-done(((bf16[4,128,1024]{2,1,0:T(8,128)(2,1)}), bf16[4,128,1024]{2,1,0:T(8,128)(2,1)S(1)}, u32[]{:S(2)}, u32[]{:S(2)}) %all-to-all-start.1) | async-done | bytes 1048608 | tf_op jit(solution)/shard_map/all_to_all | solution.py:228
  58.5 6.1 %all-to-all-start.3 = ((bf16[16,256,128]{2,1,0:T(8,128)(2,1)}), bf16[16,256,128]{2,1,0:T(8,128)(2,1)S(1)}, u32[]{:S(2)}, u32[]{:S(2)}) async-start(bf16[16,256,128]{2,1,0:T(8,128)(2,1)} %pad_maximum_fusion.1), calls=%async_computation.3 | async-start | bytes 2097152 | tf_op jit(solution)/shard_map/all_to_all | solution.py:205
  65.8 10.6 %shard_map.129 = f32[3,128,1024]{2,1,0:T(8,128)S(1)} custom-call(bf16[128,4096]{1,0:T(8,128)(2,1)S(1)} %multiply_convert_fusion.x_ref, bf16[3,4096,1024]{2,1,0:T(8,128)(2,1)} %bitcast.93), custom_call_target="tpu_custom_call" | custom-call | flops 3221225472 | bytes 27787264 | tf_op jit(solution)/shard_map/pallas_call | solution.py:160
  78.0 1.2 pad_maximum_fusion
  79.2 1.1 all-to-all-done.3
  80.3 4.6 %all-to-all-start.2 = ((bf16[16,320,128]{2,1,0:T(8,128)(2,1)}), bf16[16,320,128]{2,1,0:T(8,128)(2,1)S(1)}, u32[]{:S(2)}, u32[]{:S(2)}) async-start(bf16[16,320,128]{2,1,0:T(8,128)(2,1)} %pad_maximum_fusion), calls=%async_computation.2 | async-start | bytes 2621440 | tf_op jit(solution)/shard_map/all_to_all | solution.py:253
  85.3 1.1 fusion.12
  86.4 17.1 %all-to-all-done.2 = bf16[16,320,128]{2,1,0:T(8,128)(2,1)S(1)} async-done(((bf16[16,320,128]{2,1,0:T(8,128)(2,1)}), bf16[16,320,128]{2,1,0:T(8,128)(2,1)S(1)}, u32[]{:S(2)}, u32[]{:S(2)}) %all-to-all-start.2) | async-done | bytes 1310752 | tf_op jit(solution)/shard_map/all_to_all | solution.py:253
  103.7 0.9 copy-done.1
  104.7 6.0 %shard_map.131 = bf16[512,128]{1,0:T(8,128)(2,1)} custom-call(bf16[512,128]{1,0:T(8,128)(2,1)S(1)} %bitcast.92, bf16[4096,128]{1,0:T(8,128)(2,1)S(1)} %get-tuple-element.33.k_ref, bf16[4096,128]{1,0:T(8,128)(2,1)S(1)} %get-tuple-element.34.v_ref, s32[512,1]{1,0:T(8,128)S(1)} %reshape_reshape_squeeze.9.qpos_ref, s32[1,4096]{1,0:T(1,128)S(1)} %compare_select_fusion.kpos_ref), custom_call_target="tpu_custom_call" | custom-call | tf_op jit(solution)/shard_map/pallas_call | solution.py:137
  110.7 4.1 %all-to-all-start.5 = ((bf16[16,32,128]{2,1,0:T(8,128)(2,1)}), bf16[16,32,128]{2,1,0:T(8,128)(2,1)S(1)}, u32[]{:S(2)}, u32[]{:S(2)}) async-start(bf16[16,32,128]{2,1,0:T(8,128)(2,1)} %bitcast.34), calls=%async_computation.5 | async-start | bytes 262144 | tf_op jit(solution)/shard_map/all_to_all | solution.py:278
  115.1 5.4 %shard_map.130 = bf16[512,128]{1,0:T(8,128)(2,1)S(1)} custom-call(bf16[512,128]{1,0:T(8,128)(2,1)S(1)} %bitcast.91, bf16[4096,128]{1,0:T(8,128)(2,1)S(1)} %get-tuple-element.33.k_ref, bf16[4096,128]{1,0:T(8,128)(2,1)S(1)} %get-tuple-element.34.v_ref, s32[512,1]{1,0:T(8,128)S(1)} %reshape_reshape_squeeze.8.qpos_ref, s32[1,4096]{1,0:T(1,128)S(1)} %compare_select_fusion.kpos_ref), custom_call_target="tpu_custom_call" | custom-call | tf_op jit(solution)/shard_map/pallas_call | solution.py:137
  121.0 11.2 %all_to_all.30 = bf16[16,32,128]{2,1,0:T(8,128)(2,1)S(1)} all-to-all(bf16[16,32,128]{2,1,0:T(8,128)(2,1)S(1)} %bitcast.90), channel_id=1, replica_groups=mesh['dp'=2,'context'=16,'tensor'=4] {'context'}, dimensions={0} | all-to-all | bytes 262144 | tf_op jit(solution)/shard_map/all_to_all | solution.py:278
  (72 shorter events, 11.4 us)
Async XLA Ops:
  0.8 6.9 %collective-permute-start = (bf16[2,3,1024]{2,0,1:T(2,128)(2,1)S(1)}, bf16[2,3,1024]{2,0,1:T(2,128)(2,1)S(1)}, u32[]{:S(2)}, u32[]{:S(2)}) collective-permute-start(bf16[2,3,1024]{2,0,1:T(2,128)(2,1)S(1)} %slice.80), channel_id=1, source_target_pairs={{0,4},{4,8},{8,12},{12,16},{16,20},{20,24},{24,28},{28,32},{32,36}... | collective-permute-start | bytes 36872 | tf_op jit(solution)/shard_map/ppermute | solution.py:21
  10.5 23.4 %copy-start.2 = (f32[16,1024]{1,0:T(8,128)S(1)}, f32[16,1024]{1,0:T(8,128)}, u32[]{:S(2)}) copy-start(f32[16,1024]{1,0:T(8,128)} %rate_ref.3) | copy-start | bytes 196612
  10.5 23.5 %copy-start.4 = (f32[16,1024]{1,0:T(8,128)S(1)}, f32[16,1024]{1,0:T(8,128)}, u32[]{:S(2)}) copy-start(f32[16,1024]{1,0:T(8,128)} %param.17) | copy-start | bytes 196612
  10.5 23.5 %copy-start.7 = (f32[16,1024]{1,0:T(8,128)S(1)}, f32[16,1024]{1,0:T(8,128)}, u32[]{:S(2)}) copy-start(f32[16,1024]{1,0:T(8,128)} %param.18) | copy-start | bytes 196612
  17.6 20.9 %copy-start.3 = (bf16[128,1024]{1,0:T(8,128)(2,1)S(1)}, bf16[128,1024]{1,0:T(8,128)(2,1)}, u32[]{:S(2)}) copy-start(bf16[128,1024]{1,0:T(8,128)(2,1)} %param.20) | copy-start | bytes 786436
  17.6 20.9 %copy-start.9 = (f32[1024]{0:T(1024)S(1)}, f32[1024]{0:T(1024)}, u32[]{:S(2)}) copy-start(f32[1024]{0:T(1024)} %param.19) | copy-start | bytes 12292
  18.5 15.1 %all-to-all-start = ((bf16[16,16,1024]{2,1,0:T(8,128)(2,1)}), bf16[16,16,1024]{2,1,0:T(8,128)(2,1)S(1)}, u32[]{:S(2)}, u32[]{:S(2)}) async-start(bf16[16,16,1024]{2,1,0:T(8,128)(2,1)} %broadcast_in_dim.29), calls=%async_computation | async-start | bytes 1048576 | tf_op jit(solution)/shard_map/all_to_all | solution.py:97
  39.7 6.0 %copy-start.5 = (bf16[128,1024]{1,0:T(8,128)(2,1)S(1)}, bf16[128,1024]{1,0:T(8,128)(2,1)}, u32[]{:S(2)}) copy-start(bf16[128,1024]{1,0:T(8,128)(2,1)} %param.25) | copy-start | bytes 786436
  40.8 4.9 %copy-start.6 = (bf16[128,1024]{1,0:T(8,128)(2,1)S(1)}, bf16[128,1024]{1,0:T(8,128)(2,1)}, u32[]{:S(2)}) copy-start(bf16[128,1024]{1,0:T(8,128)(2,1)} %param.24) | copy-start | bytes 786436
  40.8 17.6 %all-to-all-start.1 = ((bf16[4,128,1024]{2,1,0:T(8,128)(2,1)}), bf16[4,128,1024]{2,1,0:T(8,128)(2,1)S(1)}, u32[]{:S(2)}, u32[]{:S(2)}) async-start(bf16[4,128,1024]{2,1,0:T(8,128)(2,1)} %broadcast_in_dim.30), calls=%async_computation.1 | async-start | bytes 2097152 | tf_op jit(solution)/shard_map/all_to_all | solution.py:228
  58.5 21.9 %all-to-all-start.3 = ((bf16[16,256,128]{2,1,0:T(8,128)(2,1)}), bf16[16,256,128]{2,1,0:T(8,128)(2,1)S(1)}, u32[]{:S(2)}, u32[]{:S(2)}) async-start(bf16[16,256,128]{2,1,0:T(8,128)(2,1)} %pad_maximum_fusion.1), calls=%async_computation.3 | async-start | bytes 2097152 | tf_op jit(solution)/shard_map/all_to_all | solution.py:205
  64.8 0.7 copy-start.8
  80.3 23.2 %all-to-all-start.2 = ((bf16[16,320,128]{2,1,0:T(8,128)(2,1)}), bf16[16,320,128]{2,1,0:T(8,128)(2,1)S(1)}, u32[]{:S(2)}, u32[]{:S(2)}) async-start(bf16[16,320,128]{2,1,0:T(8,128)(2,1)} %pad_maximum_fusion), calls=%async_computation.2 | async-start | bytes 2621440 | tf_op jit(solution)/shard_map/all_to_all | solution.py:253
  86.4 17.3 %copy-start = (bf16[16,128,128]{2,1,0:T(8,128)(2,1)S(1)}, bf16[16,128,128]{2,1,0:T(8,128)(2,1)}, u32[]{:S(2)}) copy-start(bf16[16,128,128]{2,1,0:T(8,128)(2,1)} %get-tuple-element.13) | copy-start | bytes 1572868
  103.5 1.0 copy-start.1
  110.7 10.2 %all-to-all-start.5 = ((bf16[16,32,128]{2,1,0:T(8,128)(2,1)}), bf16[16,32,128]{2,1,0:T(8,128)(2,1)S(1)}, u32[]{:S(2)}, u32[]{:S(2)}) async-start(bf16[16,32,128]{2,1,0:T(8,128)(2,1)} %bitcast.34), calls=%async_computation.5 | async-start | bytes 262144 | tf_op jit(solution)/shard_map/all_to_all | solution.py:278

commit v5 on v3

--- a/solution.py
+++ b/solution.py
@@ -95,9 +95,9 @@
         256,
     )
     finals = lax.all_to_all(
-        jnp.broadcast_to(final_local[None], (devices,) + final_local.shape),
+        jnp.broadcast_to(final_local.astype(jnp.bfloat16)[None], (devices,) + final_local.shape),
         "context", 0, 0, tiled=True,
-    )
+    ).astype(jnp.float32)
     source = jnp.arange(devices, dtype=jnp.int32)
     steps = (device_index - 1 - source).astype(jnp.float32)
     carry_weight = jnp.where(
@@ -225,9 +225,11 @@
         * (long_out.astype(jnp.float32) + skip_weight[None, :] * product.astype(jnp.float32))
     ).astype(jnp.bfloat16)
     ways = lax.axis_size("tensor")
-    gathered = lax.all_to_all(
-        jnp.broadcast_to(hidden[None], (ways,) + hidden.shape), "tensor", 0, 0, tiled=True
-    )
+    pieces = [hidden] + [
+        lax.ppermute(hidden, "tensor", [(i, (i - k) % ways) for i in range(ways)])
+        for k in range(1, ways)
+    ]
+    gathered = jnp.roll(jnp.stack(pieces), lax.axis_index("tensor"), axis=0)
     gathered = gathered.transpose(1, 0, 2).reshape(row_count, ways * hidden.shape[1])
     hidden_float = gathered.astype(jnp.float32)
     mean_square = jnp.mean(hidden_float * hidden_float, axis=1, keepdims=True)

time: 134 us -> 134 us (level)
  waiting for transfers between devices: 45.7 us -> 36.8 us
  other arithmetic: 10.8 us -> 15.4 us
  local copies, waits for them, and re-layouts: 8.55 us -> 12.9 us
    all_to_all x2 -> x1, waiting for transfers between devices: 27.4 us -> 7.27 us  [modal_chunk(): lax.all_to_all(jnp.broadcast_to(final_local.astype(jnp.bfloat16)[None], (...]
    ppermute x0 -> x3, waiting for transfers between devices: none -> 12.4 us  [shards(): lax.ppermute(hidden, 'tensor', [(i, (i - k) % ways) for i in range(ways)])]
    unnamed x22 -> x28, local copies, waits for them, and re-layouts: 1.37 us -> 7.18 us
    all_to_all x2 -> x1, starting transfers between devices: 9.94 us -> 5.65 us  [modal_chunk(): lax.all_to_all(jnp.broadcast_to(final_local.astype(jnp.bfloat16)[None], (...]
    ppermute x0 -> x3, starting transfers between devices: none -> 3.67 us  [shards(): lax.ppermute(hidden, 'tensor', [(i, (i - k) % ways) for i in range(ways)])]
    unnamed x1 -> x2, other arithmetic: 0.24 us -> 3.46 us
    broadcast_in_dim x2 -> x1, local copies, waits for them, and re-layouts: 3.06 us -> 0.85 us  [modal_chunk(): jnp.broadcast_to(final_local.astype(jnp.bfloat16)[None], (devices,) + fin...]
  transfers between devices with their start and end apart: 5 -> 7, of which waited for: 4 -> 4; matrix products, arithmetic and copies ran while one was open for 7% -> 15% of each run, Pallas kernels for 8% -> 11%
where the time goes in v5:
time: 134 us; the launch traced here: 133 us
  waiting for transfers between devices  36.8 us (27%)
  Pallas kernels  31.5 us (24%)
  starting transfers between devices  24.7 us (18%)
  other arithmetic  15.4 us (11%)
  local copies, waits for them, and re-layouts  12.9 us (10%)
  blocking collectives  10.5 us (8%)
    all_to_all x1, waiting for transfers between devices, shards(): lax.all_to_all(jnp.concatenate([query_parts, by_head(new_keys), by_head(n...  17.1 us
    ppermute x3, waiting for transfers between devices, shards(): lax.ppermute(hidden, 'tensor', [(i, (i - k) % ways) for i in range(ways)])  12.4 us
    pallas_call x1, Pallas kernels, attend(): pl.pallas_call(functools.partial(attention_kernel, 1.0 / math.sqrt(width)...  10.8 us
    pallas_call x1, Pallas kernels, project(): pl.pallas_call(project_kernel, grid=(groups, width // block), in_specs=[p...  10.6 us
    all_to_all x1, blocking collectives, shards(): back = lax.all_to_all(mine, 'context', 0, 0, tiled=True)  10.5 us
    pallas_call x2, Pallas kernels, channel_blocks(): pl.pallas_call(kernel, grid=(channels // block,), in_specs=specs, out_spe...  10.1 us
    all_to_all x1, waiting for transfers between devices, modal_chunk(): lax.all_to_all(jnp.broadcast_to(final_local.astype(jnp.bfloat16)[None], (...  7.27 us
    unnamed x28, local copies, waits for them, and re-layouts  7.18 us
  transfers between devices with their start and end apart: 7, of which 4 were waited for; matrix products, arithmetic and copies ran while one was open for 15% of the time, Pallas kernels for 11%

profile of v5, /device:TPU:1, one launch (start us, length us, event | category | flops | bytes accessed | tf_op | source)
XLA Modules:
  0.0 132.8 jit_solution(10566756599505682594)
XLA Ops:
  0.8 4.6 %collective-permute-start = (bf16[2,3,1024]{2,0,1:T(2,128)(2,1)S(1)}, bf16[2,3,1024]{2,0,1:T(2,128)(2,1)S(1)}, u32[]{:S(2)}, u32[]{:S(2)}) collective-permute-start(bf16[2,3,1024]{2,0,1:T(2,128)(2,1)S(1)} %slice.68), channel_id=1, source_target_pairs={{0,4},{4,8},{8,12},{12,16},{16,20},{20,24},{24,28},{28,32},{32,36}... | collective-permute-start | bytes 36872 | tf_op jit(solution)/shard_map/ppermute | solution.py:21
  5.4 1.5 %fusion.14 = (f32[16,1024]{1,0:T(8,128)}, f32[16,1024]{1,0:T(8,128)}, f32[16,1024]{1,0:T(8,128)}) fusion(f32[16,1024]{1,0:T(8,128)} %rate_ref.3, f32[16,1024]{1,0:T(8,128)} %param.17), kind=kLoop, calls=%fused_computation.62 | loop fusion | flops 65536 | bytes 327680 | tf_op jit(solution)/shard_map/neg | solution.py:108
  7.8 1.4 %maximum_convert_fusion = f32[130,3,1024]{2,0,1:T(8,128)S(1)} fusion(bf16[128,3,1024]{2,0,1:T(8,128)(2,1)} %param.13, bf16[2,3,1024]{2,0,1:T(2,128)(2,1)S(1)} %broadcast_select_fusion), kind=kLoop, calls=%fused_computation.14 | loop fusion | flops 1597440 | bytes 2396160 | tf_op jit(solution)/shard_map/convert_element_type | solution.py:213
  10.5 6.2 %shard_map.127 = (f32[128,1024]{1,0:T(8,128)}, f32[16,1024]{1,0:T(8,128)}) custom-call(f32[128,1024]{1,0:T(8,128)} %fusion.8.x_ref, f32[16,1024]{1,0:T(8,128)} %rate_ref.3, f32[16,1024]{1,0:T(8,128)} %get-tuple-element.24.rg_ref, f32[16,1024]{1,0:T(8,128)} %get-tuple-element.25.g_ref), custom_call_target="tpu_custom_call" | custom-call | tf_op jit(solution)/shard_map/pallas_call | solution.py:76
  18.4 5.7 %all-to-all-start = ((bf16[16,16,1024]{2,1,0:T(8,128)(2,1)}), bf16[16,16,1024]{2,1,0:T(8,128)(2,1)S(1)}, u32[]{:S(2)}, u32[]{:S(2)}) async-start(bf16[16,16,1024]{2,1,0:T(8,128)(2,1)} %broadcast_in_dim.27), calls=%async_computation | async-start | bytes 1048576 | tf_op jit(solution)/shard_map/all_to_all | solution.py:97
  25.2 1.1 pad_maximum_fusion.1
  26.3 7.3 %all-to-all-done = bf16[16,16,1024]{2,1,0:T(8,128)(2,1)S(1)} async-done(((bf16[16,16,1024]{2,1,0:T(8,128)(2,1)}), bf16[16,16,1024]{2,1,0:T(8,128)(2,1)S(1)}, u32[]{:S(2)}, u32[]{:S(2)}) %all-to-all-start) | async-done | bytes 524320 | tf_op jit(solution)/shard_map/all_to_all | solution.py:97
  33.6 4.9 %all-to-all-start.2 = ((bf16[16,256,128]{2,1,0:T(8,128)(2,1)}), bf16[16,256,128]{2,1,0:T(8,128)(2,1)S(1)}, u32[]{:S(2)}, u32[]{:S(2)}) async-start(bf16[16,256,128]{2,1,0:T(8,128)(2,1)} %pad_maximum_fusion.1), calls=%async_computation.2 | async-start | bytes 2097152 | tf_op jit(solution)/shard_map/all_to_all | solution.py:205
  38.5 1.2 multiply_reduce_fusion
  39.6 1.5 %add_multiply_fusion.weight_ref = f32[16,1024]{1,0:T(8,128)} fusion(f32[16,1024]{1,0:T(8,128)S(1)} %copy-done.4, f32[16,1024]{1,0:T(8,128)S(1)} %multiply_reduce_fusion, f32[16,1024]{1,0:T(8,128)} %param.18, f32[]{:T(128)S(6)} %mul.231, f32[16,1024]{1,0:T(8,128)S(1)} %copy-done.2), kind=kLoop, calls=%fused_computation.44 | loop fusion | flops 81920 | bytes 327684 | tf_op jit(solution)/shard_map/mul | solution.py:112
  41.1 3.9 %shard_map.128 = bf16[128,1024]{1,0:T(8,128)(2,1)} custom-call(f32[128,1024]{1,0:T(8,128)} %get-tuple-element.7.local_ref, f32[16,1024]{1,0:T(8,128)} %rate_ref.3, f32[16,1024]{1,0:T(8,128)} %add_multiply_fusion.weight_ref), custom_call_target="tpu_custom_call" | custom-call | tf_op jit(solution)/shard_map/pallas_call | solution.py:76
  45.0 1.8 %bitcast_dynamic-update-slice_fusion.6 = (bf16[8,128,1024]{2,1,0:T(8,128)(2,1)}, bf16[128,1024]{1,0:T(8,128)(2,1)S(1)}) fusion(f32[1024]{0:T(1024)S(1)} %copy-done.8, bf16[128,1024]{1,0:T(8,128)(2,1)} %shard_map.128, f32[128,3,1024]{2,0,1:T(8,128)S(1)} %fusion.1, bf16[128,1024]{1,0:T(8,128)(2,1)S(1)} %copy-done.3), kind=kLoop, calls=%fused_computation.40 | loop fusion | flops 1310719 | bytes 2625536
  46.9 2.5 %collective-permute-start.1 = (bf16[128,1024]{1,0:T(8,128)(2,1)S(1)}, bf16[128,1024]{1,0:T(8,128)(2,1)S(1)}, u32[]{:S(2)}, u32[]{:S(2)}) collective-permute-start(bf16[128,1024]{1,0:T(8,128)(2,1)S(1)} %get-tuple-element.10), channel_id=1, source_target_pairs={{0,3},{1,0},{2,1},{3,2},{4,7},{5,4},{6,5},{7,6},{8,11},{9,8},{10,9... | collective-permute-start | bytes 786440 | tf_op jit(solution)/shard_map/ppermute | solution.py:229
  50.9 9.4 %collective-permute-done.1 = bf16[128,1024]{1,0:T(8,128)(2,1)S(1)} collective-permute-done((bf16[128,1024]{1,0:T(8,128)(2,1)S(1)}, bf16[128,1024]{1,0:T(8,128)(2,1)S(1)}, u32[]{:S(2)}, u32[]{:S(2)}) %collective-permute-start.1) | collective-permute-done | bytes 262176 | tf_op jit(solution)/shard_map/ppermute | solution.py:229
  61.7 3.0 %collective-permute-done.3 = bf16[128,1024]{1,0:T(8,128)(2,1)S(1)} collective-permute-done((bf16[128,1024]{1,0:T(8,128)(2,1)S(1)}, bf16[128,1024]{1,0:T(8,128)(2,1)S(1)}, u32[]{:S(2)}, u32[]{:S(2)}) %collective-permute-start.3) | collective-permute-done | bytes 262176 | tf_op jit(solution)/shard_map/ppermute | solution.py:229
  68.3 1.6 %convert_bitcast_fusion = f32[4,16,8,1024]{3,2,1,0:T(8,128)S(1)} fusion(bf16[8,128,1024]{2,1,0:T(8,128)(2,1)} %bitcast_dynamic-update-slice_fusion.1, s32[]{:T(128)S(6)} %select_n.46), kind=kLoop, calls=%fused_computation.1 | loop fusion | flops 524288 | bytes 3145732
  71.5 10.6 %shard_map.129 = f32[3,128,1024]{2,1,0:T(8,128)S(1)} custom-call(bf16[128,4096]{1,0:T(8,128)(2,1)S(1)} %multiply_convert_fusion.x_ref, bf16[3,4096,1024]{2,1,0:T(8,128)(2,1)} %bitcast.91), custom_call_target="tpu_custom_call" | custom-call | flops 3221225472 | bytes 27787264 | tf_op jit(solution)/shard_map/pallas_call | solution.py:160
  83.7 1.2 pad_maximum_fusion
  84.9 5.9 %all-to-all-start.1 = ((bf16[16,320,128]{2,1,0:T(8,128)(2,1)}), bf16[16,320,128]{2,1,0:T(8,128)(2,1)S(1)}, u32[]{:S(2)}, u32[]{:S(2)}) async-start(bf16[16,320,128]{2,1,0:T(8,128)(2,1)} %pad_maximum_fusion), calls=%async_computation.1 | async-start | bytes 2621440 | tf_op jit(solution)/shard_map/all_to_all | solution.py:255
  91.4 0.9 fusion.13
  92.3 17.1 %all-to-all-done.1 = bf16[16,320,128]{2,1,0:T(8,128)(2,1)S(1)} async-done(((bf16[16,320,128]{2,1,0:T(8,128)(2,1)}), bf16[16,320,128]{2,1,0:T(8,128)(2,1)S(1)}, u32[]{:S(2)}, u32[]{:S(2)}) %all-to-all-start.1) | async-done | bytes 1310752 | tf_op jit(solution)/shard_map/all_to_all | solution.py:255
  109.4 1.0 copy-done.1
  110.6 10.8 %shard_map.130 = bf16[1024,128]{1,0:T(8,128)(2,1)S(1)} custom-call(bf16[1024,128]{1,0:T(8,128)(2,1)S(1)} %bitcast.89, bf16[4096,128]{1,0:T(8,128)(2,1)S(1)} %get-tuple-element.31.k_ref, bf16[4096,128]{1,0:T(8,128)(2,1)S(1)} %get-tuple-element.32.v_ref, s32[1024,1]{1,0:T(8,128)S(1)} %add.131.qpos_ref, s32[1,4096]{1,0:T(1,128)S(1)} %compare_select_fusion.kpos_ref), custom_call_target="tpu_custom_call" | custom-call | tf_op jit(solution)/shard_map/pallas_call | solution.py:137
  121.4 10.5 %all_to_all.20 = bf16[16,64,128]{2,1,0:T(8,128)(2,1)S(1)} all-to-all(bf16[16,64,128]{2,1,0:T(8,128)(2,1)S(1)} %bitcast.90), channel_id=1, replica_groups=mesh['dp'=2,'context'=16,'tensor'=4] {'context'}, dimensions={0} | all-to-all | bytes 524288 | tf_op jit(solution)/shard_map/all_to_all | solution.py:273
  (72 shorter events, 16.3 us)
Async XLA Ops:
  0.8 6.9 %collective-permute-start = (bf16[2,3,1024]{2,0,1:T(2,128)(2,1)S(1)}, bf16[2,3,1024]{2,0,1:T(2,128)(2,1)S(1)}, u32[]{:S(2)}, u32[]{:S(2)}) collective-permute-start(bf16[2,3,1024]{2,0,1:T(2,128)(2,1)S(1)} %slice.68), channel_id=1, source_target_pairs={{0,4},{4,8},{8,12},{12,16},{16,20},{20,24},{24,28},{28,32},{32,36}... | collective-permute-start | bytes 36872 | tf_op jit(solution)/shard_map/ppermute | solution.py:21
  9.6 15.1 %copy-start.5 = (bf16[128,1024]{1,0:T(8,128)(2,1)S(1)}, bf16[128,1024]{1,0:T(8,128)(2,1)}, u32[]{:S(2)}) copy-start(bf16[128,1024]{1,0:T(8,128)(2,1)} %param.24) | copy-start | bytes 786436
  10.5 14.4 %copy-start.6 = (bf16[128,1024]{1,0:T(8,128)(2,1)S(1)}, bf16[128,1024]{1,0:T(8,128)(2,1)}, u32[]{:S(2)}) copy-start(bf16[128,1024]{1,0:T(8,128)(2,1)} %param.25) | copy-start | bytes 786436
  18.4 15.1 %all-to-all-start = ((bf16[16,16,1024]{2,1,0:T(8,128)(2,1)}), bf16[16,16,1024]{2,1,0:T(8,128)(2,1)S(1)}, u32[]{:S(2)}, u32[]{:S(2)}) async-start(bf16[16,16,1024]{2,1,0:T(8,128)(2,1)} %broadcast_in_dim.27), calls=%async_computation | async-start | bytes 1048576 | tf_op jit(solution)/shard_map/all_to_all | solution.py:97
  25.2 14.4 %copy-start.2 = (f32[16,1024]{1,0:T(8,128)S(1)}, f32[16,1024]{1,0:T(8,128)}, u32[]{:S(2)}) copy-start(f32[16,1024]{1,0:T(8,128)} %rate_ref.3) | copy-start | bytes 196612
  25.2 14.4 %copy-start.4 = (f32[16,1024]{1,0:T(8,128)S(1)}, f32[16,1024]{1,0:T(8,128)}, u32[]{:S(2)}) copy-start(f32[16,1024]{1,0:T(8,128)} %param.17) | copy-start | bytes 196612
  26.3 18.7 %copy-start.3 = (bf16[128,1024]{1,0:T(8,128)(2,1)S(1)}, bf16[128,1024]{1,0:T(8,128)(2,1)}, u32[]{:S(2)}) copy-start(bf16[128,1024]{1,0:T(8,128)(2,1)} %param.20) | copy-start | bytes 786436
  26.3 18.7 %copy-start.8 = (f32[1024]{0:T(1024)S(1)}, f32[1024]{0:T(1024)}, u32[]{:S(2)}) copy-start(f32[1024]{0:T(1024)} %param.19) | copy-start | bytes 12292
  33.6 51.3 %all-to-all-start.2 = ((bf16[16,256,128]{2,1,0:T(8,128)(2,1)}), bf16[16,256,128]{2,1,0:T(8,128)(2,1)S(1)}, u32[]{:S(2)}, u32[]{:S(2)}) async-start(bf16[16,256,128]{2,1,0:T(8,128)(2,1)} %pad_maximum_fusion.1), calls=%async_computation.2 | async-start | bytes 2097152 | tf_op jit(solution)/shard_map/all_to_all | solution.py:205
  46.9 13.4 %collective-permute-start.1 = (bf16[128,1024]{1,0:T(8,128)(2,1)S(1)}, bf16[128,1024]{1,0:T(8,128)(2,1)S(1)}, u32[]{:S(2)}, u32[]{:S(2)}) collective-permute-start(bf16[128,1024]{1,0:T(8,128)(2,1)S(1)} %get-tuple-element.10), channel_id=1, source_target_pairs={{0,3},{1,0},{2,1},{3,2},{4,7},{5,4},{6,5},{7,6},{8,11},{9,8},{10,9... | collective-permute-start | bytes 786440 | tf_op jit(solution)/shard_map/ppermute | solution.py:229
  49.4 11.6 %collective-permute-start.2 = (bf16[128,1024]{1,0:T(8,128)(2,1)S(1)}, bf16[128,1024]{1,0:T(8,128)(2,1)S(1)}, u32[]{:S(2)}, u32[]{:S(2)}) collective-permute-start(bf16[128,1024]{1,0:T(8,128)(2,1)S(1)} %get-tuple-element.10), channel_id=1, source_target_pairs={{0,2},{1,3},{2,0},{3,1},{4,6},{5,7},{6,4},{7,5},{8,10},{9,11},{10,... | collective-permute-start | bytes 786440 | tf_op jit(solution)/shard_map/ppermute | solution.py:229
  50.2 14.5 %collective-permute-start.3 = (bf16[128,1024]{1,0:T(8,128)(2,1)S(1)}, bf16[128,1024]{1,0:T(8,128)(2,1)S(1)}, u32[]{:S(2)}, u32[]{:S(2)}) collective-permute-start(bf16[128,1024]{1,0:T(8,128)(2,1)S(1)} %get-tuple-element.10), channel_id=1, source_target_pairs={{0,1},{1,2},{2,3},{3,0},{4,5},{5,6},{6,7},{7,4},{8,9},{9,10},{10,1... | collective-permute-start | bytes 786440 | tf_op jit(solution)/shard_map/ppermute | solution.py:229
  68.3 1.9 %copy-start = (bf16[8,128,1024]{2,1,0:T(8,128)(2,1)S(1)}, bf16[8,128,1024]{2,1,0:T(8,128)(2,1)}, u32[]{:S(2)}) copy-start(bf16[8,128,1024]{2,1,0:T(8,128)(2,1)} %bitcast_dynamic-update-slice_fusion.1) | copy-start | bytes 6291460
  70.5 0.7 copy-start.7
  84.9 24.5 %all-to-all-start.1 = ((bf16[16,320,128]{2,1,0:T(8,128)(2,1)}), bf16[16,320,128]{2,1,0:T(8,128)(2,1)S(1)}, u32[]{:S(2)}, u32[]{:S(2)}) async-start(bf16[16,320,128]{2,1,0:T(8,128)(2,1)} %pad_maximum_fusion), calls=%async_computation.1 | async-start | bytes 2621440 | tf_op jit(solution)/shard_map/all_to_all | solution.py:255
  109.4 1.0 copy-start.1

commit v6 on v3

--- a/solution.py
+++ b/solution.py
@@ -95,9 +95,9 @@
         256,
     )
     finals = lax.all_to_all(
-        jnp.broadcast_to(final_local[None], (devices,) + final_local.shape),
+        jnp.broadcast_to(final_local.astype(jnp.bfloat16)[None], (devices,) + final_local.shape),
         "context", 0, 0, tiled=True,
-    )
+    ).astype(jnp.float32)
     source = jnp.arange(devices, dtype=jnp.int32)
     steps = (device_index - 1 - source).astype(jnp.float32)
     carry_weight = jnp.where(
@@ -116,38 +116,48 @@
     return long_out
 
 
-def attention_kernel(scale, q_ref, k_ref, v_ref, qpos_ref, kpos_ref, out_ref):
-    scores = (
-        lax.dot_general(
-            q_ref[...], k_ref[...], (((1,), (1,)), ((), ())), preferred_element_type=jnp.float32
-        )
-        * scale
-    )
-    visible = kpos_ref[...] <= qpos_ref[...]
-    row_max = jnp.max(jnp.where(visible, scores, -jnp.inf), axis=1, keepdims=True)
-    weights = jnp.where(visible, jnp.exp(scores - row_max), 0.0).astype(jnp.bfloat16)
-    weight_sum = jnp.sum(weights.astype(jnp.float32), axis=1, keepdims=True)
-    numerator = jnp.dot(weights, v_ref[...], preferred_element_type=jnp.float32)
-    out_ref[...] = (numerator / weight_sum).astype(out_ref.dtype)
-
-
-def attend(queries, keys, values, query_pos, key_pos, block=256):
+def attention_kernel(scale, history, q_ref, k_ref, v_ref, qpos_ref, out_ref):
+    q = q_ref[...]
+    contract = (((1,), (1,)), ((), ()))
+    old_scores = (
+        lax.dot_general(q, k_ref[:history], contract, preferred_element_type=jnp.float32) * scale
+    )
+    new_scores = (
+        lax.dot_general(q, k_ref[history:], contract, preferred_element_type=jnp.float32) * scale
+    )
+    new_pos = lax.broadcasted_iota(jnp.int32, (1, new_scores.shape[1]), 1)
+    new_scores = jnp.where(new_pos <= qpos_ref[...], new_scores, -jnp.inf)
+    row_max = jnp.maximum(
+        jnp.max(old_scores, axis=1, keepdims=True), jnp.max(new_scores, axis=1, keepdims=True)
+    )
+    old_w = jnp.exp(old_scores - row_max).astype(jnp.bfloat16)
+    new_w = jnp.exp(new_scores - row_max).astype(jnp.bfloat16)
+    ones = jnp.ones((history, 128), jnp.bfloat16)
+    weight_sum = jnp.dot(old_w, ones, preferred_element_type=jnp.float32) + jnp.dot(
+        new_w, ones[: new_w.shape[1]], preferred_element_type=jnp.float32
+    )
+    numerator = jnp.dot(old_w, v_ref[:history], preferred_element_type=jnp.float32) + jnp.dot(
+        new_w, v_ref[history:], preferred_element_type=jnp.float32
+    )
+    out_ref[...] = (numerator / weight_sum[:, :1]).astype(out_ref.dtype)
+
+
+def attend(queries, keys, values, query_pos, history, block=256):
     rows, width = queries.shape
     key_rows = keys.shape[0]
     return pl.pallas_call(
-        functools.partial(attention_kernel, 1.0 / math.sqrt(width)),
+        functools.partial(attention_kernel, 1.0 / math.sqrt(width), history),
         grid=(rows // block,),
         in_specs=[
             pl.BlockSpec((block, width), lambda i: (i, 0)),
             pl.BlockSpec((key_rows, width), lambda i: (0, 0)),
             pl.BlockSpec((key_rows, width), lambda i: (0, 0)),
             pl.BlockSpec((block, 1), lambda i: (i, 0)),
-            pl.BlockSpec((1, key_rows), lambda i: (0, 0)),
         ],
         out_specs=pl.BlockSpec((block, width), lambda i: (i, 0)),
         out_shape=jax.ShapeDtypeStruct((rows, width), jnp.bfloat16),
         compiler_params=pltpu.CompilerParams(vmem_limit_bytes=48 * 1024 * 1024),
-    )(queries, keys, values, query_pos.reshape(rows, 1), key_pos.reshape(1, key_rows))
+    )(queries, keys, values, query_pos.reshape(rows, 1))
 
 
 def project_kernel(x_ref, w_ref, out_ref):
@@ -262,12 +272,10 @@
     all_k = jnp.concatenate([cache_k.reshape(-1, HEAD), new_k.reshape(-1, HEAD)], axis=0)
     all_v = jnp.concatenate([cache_v.reshape(-1, HEAD), new_v.reshape(-1, HEAD)], axis=0)
     q_flat = my_queries.reshape(-1, HEAD)
-    key_index = jnp.arange(all_k.shape[0], dtype=jnp.int32)
-    key_pos = jnp.where(key_index < hist_rows, -1, key_index - hist_rows)
     src = jnp.arange(devices, dtype=jnp.int32)[:, None]
     row = jnp.arange(half_rows, dtype=jnp.int32)[None, :]
     query_pos = (src * row_count + (device_index % 2) * half_rows + row).reshape(-1)
-    mine = attend(q_flat, all_k, all_v, query_pos, key_pos).reshape(devices, half_rows, HEAD)
+    mine = attend(q_flat, all_k, all_v, query_pos, hist_rows).reshape(devices, half_rows, HEAD)
     back = lax.all_to_all(mine, "context", 0, 0, tiled=True)
     attended = (
         back.reshape(heads_here, 2, half_rows, HEAD)

time: 134 us -> 127 us (0.948)
  waiting for transfers between devices: 45.7 us -> 38.7 us
    all_to_all x1, waiting for transfers between devices: 15.7 us -> 9.47 us  [modal_chunk(): lax.all_to_all(jnp.broadcast_to(final_local.astype(jnp.bfloat16)[None], (...]
where the time goes in v6:
time: 127 us; the launch traced here: 126 us
  waiting for transfers between devices  38.7 us (30%)
  Pallas kernels  31.8 us (25%)
  starting transfers between devices  25.1 us (20%)
  other arithmetic  11.6 us (9%)
  blocking collectives  10.5 us (8%)
  local copies, waits for them, and re-layouts  7.48 us (6%)
    all_to_all x1, waiting for transfers between devices, shards(): lax.all_to_all(jnp.concatenate([query_parts, by_head(new_keys), by_head(n...  17.1 us
    pallas_call x1, Pallas kernels, attend(): pl.pallas_call(functools.partial(attention_kernel, 1.0 / math.sqrt(width)...  11.1 us
    all_to_all x1, waiting for transfers between devices, shards(): lax.all_to_all(jnp.broadcast_to(hidden[None], (ways,) + hidden.shape), 't...  11 us
    pallas_call x1, Pallas kernels, project(): pl.pallas_call(project_kernel, grid=(groups, width // block), in_specs=[p...  10.6 us
    all_to_all x1, blocking collectives, shards(): back = lax.all_to_all(mine, 'context', 0, 0, tiled=True)  10.5 us
    pallas_call x2, Pallas kernels, channel_blocks(): pl.pallas_call(kernel, grid=(channels // block,), in_specs=specs, out_spe...  10.1 us
    all_to_all x1, waiting for transfers between devices, modal_chunk(): lax.all_to_all(jnp.broadcast_to(final_local.astype(jnp.bfloat16)[None], (...  9.47 us
    all_to_all x1, starting transfers between devices, shards(): lax.all_to_all(jnp.concatenate([by_head(cache_keys), by_head(cache_values...  6.07 us
  transfers between devices with their start and end apart: 5, of which 4 were waited for; matrix products, arithmetic and copies ran while one was open for 7% of the time, Pallas kernels for 8%

profile of v6, /device:TPU:1, one launch (start us, length us, event | category | flops | bytes accessed | tf_op | source)
XLA Modules:
  0.0 126.2 jit_solution(743356998722515315)
XLA Ops:
  0.8 4.6 %collective-permute-start = (bf16[2,3,1024]{2,0,1:T(2,128)(2,1)S(1)}, bf16[2,3,1024]{2,0,1:T(2,128)(2,1)S(1)}, u32[]{:S(2)}, u32[]{:S(2)}) collective-permute-start(bf16[2,3,1024]{2,0,1:T(2,128)(2,1)S(1)} %slice.68), channel_id=1, source_target_pairs={{0,4},{4,8},{8,12},{12,16},{16,20},{20,24},{24,28},{28,32},{32,36}... | collective-permute-start | bytes 36872 | tf_op jit(solution)/shard_map/ppermute | solution.py:21
  5.4 1.6 %fusion.13 = (f32[16,1024]{1,0:T(8,128)S(1)}, f32[16,1024]{1,0:T(8,128)}, f32[16,1024]{1,0:T(8,128)}) fusion(f32[16,1024]{1,0:T(8,128)} %rate_ref.3, f32[16,1024]{1,0:T(8,128)} %param.17), kind=kLoop, calls=%fused_computation.52 | loop fusion | flops 65536 | bytes 327680 | tf_op jit(solution)/shard_map/neg | solution.py:108
  7.8 1.4 %maximum_convert_fusion = f32[130,3,1024]{2,0,1:T(8,128)S(1)} fusion(bf16[128,3,1024]{2,0,1:T(8,128)(2,1)} %param.13, bf16[2,3,1024]{2,0,1:T(2,128)(2,1)S(1)} %broadcast_select_fusion), kind=kLoop, calls=%fused_computation.14 | loop fusion | flops 1597440 | bytes 2396160 | tf_op jit(solution)/shard_map/convert_element_type | solution.py:223
  9.6 0.8 fusion.8.x_ref
  10.5 6.2 %shard_map.127 = (f32[128,1024]{1,0:T(8,128)}, f32[16,1024]{1,0:T(8,128)}) custom-call(f32[128,1024]{1,0:T(8,128)} %fusion.8.x_ref, f32[16,1024]{1,0:T(8,128)} %rate_ref.3, f32[16,1024]{1,0:T(8,128)} %get-tuple-element.22.rg_ref, f32[16,1024]{1,0:T(8,128)} %get-tuple-element.23.g_ref), custom_call_target="tpu_custom_call" | custom-call | tf_op jit(solution)/shard_map/pallas_call | solution.py:76
  16.7 0.8 convert_element_type.75
  17.6 0.8 broadcast_in_dim.26
  18.4 5.7 %all-to-all-start = ((bf16[16,16,1024]{2,1,0:T(8,128)(2,1)}), bf16[16,16,1024]{2,1,0:T(8,128)(2,1)S(1)}, u32[]{:S(2)}, u32[]{:S(2)}) async-start(bf16[16,16,1024]{2,1,0:T(8,128)(2,1)} %broadcast_in_dim.26), calls=%async_computation | async-start | bytes 1048576 | tf_op jit(solution)/shard_map/all_to_all | solution.py:97
  24.1 9.5 %all-to-all-done = bf16[16,16,1024]{2,1,0:T(8,128)(2,1)S(1)} async-done(((bf16[16,16,1024]{2,1,0:T(8,128)(2,1)}), bf16[16,16,1024]{2,1,0:T(8,128)(2,1)S(1)}, u32[]{:S(2)}, u32[]{:S(2)}) %all-to-all-start) | async-done | bytes 524320 | tf_op jit(solution)/shard_map/all_to_all | solution.py:97
  34.6 3.9 %shard_map.128 = bf16[128,1024]{1,0:T(8,128)(2,1)} custom-call(f32[128,1024]{1,0:T(8,128)} %get-tuple-element.7.local_ref, f32[16,1024]{1,0:T(8,128)} %rate_ref.3, f32[16,1024]{1,0:T(8,128)} %add_multiply_fusion.weight_ref), custom_call_target="tpu_custom_call" | custom-call | tf_op jit(solution)/shard_map/pallas_call | solution.py:76
  38.5 1.1 fusion.6
  39.7 1.1 broadcast_in_dim.27
  40.8 4.1 %all-to-all-start.1 = ((bf16[4,128,1024]{2,1,0:T(8,128)(2,1)}), bf16[4,128,1024]{2,1,0:T(8,128)(2,1)S(1)}, u32[]{:S(2)}, u32[]{:S(2)}) async-start(bf16[4,128,1024]{2,1,0:T(8,128)(2,1)} %broadcast_in_dim.27), calls=%async_computation.1 | async-start | bytes 2097152 | tf_op jit(solution)/shard_map/all_to_all | solution.py:238
  46.0 1.1 pad_maximum_fusion.1
  47.4 11.0 %all-to-all-done.1 = bf16[4,128,1024]{2,1,0:T(8,128)(2,1)S(1)} async-done(((bf16[4,128,1024]{2,1,0:T(8,128)(2,1)}), bf16[4,128,1024]{2,1,0:T(8,128)(2,1)S(1)}, u32[]{:S(2)}, u32[]{:S(2)}) %all-to-all-start.1) | async-done | bytes 1048608 | tf_op jit(solution)/shard_map/all_to_all | solution.py:238
  58.4 6.1 %all-to-all-start.3 = ((bf16[16,256,128]{2,1,0:T(8,128)(2,1)}), bf16[16,256,128]{2,1,0:T(8,128)(2,1)S(1)}, u32[]{:S(2)}, u32[]{:S(2)}) async-start(bf16[16,256,128]{2,1,0:T(8,128)(2,1)} %pad_maximum_fusion.1), calls=%async_computation.3 | async-start | bytes 2097152 | tf_op jit(solution)/shard_map/all_to_all | solution.py:215
  65.7 10.6 %shard_map.129 = f32[3,128,1024]{2,1,0:T(8,128)S(1)} custom-call(bf16[128,4096]{1,0:T(8,128)(2,1)S(1)} %multiply_convert_fusion.x_ref, bf16[3,4096,1024]{2,1,0:T(8,128)(2,1)} %bitcast.78), custom_call_target="tpu_custom_call" | custom-call | flops 3221225472 | bytes 27787264 | tf_op jit(solution)/shard_map/pallas_call | solution.py:170
  78.0 1.2 pad_maximum_fusion
  79.1 1.1 all-to-all-done.3
  80.3 4.6 %all-to-all-start.2 = ((bf16[16,320,128]{2,1,0:T(8,128)(2,1)}), bf16[16,320,128]{2,1,0:T(8,128)(2,1)S(1)}, u32[]{:S(2)}, u32[]{:S(2)}) async-start(bf16[16,320,128]{2,1,0:T(8,128)(2,1)} %pad_maximum_fusion), calls=%async_computation.2 | async-start | bytes 2621440 | tf_op jit(solution)/shard_map/all_to_all | solution.py:263
  85.4 0.9 fusion.12
  86.3 17.1 %all-to-all-done.2 = bf16[16,320,128]{2,1,0:T(8,128)(2,1)S(1)} async-done(((bf16[16,320,128]{2,1,0:T(8,128)(2,1)}), bf16[16,320,128]{2,1,0:T(8,128)(2,1)S(1)}, u32[]{:S(2)}, u32[]{:S(2)}) %all-to-all-start.2) | async-done | bytes 1310752 | tf_op jit(solution)/shard_map/all_to_all | solution.py:263
  103.7 11.1 %shard_map.130 = bf16[1024,128]{1,0:T(8,128)(2,1)S(1)} custom-call(bf16[1024,128]{1,0:T(8,128)(2,1)S(1)} %bitcast.76, bf16[4096,128]{1,0:T(8,128)(2,1)S(1)} %get-tuple-element.29.k_ref, bf16[4096,128]{1,0:T(8,128)(2,1)S(1)} %get-tuple-element.30.v_ref, s32[1024,1]{1,0:T(8,128)S(1)} %add.111.qpos_ref), custom_call_target="tpu_custom_call" | custom-call | tf_op jit(solution)/shard_map/pallas_call | solution.py:148
  114.8 10.5 %all_to_all.25 = bf16[16,64,128]{2,1,0:T(8,128)(2,1)S(1)} all-to-all(bf16[16,64,128]{2,1,0:T(8,128)(2,1)S(1)} %bitcast.77), channel_id=1, replica_groups=mesh['dp'=2,'context'=16,'tensor'=4] {'context'}, dimensions={0} | all-to-all | bytes 524288 | tf_op jit(solution)/shard_map/all_to_all | solution.py:279
  (61 shorter events, 8.2 us)
Async XLA Ops:
  0.8 6.9 %collective-permute-start = (bf16[2,3,1024]{2,0,1:T(2,128)(2,1)S(1)}, bf16[2,3,1024]{2,0,1:T(2,128)(2,1)S(1)}, u32[]{:S(2)}, u32[]{:S(2)}) collective-permute-start(bf16[2,3,1024]{2,0,1:T(2,128)(2,1)S(1)} %slice.68), channel_id=1, source_target_pairs={{0,4},{4,8},{8,12},{12,16},{16,20},{20,24},{24,28},{28,32},{32,36}... | collective-permute-start | bytes 36872 | tf_op jit(solution)/shard_map/ppermute | solution.py:21
  10.5 23.4 %copy-start.1 = (f32[16,1024]{1,0:T(8,128)S(1)}, f32[16,1024]{1,0:T(8,128)}, u32[]{:S(2)}) copy-start(f32[16,1024]{1,0:T(8,128)} %rate_ref.3) | copy-start | bytes 196612
  10.5 23.4 %copy-start.3 = (f32[16,1024]{1,0:T(8,128)S(1)}, f32[16,1024]{1,0:T(8,128)}, u32[]{:S(2)}) copy-start(f32[16,1024]{1,0:T(8,128)} %param.17) | copy-start | bytes 196612
  10.5 23.5 %copy-start.6 = (f32[16,1024]{1,0:T(8,128)S(1)}, f32[16,1024]{1,0:T(8,128)}, u32[]{:S(2)}) copy-start(f32[16,1024]{1,0:T(8,128)} %param.18) | copy-start | bytes 196612
  17.6 20.9 %copy-start.2 = (bf16[128,1024]{1,0:T(8,128)(2,1)S(1)}, bf16[128,1024]{1,0:T(8,128)(2,1)}, u32[]{:S(2)}) copy-start(bf16[128,1024]{1,0:T(8,128)(2,1)} %param.20) | copy-start | bytes 786436
  17.6 20.9 %copy-start.8 = (f32[1024]{0:T(1024)S(1)}, f32[1024]{0:T(1024)}, u32[]{:S(2)}) copy-start(f32[1024]{0:T(1024)} %param.19) | copy-start | bytes 12292
  18.4 15.2 %all-to-all-start = ((bf16[16,16,1024]{2,1,0:T(8,128)(2,1)}), bf16[16,16,1024]{2,1,0:T(8,128)(2,1)S(1)}, u32[]{:S(2)}, u32[]{:S(2)}) async-start(bf16[16,16,1024]{2,1,0:T(8,128)(2,1)} %broadcast_in_dim.26), calls=%async_computation | async-start | bytes 1048576 | tf_op jit(solution)/shard_map/all_to_all | solution.py:97
  39.6 5.9 %copy-start.4 = (bf16[128,1024]{1,0:T(8,128)(2,1)S(1)}, bf16[128,1024]{1,0:T(8,128)(2,1)}, u32[]{:S(2)}) copy-start(bf16[128,1024]{1,0:T(8,128)(2,1)} %param.25) | copy-start | bytes 786436
  40.8 4.9 %copy-start.5 = (bf16[128,1024]{1,0:T(8,128)(2,1)S(1)}, bf16[128,1024]{1,0:T(8,128)(2,1)}, u32[]{:S(2)}) copy-start(bf16[128,1024]{1,0:T(8,128)(2,1)} %param.24) | copy-start | bytes 786436
  40.8 17.6 %all-to-all-start.1 = ((bf16[4,128,1024]{2,1,0:T(8,128)(2,1)}), bf16[4,128,1024]{2,1,0:T(8,128)(2,1)S(1)}, u32[]{:S(2)}, u32[]{:S(2)}) async-start(bf16[4,128,1024]{2,1,0:T(8,128)(2,1)} %broadcast_in_dim.27), calls=%async_computation.1 | async-start | bytes 2097152 | tf_op jit(solution)/shard_map/all_to_all | solution.py:238
  58.4 21.9 %all-to-all-start.3 = ((bf16[16,256,128]{2,1,0:T(8,128)(2,1)}), bf16[16,256,128]{2,1,0:T(8,128)(2,1)S(1)}, u32[]{:S(2)}, u32[]{:S(2)}) async-start(bf16[16,256,128]{2,1,0:T(8,128)(2,1)} %pad_maximum_fusion.1), calls=%async_computation.3 | async-start | bytes 2097152 | tf_op jit(solution)/shard_map/all_to_all | solution.py:215
  64.7 0.7 copy-start.7
  80.3 23.2 %all-to-all-start.2 = ((bf16[16,320,128]{2,1,0:T(8,128)(2,1)}), bf16[16,320,128]{2,1,0:T(8,128)(2,1)S(1)}, u32[]{:S(2)}, u32[]{:S(2)}) async-start(bf16[16,320,128]{2,1,0:T(8,128)(2,1)} %pad_maximum_fusion), calls=%async_computation.2 | async-start | bytes 2621440 | tf_op jit(solution)/shard_map/all_to_all | solution.py:263
  86.3 17.2 %copy-start = (bf16[16,128,128]{2,1,0:T(8,128)(2,1)S(1)}, bf16[16,128,128]{2,1,0:T(8,128)(2,1)}, u32[]{:S(2)}) copy-start(bf16[16,128,128]{2,1,0:T(8,128)(2,1)} %get-tuple-element.14) | copy-start | bytes 1572868

commit v7 on v6

--- a/solution.py
+++ b/solution.py
@@ -35,10 +35,26 @@
     )
 
 
-def local_modes_kernel(x_ref, rate_ref, rg_ref, g_ref, out_ref, final_ref):
-    length = x_ref.shape[0]
+def front_kernel(
+    s_ref, b_ref, tap_ref, rate_ref, rg_ref, g_ref, prod_ref, f1_ref, out_ref, fin_ref, fin_scr
+):
+    length = s_ref.shape[1]
     mode_count = rate_ref.shape[0]
-    x = x_ref[...]
+    row = lax.broadcasted_iota(jnp.int32, (length, s_ref.shape[2]), 0)
+    filtered = []
+    for i in range(3):
+        now = s_ref[i].astype(jnp.float32)
+        before = b_ref[i].astype(jnp.float32)
+        back1 = jnp.where(row == 0, before[1:2], pltpu.roll(now, 1, 0))
+        back2 = jnp.where(
+            row == 0, before[0:1], jnp.where(row == 1, before[1:2], pltpu.roll(now, 2, 0))
+        )
+        taps = tap_ref[:, i, :]
+        filtered.append(taps[0:1] * now + taps[1:2] * back1 + taps[2:3] * back2)
+    product = (filtered[0] * filtered[2]).astype(jnp.bfloat16)
+    prod_ref[...] = product
+    f1_ref[...] = filtered[1]
+    x = product.astype(jnp.float32)
     rows = lax.broadcasted_iota(jnp.int32, (length, length), 0)
     cols = lax.broadcasted_iota(jnp.int32, (length, length), 1)
     lower = (rows >= cols).astype(jnp.bfloat16)
@@ -53,67 +69,51 @@
             lower, low, preferred_element_type=jnp.float32
         )
         total = total + rg_ref[m : m + 1, :] * jnp.exp(-rate * offsets) * prefix
-        final_ref[m : m + 1, :] = (
+        fin_scr[m : m + 1, :] = (
             g_ref[m : m + 1, :] * jnp.exp(-rate * (length - 1.0)) * prefix[length - 1 : length, :]
         )
     out_ref[...] = total
-
-
-def carried_kernel(local_ref, rate_ref, weight_ref, out_ref):
+    fin_ref[...] = jnp.broadcast_to(fin_scr[...][None], fin_ref.shape).astype(fin_ref.dtype)
+
+
+def back_kernel(
+    local_ref, rate_ref, res_ref, fin_ref, hs_ref, steps_ref, mask_ref, first_ref,
+    f1_ref, prod_ref, resid_ref, skip_ref, out_ref,
+):
     length = local_ref.shape[0]
     mode_count = rate_ref.shape[0]
+    rates = rate_ref[...]
+    incoming = jnp.exp(-rates * first_ref[...]) * hs_ref[...]
+    for src in range(fin_ref.shape[0]):
+        incoming = incoming + mask_ref[src : src + 1, :] * jnp.exp(
+            -rates * steps_ref[src : src + 1, :]
+        ) * fin_ref[src].astype(jnp.float32)
+    weight = res_ref[...] * incoming
     steps = lax.broadcasted_iota(jnp.int32, (length, 1), 0).astype(jnp.float32) + 1.0
     total = local_ref[...]
     for m in range(mode_count):
-        total = total + weight_ref[m : m + 1, :] * jnp.exp(-rate_ref[m : m + 1, :] * steps)
-    out_ref[...] = total.astype(out_ref.dtype)
-
-
-def channel_blocks(kernel, inputs, outputs, block):
-    channels = inputs[0].shape[1]
-    specs = [pl.BlockSpec((a.shape[0], block), lambda j: (0, j)) for a in inputs]
-    out_specs = [pl.BlockSpec((o.shape[0], block), lambda j: (0, j)) for o in outputs]
+        total = total + weight[m : m + 1, :] * jnp.exp(-rates[m : m + 1, :] * steps)
+    long_out = total.astype(jnp.bfloat16).astype(jnp.float32)
+    hidden = (
+        resid_ref[...].astype(jnp.float32)
+        + f1_ref[...] * (long_out + skip_ref[...] * prod_ref[...].astype(jnp.float32))
+    ).astype(out_ref.dtype)
+    out_ref[...] = jnp.broadcast_to(hidden[None], out_ref.shape)
+
+
+def channel_blocks(kernel, inputs, outputs, block, scratch=()):
+    def spec(shape):
+        lead = tuple(0 for _ in shape[:-1])
+        return pl.BlockSpec(tuple(shape[:-1]) + (block,), lambda j: lead + (j,))
+
     return pl.pallas_call(
         kernel,
-        grid=(channels // block,),
-        in_specs=specs,
-        out_specs=out_specs,
+        grid=(outputs[0].shape[-1] // block,),
+        in_specs=[spec(a.shape) for a in inputs],
+        out_specs=[spec(o.shape) for o in outputs],
         out_shape=outputs,
+        scratch_shapes=list(scratch),
     )(*inputs)
-
-
-def modal_chunk(signal, mode_rates, mode_residues, hyena_state, device_index, devices):
-    length, channels = signal.shape
-    mode_gain = jnp.sqrt(1.0 - jnp.exp(-2.0 * mode_rates))
-    local_out, final_local = channel_blocks(
-        local_modes_kernel,
-        [signal, mode_rates, mode_residues * mode_gain, mode_gain],
-        [
-            jax.ShapeDtypeStruct((length, channels), jnp.float32),
-            jax.ShapeDtypeStruct(mode_rates.shape, jnp.float32),
-        ],
-        256,
-    )
-    finals = lax.all_to_all(
-        jnp.broadcast_to(final_local.astype(jnp.bfloat16)[None], (devices,) + final_local.shape),
-        "context", 0, 0, tiled=True,
-    ).astype(jnp.float32)
-    source = jnp.arange(devices, dtype=jnp.int32)
-    steps = (device_index - 1 - source).astype(jnp.float32)
-    carry_weight = jnp.where(
-        (source < device_index)[:, None, None],
-        jnp.exp(-mode_rates[None] * (length * jnp.maximum(steps, 0.0))[:, None, None]),
-        0.0,
-    )
-    incoming = jnp.exp(-mode_rates * (length * device_index.astype(jnp.float32))) * hyena_state
-    incoming = incoming + jnp.sum(carry_weight * finals, axis=0)
-    (long_out,) = channel_blocks(
-        carried_kernel,
-        [local_out, mode_rates, mode_residues * incoming],
-        [jax.ShapeDtypeStruct((length, channels), jnp.bfloat16)],
-        256,
-    )
-    return long_out
 
 
 def attention_kernel(scale, history, q_ref, k_ref, v_ref, qpos_ref, out_ref):
@@ -220,25 +220,56 @@
 
     before = shifted(streams[row_count - (tap_count - 1) :], "context", 1)
     before = jnp.where(device_index == 0, stream_tail, before)
-    extended = jnp.concatenate([before, streams], axis=0).astype(jnp.float32)
-    filtered = jnp.zeros(streams.shape, jnp.float32)
-    for step_back in range(tap_count):
-        begin = tap_count - 1 - step_back
-        filtered = filtered + short_taps[step_back][None] * extended[begin : begin + row_count]
-    product = (filtered[:, 0] * filtered[:, 2]).astype(jnp.bfloat16)
-    long_out = modal_chunk(
-        product.astype(jnp.float32), decay_rates, residues, hyena_state, device_index, devices
-    )
-    hidden = (
-        residual.astype(jnp.float32)
-        + filtered[:, 1]
-        * (long_out.astype(jnp.float32) + skip_weight[None, :] * product.astype(jnp.float32))
-    ).astype(jnp.bfloat16)
+    channels = streams.shape[2]
+    mode_count = decay_rates.shape[0]
     ways = lax.axis_size("tensor")
-    gathered = lax.all_to_all(
-        jnp.broadcast_to(hidden[None], (ways,) + hidden.shape), "tensor", 0, 0, tiled=True
-    )
-    gathered = gathered.transpose(1, 0, 2).reshape(row_count, ways * hidden.shape[1])
+    mode_gain = jnp.sqrt(1.0 - jnp.exp(-2.0 * decay_rates))
+    block = 256
+    product, filtered1, local_out, finals_out = channel_blocks(
+        front_kernel,
+        [
+            streams.transpose(1, 0, 2),
+            before.transpose(1, 0, 2),
+            short_taps,
+            decay_rates,
+            residues * mode_gain,
+            mode_gain,
+        ],
+        [
+            jax.ShapeDtypeStruct((row_count, channels), jnp.bfloat16),
+            jax.ShapeDtypeStruct((row_count, channels), jnp.float32),
+            jax.ShapeDtypeStruct((row_count, channels), jnp.float32),
+            jax.ShapeDtypeStruct((devices, mode_count, channels), jnp.bfloat16),
+        ],
+        block,
+        [pltpu.VMEM((mode_count, block), jnp.float32)],
+    )
+    finals = lax.all_to_all(finals_out, "context", 0, 0, tiled=True)
+    source = jnp.arange(devices, dtype=jnp.int32)
+    earlier = source < device_index
+    steps = jnp.where(earlier, (device_index - 1 - source) * row_count, 0).astype(jnp.float32)
+    ones_row = jnp.ones((1, channels), jnp.float32)
+    (hidden_out,) = channel_blocks(
+        back_kernel,
+        [
+            local_out,
+            decay_rates,
+            residues,
+            finals,
+            hyena_state,
+            steps[:, None] * ones_row,
+            earlier.astype(jnp.float32)[:, None] * ones_row,
+            (device_index * row_count).astype(jnp.float32) * ones_row,
+            filtered1,
+            product,
+            residual,
+            skip_weight[None, :],
+        ],
+        [jax.ShapeDtypeStruct((ways, row_count, channels), jnp.bfloat16)],
+        block,
+    )
+    gathered = lax.all_to_all(hidden_out, "tensor", 0, 0, tiled=True)
+    gathered = gathered.transpose(1, 0, 2).reshape(row_count, ways * channels)
     hidden_float = gathered.astype(jnp.float32)
     mean_square = jnp.mean(hidden_float * hidden_float, axis=1, keepdims=True)
     normed = (hidden_float * lax.rsqrt(mean_square + NORM_EPSILON) * norm_gain[None, :]).astype(

time: 127 us -> 123 us (0.969)
  other arithmetic: 11.6 us -> 6.56 us
  Pallas kernels: 31.8 us -> 33.4 us
    convert_element_type x4 -> x2, other arithmetic: 4.2 us -> 0.01 us  [the longest x1 0.01 us: shards(): jnp.where(earlier, (device_index - 1 - source) * row_count, 0)]
    broadcast_in_dim x2 -> x0, local copies, waits for them, and re-layouts: 1.96 us -> none  [the longest x1 1.12 us: shards(): jnp.broadcast_to(hidden[None], (ways,) + hidden.shape)]
    pallas_call x2, Pallas kernels: 10.1 us -> 11.7 us  [channel_blocks(): pl.pallas_call(kernel, grid=(outputs[0].shape[-1] // block,), in_specs=[s...]
    neg x1 -> x0, other arithmetic: 1.56 us -> none  [modal_chunk(): -mode_rates * (length * device_index.astype(jnp.float32))]
    sqrt x0 -> x1, other arithmetic: none -> 1.55 us  [shards(): mode_gain = jnp.sqrt(1.0 - jnp.exp(-2.0 * decay_rates))]
    mul x1 -> x3, local copies, waits for them, and re-layouts: 0.76 us -> 2.07 us  [the longest x1 0.78 us: shards(): steps[:, None] * ones_row]
  transfers between devices with their start and end apart: 5 -> 5, of which waited for: 4 -> 4; matrix products, arithmetic and copies ran while one was open for 7% -> 7% of each run, Pallas kernels for 8% -> 9%
where the time goes in v7:
time: 123 us
  waiting for transfers between devices  38.7 us (31%)
  Pallas kernels  33.4 us (27%)
  starting transfers between devices  25.6 us (21%)
  blocking collectives  10.5 us (9%)
  local copies, waits for them, and re-layouts  6.8 us (6%)
  other arithmetic  6.56 us (5%)
    all_to_all x1, waiting for transfers between devices, shards(): lax.all_to_all(jnp.concatenate([query_parts, by_head(new_keys), by_head(n...  17.1 us
    pallas_call x2, Pallas kernels, channel_blocks(): pl.pallas_call(kernel, grid=(outputs[0].shape[-1] // block,), in_specs=[s...  11.7 us
    pallas_call x1, Pallas kernels, attend(): pl.pallas_call(functools.partial(attention_kernel, 1.0 / math.sqrt(width)...  11.1 us
    all_to_all x1, waiting for transfers between devices, shards(): gathered = lax.all_to_all(hidden_out, 'tensor', 0, 0, tiled=True)  11 us
    pallas_call x1, Pallas kernels, project(): pl.pallas_call(project_kernel, grid=(groups, width // block), in_specs=[p...  10.6 us
    all_to_all x1, blocking collectives, shards(): back = lax.all_to_all(mine, 'context', 0, 0, tiled=True)  10.5 us
    all_to_all x1, waiting for transfers between devices, shards(): finals = lax.all_to_all(finals_out, 'context', 0, 0, tiled=True)  9.47 us
    all_to_all x1, starting transfers between devices, shards(): finals = lax.all_to_all(finals_out, 'context', 0, 0, tiled=True)  6.2 us
  transfers between devices with their start and end apart: 5, of which 4 were waited for; matrix products, arithmetic and copies ran while one was open for 7% of the time, Pallas kernels for 9%

profile of v7, /device:TPU:1, one launch (start us, length us, event | category | flops | bytes accessed | tf_op | source)
XLA Modules:
  0.0 122.5 jit_solution(13869455425271457174)
XLA Ops:
  0.0 0.8 slice.40
  0.8 4.6 %collective-permute-start = (bf16[2,3,1024]{2,0,1:T(2,128)(2,1)S(1)}, bf16[2,3,1024]{2,0,1:T(2,128)(2,1)S(1)}, u32[]{:S(2)}, u32[]{:S(2)}) collective-permute-start(bf16[2,3,1024]{2,0,1:T(2,128)(2,1)S(1)} %slice.40), channel_id=1, source_target_pairs={{0,4},{4,8},{8,12},{12,16},{16,20},{20,24},{24,28},{28,32},{32,36}... | collective-permute-start | bytes 36872 | tf_op jit(solution)/shard_map/ppermute | solution.py:21
  5.4 1.6 %subtract_sqrt_fusion = (f32[16,1024]{1,0:T(8,128)}, f32[16,1024]{1,0:T(8,128)}) fusion(f32[16,1024]{1,0:T(8,128)} %rate_ref.3, f32[16,1024]{1,0:T(8,128)} %res_ref.1), kind=kLoop, calls=%fused_computation.21 | loop fusion | flops 49152 | bytes 262144 | tf_op jit(solution)/shard_map/sqrt | solution.py:226
  7.0 0.6 fusion.2.b_ref
  7.6 6.9 %shard_map.127 = (bf16[128,1024]{1,0:T(8,128)(2,1)}, f32[128,1024]{1,0:T(8,128)}, f32[128,1024]{1,0:T(8,128)}, bf16[16,16,1024]{2,1,0:T(8,128)(2,1)}) custom-call(bf16[3,128,1024]{2,1,0:T(8,128)(2,1)} %bitcast.80, bf16[3,2,1024]{2,1,0:T(2,128)(2,1)} %fusion.2.b_ref, f32[3,3,1024]{2,1,0:T(4,128)} %tap_ref.1, f32[16,1024]{1,0:T(8,128)} %rate_ref.3, ...), custom_call_target="tpu_custom_call" | custom-call | tf_op jit(solution)/shard_map/pallas_call | solution.py:109
  14.5 6.2 %all-to-all-start = ((bf16[16,16,1024]{2,1,0:T(8,128)(2,1)}), bf16[16,16,1024]{2,1,0:T(8,128)(2,1)S(1)}, u32[]{:S(2)}, u32[]{:S(2)}) async-start(bf16[16,16,1024]{2,1,0:T(8,128)(2,1)} %get-tuple-element.10), calls=%async_computation | async-start | bytes 1048576 | tf_op jit(solution)/shard_map/all_to_all | solution.py:247
  20.7 9.5 %all-to-all-done.fin_ref = bf16[16,16,1024]{2,1,0:T(8,128)(2,1)S(1)} async-done(((bf16[16,16,1024]{2,1,0:T(8,128)(2,1)}), bf16[16,16,1024]{2,1,0:T(8,128)(2,1)S(1)}, u32[]{:S(2)}, u32[]{:S(2)}) %all-to-all-start) | async-done | bytes 524320 | tf_op jit(solution)/shard_map/all_to_all | solution.py:247
  30.2 0.8 mul.160.steps_ref
  31.0 0.7 mul.161.mask_ref
  31.7 0.6 mul.163.first_ref
  32.3 4.8 %shard_map.128 = bf16[4,128,1024]{2,1,0:T(8,128)(2,1)} custom-call(f32[128,1024]{1,0:T(8,128)} %get-tuple-element.9.local_ref, f32[16,1024]{1,0:T(8,128)} %rate_ref.3, f32[16,1024]{1,0:T(8,128)} %res_ref.1, bf16[16,16,1024]{2,1,0:T(8,128)(2,1)} %copy-done, f32[16,1024]{1,0:T(8,128)} %hs_ref.1, f32[16,1024]{1,0:T(8,128)} %mul.160.steps_ref, ...), custom_call_target="tpu_custom_call" | custom-call | tf_op jit(solution)/shard_map/pallas_call | solution.py:109
  37.1 4.2 %all-to-all-start.1 = ((bf16[4,128,1024]{2,1,0:T(8,128)(2,1)}), bf16[4,128,1024]{2,1,0:T(8,128)(2,1)S(1)}, u32[]{:S(2)}, u32[]{:S(2)}) async-start(bf16[4,128,1024]{2,1,0:T(8,128)(2,1)} %shard_map.128), calls=%async_computation.1 | async-start | bytes 2097152 | tf_op jit(solution)/shard_map/all_to_all | solution.py:271
  42.3 1.1 pad_maximum_fusion.1
  43.7 11.0 %all-to-all-done.1 = bf16[4,128,1024]{2,1,0:T(8,128)(2,1)S(1)} async-done(((bf16[4,128,1024]{2,1,0:T(8,128)(2,1)}), bf16[4,128,1024]{2,1,0:T(8,128)(2,1)S(1)}, u32[]{:S(2)}, u32[]{:S(2)}) %all-to-all-start.1) | async-done | bytes 1048608 | tf_op jit(solution)/shard_map/all_to_all | solution.py:271
  54.7 6.1 %all-to-all-start.3 = ((bf16[16,256,128]{2,1,0:T(8,128)(2,1)}), bf16[16,256,128]{2,1,0:T(8,128)(2,1)S(1)}, u32[]{:S(2)}, u32[]{:S(2)}) async-start(bf16[16,256,128]{2,1,0:T(8,128)(2,1)} %pad_maximum_fusion.1), calls=%async_computation.3 | async-start | bytes 2097152 | tf_op jit(solution)/shard_map/all_to_all | solution.py:215
  62.1 10.6 %shard_map.129 = f32[3,128,1024]{2,1,0:T(8,128)S(1)} custom-call(bf16[128,4096]{1,0:T(8,128)(2,1)S(1)} %multiply_convert_fusion.x_ref, bf16[3,4096,1024]{2,1,0:T(8,128)(2,1)} %bitcast.61), custom_call_target="tpu_custom_call" | custom-call | flops 3221225472 | bytes 27787264 | tf_op jit(solution)/shard_map/pallas_call | solution.py:170
  74.3 1.2 pad_maximum_fusion
  75.5 1.1 all-to-all-done.3
  76.6 4.6 %all-to-all-start.2 = ((bf16[16,320,128]{2,1,0:T(8,128)(2,1)}), bf16[16,320,128]{2,1,0:T(8,128)(2,1)S(1)}, u32[]{:S(2)}, u32[]{:S(2)}) async-start(bf16[16,320,128]{2,1,0:T(8,128)(2,1)} %pad_maximum_fusion), calls=%async_computation.2 | async-start | bytes 2621440 | tf_op jit(solution)/shard_map/all_to_all | solution.py:294
  81.8 0.9 fusion.6
  82.7 17.1 %all-to-all-done.2 = bf16[16,320,128]{2,1,0:T(8,128)(2,1)S(1)} async-done(((bf16[16,320,128]{2,1,0:T(8,128)(2,1)}), bf16[16,320,128]{2,1,0:T(8,128)(2,1)S(1)}, u32[]{:S(2)}, u32[]{:S(2)}) %all-to-all-start.2) | async-done | bytes 1310752 | tf_op jit(solution)/shard_map/all_to_all | solution.py:294
  100.0 11.1 %shard_map.130 = bf16[1024,128]{1,0:T(8,128)(2,1)S(1)} custom-call(bf16[1024,128]{1,0:T(8,128)(2,1)S(1)} %bitcast.59, bf16[4096,128]{1,0:T(8,128)(2,1)S(1)} %get-tuple-element.29.k_ref, bf16[4096,128]{1,0:T(8,128)(2,1)S(1)} %get-tuple-element.30.v_ref, s32[1024,1]{1,0:T(8,128)S(1)} %add.91.qpos_ref), custom_call_target="tpu_custom_call" | custom-call | tf_op jit(solution)/shard_map/pallas_call | solution.py:148
  111.1 10.5 %all_to_all.25 = bf16[16,64,128]{2,1,0:T(8,128)(2,1)S(1)} all-to-all(bf16[16,64,128]{2,1,0:T(8,128)(2,1)S(1)} %bitcast.60), channel_id=1, replica_groups=mesh['dp'=2,'context'=16,'tensor'=4] {'context'}, dimensions={0} | all-to-all | bytes 524288 | tf_op jit(solution)/shard_map/all_to_all | solution.py:310
  121.8 0.8 copy.37
  (46 shorter events, 4.4 us)
Async XLA Ops:
  0.8 6.1 %collective-permute-start = (bf16[2,3,1024]{2,0,1:T(2,128)(2,1)S(1)}, bf16[2,3,1024]{2,0,1:T(2,128)(2,1)S(1)}, u32[]{:S(2)}, u32[]{:S(2)}) collective-permute-start(bf16[2,3,1024]{2,0,1:T(2,128)(2,1)S(1)} %slice.40), channel_id=1, source_target_pairs={{0,4},{4,8},{8,12},{12,16},{16,20},{20,24},{24,28},{28,32},{32,36}... | collective-permute-start | bytes 36872 | tf_op jit(solution)/shard_map/ppermute | solution.py:21
  14.5 15.7 %all-to-all-start = ((bf16[16,16,1024]{2,1,0:T(8,128)(2,1)}), bf16[16,16,1024]{2,1,0:T(8,128)(2,1)S(1)}, u32[]{:S(2)}, u32[]{:S(2)}) async-start(bf16[16,16,1024]{2,1,0:T(8,128)(2,1)} %get-tuple-element.10), calls=%async_computation | async-start | bytes 1048576 | tf_op jit(solution)/shard_map/all_to_all | solution.py:247
  30.2 2.1 %copy-start = (bf16[16,16,1024]{2,1,0:T(8,128)(2,1)}, bf16[16,16,1024]{2,1,0:T(8,128)(2,1)S(1)}, u32[]{:S(2)}) copy-start(bf16[16,16,1024]{2,1,0:T(8,128)(2,1)S(1)} %all-to-all-done.fin_ref) | copy-start | bytes 1572868
  32.3 9.6 %copy-start.2 = (bf16[128,1024]{1,0:T(8,128)(2,1)S(1)}, bf16[128,1024]{1,0:T(8,128)(2,1)}, u32[]{:S(2)}) copy-start(bf16[128,1024]{1,0:T(8,128)(2,1)} %param.25) | copy-start | bytes 786436
  37.1 4.9 %copy-start.3 = (bf16[128,1024]{1,0:T(8,128)(2,1)S(1)}, bf16[128,1024]{1,0:T(8,128)(2,1)}, u32[]{:S(2)}) copy-start(bf16[128,1024]{1,0:T(8,128)(2,1)} %param.24) | copy-start | bytes 786436
  37.1 17.6 %all-to-all-start.1 = ((bf16[4,128,1024]{2,1,0:T(8,128)(2,1)}), bf16[4,128,1024]{2,1,0:T(8,128)(2,1)S(1)}, u32[]{:S(2)}, u32[]{:S(2)}) async-start(bf16[4,128,1024]{2,1,0:T(8,128)(2,1)} %shard_map.128), calls=%async_computation.1 | async-start | bytes 2097152 | tf_op jit(solution)/shard_map/all_to_all | solution.py:271
  54.7 21.9 %all-to-all-start.3 = ((bf16[16,256,128]{2,1,0:T(8,128)(2,1)}), bf16[16,256,128]{2,1,0:T(8,128)(2,1)S(1)}, u32[]{:S(2)}, u32[]{:S(2)}) async-start(bf16[16,256,128]{2,1,0:T(8,128)(2,1)} %pad_maximum_fusion.1), calls=%async_computation.3 | async-start | bytes 2097152 | tf_op jit(solution)/shard_map/all_to_all | solution.py:215
  61.0 0.7 copy-start.4
  76.6 23.2 %all-to-all-start.2 = ((bf16[16,320,128]{2,1,0:T(8,128)(2,1)}), bf16[16,320,128]{2,1,0:T(8,128)(2,1)S(1)}, u32[]{:S(2)}, u32[]{:S(2)}) async-start(bf16[16,320,128]{2,1,0:T(8,128)(2,1)} %pad_maximum_fusion), calls=%async_computation.2 | async-start | bytes 2621440 | tf_op jit(solution)/shard_map/all_to_all | solution.py:294
  82.7 17.2 %copy-start.1 = (bf16[16,128,128]{2,1,0:T(8,128)(2,1)S(1)}, bf16[16,128,128]{2,1,0:T(8,128)(2,1)}, u32[]{:S(2)}) copy-start(bf16[16,128,128]{2,1,0:T(8,128)(2,1)} %get-tuple-element.18) | copy-start | bytes 1572868

commit v8 on v7

--- a/solution.py
+++ b/solution.py
@@ -36,7 +36,8 @@
 
 
 def front_kernel(
-    s_ref, b_ref, tap_ref, rate_ref, rg_ref, g_ref, prod_ref, f1_ref, out_ref, fin_ref, fin_scr
+    idx_ref, s_ref, recv_ref, tail_ref, tap_ref, rate_ref, res_ref,
+    prod_ref, f1_ref, out_ref, fin_ref, fin_scr,
 ):
     length = s_ref.shape[1]
     mode_count = rate_ref.shape[0]
@@ -44,7 +45,9 @@
     filtered = []
     for i in range(3):
         now = s_ref[i].astype(jnp.float32)
-        before = b_ref[i].astype(jnp.float32)
+        before = jnp.where(
+            idx_ref[0] == 0, tail_ref[i].astype(jnp.float32), recv_ref[i].astype(jnp.float32)
+        )
         back1 = jnp.where(row == 0, before[1:2], pltpu.roll(now, 1, 0))
         back2 = jnp.where(
             row == 0, before[0:1], jnp.where(row == 1, before[1:2], pltpu.roll(now, 2, 0))
@@ -59,6 +62,8 @@
     cols = lax.broadcasted_iota(jnp.int32, (length, length), 1)
     lower = (rows >= cols).astype(jnp.bfloat16)
     offsets = lax.broadcasted_iota(jnp.int32, (length, 1), 0).astype(jnp.float32)
+    gains = jnp.sqrt(1.0 - jnp.exp(-2.0 * rate_ref[...]))
+    rgains = res_ref[...] * gains
     total = jnp.zeros(x.shape, jnp.float32)
     for m in range(mode_count):
         rate = rate_ref[m : m + 1, :]
@@ -68,26 +73,27 @@
         prefix = jnp.dot(lower, high, preferred_element_type=jnp.float32) + jnp.dot(
             lower, low, preferred_element_type=jnp.float32
         )
-        total = total + rg_ref[m : m + 1, :] * jnp.exp(-rate * offsets) * prefix
+        total = total + rgains[m : m + 1, :] * jnp.exp(-rate * offsets) * prefix
         fin_scr[m : m + 1, :] = (
-            g_ref[m : m + 1, :] * jnp.exp(-rate * (length - 1.0)) * prefix[length - 1 : length, :]
+            gains[m : m + 1, :] * jnp.exp(-rate * (length - 1.0)) * prefix[length - 1 : length, :]
         )
     out_ref[...] = total
     fin_ref[...] = jnp.broadcast_to(fin_scr[...][None], fin_ref.shape).astype(fin_ref.dtype)
 
 
 def back_kernel(
-    local_ref, rate_ref, res_ref, fin_ref, hs_ref, steps_ref, mask_ref, first_ref,
+    idx_ref, local_ref, rate_ref, res_ref, fin_ref, hs_ref,
     f1_ref, prod_ref, resid_ref, skip_ref, out_ref,
 ):
     length = local_ref.shape[0]
     mode_count = rate_ref.shape[0]
     rates = rate_ref[...]
-    incoming = jnp.exp(-rates * first_ref[...]) * hs_ref[...]
+    me = idx_ref[0]
+    incoming = jnp.exp(-rates * (me * length).astype(jnp.float32)) * hs_ref[...]
     for src in range(fin_ref.shape[0]):
-        incoming = incoming + mask_ref[src : src + 1, :] * jnp.exp(
-            -rates * steps_ref[src : src + 1, :]
-        ) * fin_ref[src].astype(jnp.float32)
+        steps_back = (jnp.maximum(me - 1 - src, 0) * length).astype(jnp.float32)
+        weight_src = jnp.where(src < me, jnp.exp(-rates * steps_back), 0.0)
+        incoming = incoming + weight_src * fin_ref[src].astype(jnp.float32)
     weight = res_ref[...] * incoming
     steps = lax.broadcasted_iota(jnp.int32, (length, 1), 0).astype(jnp.float32) + 1.0
     total = local_ref[...]
@@ -101,19 +107,19 @@
     out_ref[...] = jnp.broadcast_to(hidden[None], out_ref.shape)
 
 
-def channel_blocks(kernel, inputs, outputs, block, scratch=()):
+def channel_blocks(kernel, index, inputs, outputs, block, scratch=()):
     def spec(shape):
         lead = tuple(0 for _ in shape[:-1])
-        return pl.BlockSpec(tuple(shape[:-1]) + (block,), lambda j: lead + (j,))
-
-    return pl.pallas_call(
-        kernel,
+        return pl.BlockSpec(tuple(shape[:-1]) + (block,), lambda j, idx: lead + (j,))
+
+    grid_spec = pltpu.PrefetchScalarGridSpec(
+        num_scalar_prefetch=1,
         grid=(outputs[0].shape[-1] // block,),
         in_specs=[spec(a.shape) for a in inputs],
         out_specs=[spec(o.shape) for o in outputs],
-        out_shape=outputs,
         scratch_shapes=list(scratch),
-    )(*inputs)
+    )
+    return pl.pallas_call(kernel, grid_spec=grid_spec, out_shape=outputs)(index, *inputs)
 
 
 def attention_kernel(scale, history, q_ref, k_ref, v_ref, qpos_ref, out_ref):
@@ -218,22 +224,22 @@
     )
     cache_k, cache_v = cache_kv[:, :row_count], cache_kv[:, row_count:]
 
-    before = shifted(streams[row_count - (tap_count - 1) :], "context", 1)
-    before = jnp.where(device_index == 0, stream_tail, before)
+    received = shifted(streams[row_count - (tap_count - 1) :], "context", 1)
     channels = streams.shape[2]
     mode_count = decay_rates.shape[0]
     ways = lax.axis_size("tensor")
-    mode_gain = jnp.sqrt(1.0 - jnp.exp(-2.0 * decay_rates))
+    index = device_index.astype(jnp.int32).reshape(1)
     block = 256
     product, filtered1, local_out, finals_out = channel_blocks(
         front_kernel,
+        index,
         [
             streams.transpose(1, 0, 2),
-            before.transpose(1, 0, 2),
+            received.transpose(1, 0, 2),
+            stream_tail.transpose(1, 0, 2),
             short_taps,
             decay_rates,
-            residues * mode_gain,
-            mode_gain,
+            residues,
         ],
         [
             jax.ShapeDtypeStruct((row_count, channels), jnp.bfloat16),
@@ -245,21 +251,15 @@
         [pltpu.VMEM((mode_count, block), jnp.float32)],
     )
     finals = lax.all_to_all(finals_out, "context", 0, 0, tiled=True)
-    source = jnp.arange(devices, dtype=jnp.int32)
-    earlier = source < device_index
-    steps = jnp.where(earlier, (device_index - 1 - source) * row_count, 0).astype(jnp.float32)
-    ones_row = jnp.ones((1, channels), jnp.float32)
     (hidden_out,) = channel_blocks(
         back_kernel,
+        index,
         [
             local_out,
             decay_rates,
             residues,
             finals,
             hyena_state,
-            steps[:, None] * ones_row,
-            earlier.astype(jnp.float32)[:, None] * ones_row,
-            (device_index * row_count).astype(jnp.float32) * ones_row,
             filtered1,
             product,
             residual,

time: 123 us -> 121 us (0.984)
  blocking collectives: 10.5 us -> 27 us
  waiting for transfers between devices: 38.7 us -> 30 us
  starting transfers between devices: 25.6 us -> 19.4 us
  other arithmetic: 6.56 us -> 4.36 us
  local copies, waits for them, and re-layouts: 6.8 us -> 5.35 us
    all_to_all x0 -> x1, blocking collectives: none -> 16.5 us  [shards(): finals = lax.all_to_all(finals_out, 'context', 0, 0, tiled=True)]
    all_to_all x1 -> x0, waiting for transfers between devices: 9.47 us -> none  [shards(): finals = lax.all_to_all(finals_out, 'context', 0, 0, tiled=True)]
    all_to_all x1 -> x0, starting transfers between devices: 6.2 us -> none  [shards(): finals = lax.all_to_all(finals_out, 'context', 0, 0, tiled=True)]
    mul x3 -> x0, local copies, waits for them, and re-layouts: 2.07 us -> none  [the longest x1 0.78 us: shards(): steps[:, None] * ones_row]
    sqrt x1 -> x0, other arithmetic: 1.55 us -> none  [shards(): mode_gain = jnp.sqrt(1.0 - jnp.exp(-2.0 * decay_rates))]
  transfers between devices with their start and end apart: 5 -> 4, of which waited for: 4 -> 4; matrix products, arithmetic and copies ran while one was open for 7% -> 6% of each run, Pallas kernels for 9% -> 9%
where the time goes in v8:
time: 121 us; the launch traced here: 120 us
  Pallas kernels  33.4 us (28%)
  waiting for transfers between devices  30 us (25%)
  blocking collectives  27 us (22%)
  starting transfers between devices  19.4 us (16%)
  local copies, waits for them, and re-layouts  5.35 us (4%)
  other arithmetic  4.36 us (4%)
    all_to_all x1, waiting for transfers between devices, shards(): lax.all_to_all(jnp.concatenate([query_parts, by_head(new_keys), by_head(n...  17.1 us
    all_to_all x1, blocking collectives, shards(): finals = lax.all_to_all(finals_out, 'context', 0, 0, tiled=True)  16.5 us
    pallas_call x2, Pallas kernels, channel_blocks(): pl.pallas_call(kernel, grid_spec=grid_spec, out_shape=outputs)  11.7 us
    pallas_call x1, Pallas kernels, attend(): pl.pallas_call(functools.partial(attention_kernel, 1.0 / math.sqrt(width)...  11.1 us
    all_to_all x1, waiting for transfers between devices, shards(): gathered = lax.all_to_all(hidden_out, 'tensor', 0, 0, tiled=True)  11 us
    pallas_call x1, Pallas kernels, project(): pl.pallas_call(project_kernel, grid=(groups, width // block), in_specs=[p...  10.6 us
    all_to_all x1, blocking collectives, shards(): back = lax.all_to_all(mine, 'context', 0, 0, tiled=True)  10.5 us
    all_to_all x1, starting transfers between devices, shards(): lax.all_to_all(jnp.concatenate([by_head(cache_keys), by_head(cache_values...  6.07 us
  transfers between devices with their start and end apart: 4, of which 4 were waited for; matrix products, arithmetic and copies ran while one was open for 6% of the time, Pallas kernels for 9%

profile of v8, /device:TPU:1, one launch (start us, length us, event | category | flops | bytes accessed | tf_op | source)
XLA Modules:
  0.0 120.5 jit_solution(18429365055217084015)
XLA Ops:
  0.0 0.8 slice.40
  0.8 4.6 %collective-permute-start = (bf16[2,3,1024]{2,0,1:T(2,128)(2,1)S(1)}, bf16[2,3,1024]{2,0,1:T(2,128)(2,1)S(1)}, u32[]{:S(2)}, u32[]{:S(2)}) collective-permute-start(bf16[2,3,1024]{2,0,1:T(2,128)(2,1)S(1)} %slice.40), channel_id=1, source_target_pairs={{0,4},{4,8},{8,12},{12,16},{16,20},{20,24},{24,28},{28,32},{32,36}... | collective-permute-start | bytes 36872 | tf_op jit(solution)/shard_map/ppermute | solution.py:21
  5.4 0.8 collective-permute-done
  6.2 0.6 copy-done.4
  6.8 7.0 %shard_map.127 = (bf16[128,1024]{1,0:T(8,128)(2,1)}, f32[128,1024]{1,0:T(8,128)}, f32[128,1024]{1,0:T(8,128)}, bf16[16,16,1024]{2,1,0:T(8,128)(2,1)}) custom-call(s32[1]{0:T(128)} %bitcast.idx_ref, bf16[3,128,1024]{2,1,0:T(8,128)(2,1)} %bitcast.81, bf16[3,2,1024]{2,1,0:T(2,128)(2,1)} %bitcast.85, bf16[3,2,1024]{2,1,0:T(2,128)(2,1)} %bitcast.84, ...), custom_call_target="tpu_custom_call" | custom-call | tf_op jit(solution)/shard_map/pallas_call | solution.py:122
  13.8 16.5 %all_to_all.25.fin_ref = bf16[16,16,1024]{2,1,0:T(8,128)(2,1)} all-to-all(bf16[16,16,1024]{2,1,0:T(8,128)(2,1)} %get-tuple-element.10), channel_id=1, replica_groups=mesh['dp'=2,'context'=16,'tensor'=4] {'context'}, dimensions={0} | all-to-all | bytes 1048576 | tf_op jit(solution)/shard_map/all_to_all | solution.py:253
  30.3 4.7 %shard_map.128 = bf16[4,128,1024]{2,1,0:T(8,128)(2,1)} custom-call(s32[1]{0:T(128)} %bitcast.idx_ref, f32[128,1024]{1,0:T(8,128)} %get-tuple-element.9.local_ref, f32[16,1024]{1,0:T(8,128)} %rate_ref.3, f32[16,1024]{1,0:T(8,128)} %res_ref.3, bf16[16,16,1024]{2,1,0:T(8,128)(2,1)} %all_to_all.25.fin_ref, f32[16,1024]{1,0:T(8,128)} %hs_ref.1, ...), custom_call_target="tpu_custom_call" | custom-call | tf_op jit(solution)/shard_map/pallas_call | solution.py:122
  35.1 4.1 %all-to-all-start.1 = ((bf16[4,128,1024]{2,1,0:T(8,128)(2,1)}), bf16[4,128,1024]{2,1,0:T(8,128)(2,1)S(1)}, u32[]{:S(2)}, u32[]{:S(2)}) async-start(bf16[4,128,1024]{2,1,0:T(8,128)(2,1)} %shard_map.128), calls=%async_computation.1 | async-start | bytes 2097152 | tf_op jit(solution)/shard_map/all_to_all | solution.py:271
  40.3 1.1 pad_maximum_fusion.1
  41.4 0.3 multiply_cosine_fusion
  41.7 11.0 %all-to-all-done.1 = bf16[4,128,1024]{2,1,0:T(8,128)(2,1)S(1)} async-done(((bf16[4,128,1024]{2,1,0:T(8,128)(2,1)}), bf16[4,128,1024]{2,1,0:T(8,128)(2,1)S(1)}, u32[]{:S(2)}, u32[]{:S(2)}) %all-to-all-start.1) | async-done | bytes 1048608 | tf_op jit(solution)/shard_map/all_to_all | solution.py:271
  52.7 6.1 %all-to-all-start.3 = ((bf16[16,256,128]{2,1,0:T(8,128)(2,1)}), bf16[16,256,128]{2,1,0:T(8,128)(2,1)S(1)}, u32[]{:S(2)}, u32[]{:S(2)}) async-start(bf16[16,256,128]{2,1,0:T(8,128)(2,1)} %pad_maximum_fusion.1), calls=%async_computation.3 | async-start | bytes 2097152 | tf_op jit(solution)/shard_map/all_to_all | solution.py:221
  60.0 10.6 %shard_map.129 = f32[3,128,1024]{2,1,0:T(8,128)S(1)} custom-call(bf16[128,4096]{1,0:T(8,128)(2,1)S(1)} %multiply_convert_fusion.x_ref, bf16[3,4096,1024]{2,1,0:T(8,128)(2,1)} %bitcast.62), custom_call_target="tpu_custom_call" | custom-call | flops 3221225472 | bytes 27787264 | tf_op jit(solution)/shard_map/pallas_call | solution.py:176
  70.6 0.3 copy.32
  71.1 0.5 subtract_convert_fusion.1
  72.3 1.2 pad_maximum_fusion
  73.4 1.1 all-to-all-done.3
  74.6 4.6 %all-to-all-start.2 = ((bf16[16,320,128]{2,1,0:T(8,128)(2,1)}), bf16[16,320,128]{2,1,0:T(8,128)(2,1)S(1)}, u32[]{:S(2)}, u32[]{:S(2)}) async-start(bf16[16,320,128]{2,1,0:T(8,128)(2,1)} %pad_maximum_fusion), calls=%async_computation.2 | async-start | bytes 2621440 | tf_op jit(solution)/shard_map/all_to_all | solution.py:294
  79.2 0.5 add.90.qpos_ref
  79.7 0.9 fusion.3
  80.6 17.1 %all-to-all-done.2 = bf16[16,320,128]{2,1,0:T(8,128)(2,1)S(1)} async-done(((bf16[16,320,128]{2,1,0:T(8,128)(2,1)}), bf16[16,320,128]{2,1,0:T(8,128)(2,1)S(1)}, u32[]{:S(2)}, u32[]{:S(2)}) %all-to-all-start.2) | async-done | bytes 1310752 | tf_op jit(solution)/shard_map/all_to_all | solution.py:294
  98.0 11.1 %shard_map.130 = bf16[1024,128]{1,0:T(8,128)(2,1)S(1)} custom-call(bf16[1024,128]{1,0:T(8,128)(2,1)S(1)} %bitcast.60, bf16[4096,128]{1,0:T(8,128)(2,1)S(1)} %get-tuple-element.27.k_ref, bf16[4096,128]{1,0:T(8,128)(2,1)S(1)} %get-tuple-element.28.v_ref, s32[1024,1]{1,0:T(8,128)S(1)} %add.90.qpos_ref), custom_call_target="tpu_custom_call" | custom-call | tf_op jit(solution)/shard_map/pallas_call | solution.py:154
  109.1 10.5 %all_to_all.26 = bf16[16,64,128]{2,1,0:T(8,128)(2,1)S(1)} all-to-all(bf16[16,64,128]{2,1,0:T(8,128)(2,1)S(1)} %bitcast.61), channel_id=1, replica_groups=mesh['dp'=2,'context'=16,'tensor'=4] {'context'}, dimensions={0} | all-to-all | bytes 524288 | tf_op jit(solution)/shard_map/all_to_all | solution.py:310
  119.7 0.8 copy.37
  (38 shorter events, 2.8 us)
Async XLA Ops:
  0.8 5.4 %collective-permute-start = (bf16[2,3,1024]{2,0,1:T(2,128)(2,1)S(1)}, bf16[2,3,1024]{2,0,1:T(2,128)(2,1)S(1)}, u32[]{:S(2)}, u32[]{:S(2)}) collective-permute-start(bf16[2,3,1024]{2,0,1:T(2,128)(2,1)S(1)} %slice.40), channel_id=1, source_target_pairs={{0,4},{4,8},{8,12},{12,16},{16,20},{20,24},{24,28},{28,32},{32,36}... | collective-permute-start | bytes 36872 | tf_op jit(solution)/shard_map/ppermute | solution.py:21
  6.2 0.6 copy-start.4
  30.3 9.5 %copy-start.1 = (bf16[128,1024]{1,0:T(8,128)(2,1)S(1)}, bf16[128,1024]{1,0:T(8,128)(2,1)}, u32[]{:S(2)}) copy-start(bf16[128,1024]{1,0:T(8,128)(2,1)} %param.25) | copy-start | bytes 786436
  35.1 4.9 %copy-start.2 = (bf16[128,1024]{1,0:T(8,128)(2,1)S(1)}, bf16[128,1024]{1,0:T(8,128)(2,1)}, u32[]{:S(2)}) copy-start(bf16[128,1024]{1,0:T(8,128)(2,1)} %param.24) | copy-start | bytes 786436
  35.1 17.6 %all-to-all-start.1 = ((bf16[4,128,1024]{2,1,0:T(8,128)(2,1)}), bf16[4,128,1024]{2,1,0:T(8,128)(2,1)S(1)}, u32[]{:S(2)}, u32[]{:S(2)}) async-start(bf16[4,128,1024]{2,1,0:T(8,128)(2,1)} %shard_map.128), calls=%async_computation.1 | async-start | bytes 2097152 | tf_op jit(solution)/shard_map/all_to_all | solution.py:271
  52.7 21.9 %all-to-all-start.3 = ((bf16[16,256,128]{2,1,0:T(8,128)(2,1)}), bf16[16,256,128]{2,1,0:T(8,128)(2,1)S(1)}, u32[]{:S(2)}, u32[]{:S(2)}) async-start(bf16[16,256,128]{2,1,0:T(8,128)(2,1)} %pad_maximum_fusion.1), calls=%async_computation.3 | async-start | bytes 2097152 | tf_op jit(solution)/shard_map/all_to_all | solution.py:221
  59.0 0.7 copy-start.3
  74.6 23.2 %all-to-all-start.2 = ((bf16[16,320,128]{2,1,0:T(8,128)(2,1)}), bf16[16,320,128]{2,1,0:T(8,128)(2,1)S(1)}, u32[]{:S(2)}, u32[]{:S(2)}) async-start(bf16[16,320,128]{2,1,0:T(8,128)(2,1)} %pad_maximum_fusion), calls=%async_computation.2 | async-start | bytes 2621440 | tf_op jit(solution)/shard_map/all_to_all | solution.py:294
  80.6 17.2 %copy-start = (bf16[16,128,128]{2,1,0:T(8,128)(2,1)S(1)}, bf16[16,128,128]{2,1,0:T(8,128)(2,1)}, u32[]{:S(2)}) copy-start(bf16[16,128,128]{2,1,0:T(8,128)(2,1)} %get-tuple-element.18) | copy-start | bytes 1572868

commit v9 on v8

--- a/solution.py
+++ b/solution.py
@@ -166,21 +166,33 @@
     )(queries, keys, values, query_pos.reshape(rows, 1))
 
 
-def project_kernel(x_ref, w_ref, out_ref):
+def local_project_kernel(idx_ref, x_ref, w_ref, out_ref):
     out_ref[...] = jnp.dot(x_ref[...], w_ref[...], preferred_element_type=jnp.float32)
 
 
-def project(x, w, block=512):
+def rest_project_kernel(idx_ref, x_ref, w_ref, part_ref, out_ref):
+    @pl.when(pl.program_id(2) == 0)
+    def _():
+        out_ref[...] = part_ref[...]
+
+    out_ref[...] += jnp.dot(x_ref[...], w_ref[...], preferred_element_type=jnp.float32)
+
+
+def project_own(index, x, w, block=512):
     rows, depth = x.shape
     groups, _, width = w.shape
-    return pl.pallas_call(
-        project_kernel,
+    grid_spec = pltpu.PrefetchScalarGridSpec(
+        num_scalar_prefetch=1,
         grid=(groups, width // block),
         in_specs=[
-            pl.BlockSpec((rows, depth), lambda g, j: (0, 0)),
-            pl.BlockSpec((None, depth, block), lambda g, j: (g, 0, j)),
-        ],
-        out_specs=pl.BlockSpec((None, rows, block), lambda g, j: (g, 0, j)),
+            pl.BlockSpec((rows, depth), lambda g, j, idx: (0, 0)),
+            pl.BlockSpec((None, depth, block), lambda g, j, idx: (g, idx[0], j)),
+        ],
+        out_specs=pl.BlockSpec((None, rows, block), lambda g, j, idx: (g, 0, j)),
+    )
+    return pl.pallas_call(
+        local_project_kernel,
+        grid_spec=grid_spec,
         out_shape=jax.ShapeDtypeStruct((groups, rows, width), jnp.float32),
         compiler_params=pltpu.CompilerParams(vmem_limit_bytes=48 * 1024 * 1024),
         cost_estimate=pl.CostEstimate(
@@ -188,7 +200,38 @@
             bytes_accessed=2 * (rows * depth + groups * depth * width) + 4 * groups * rows * width,
             transcendentals=0,
         ),
-    )(x, w)
+    )(index, x, w)
+
+
+def project_rest(index, xs, w, part, block=512):
+    ways, rows, depth = xs.shape
+    groups, _, width = w.shape
+
+    def other(k, idx):
+        return (idx[0] + 1 + k) % ways
+
+    grid_spec = pltpu.PrefetchScalarGridSpec(
+        num_scalar_prefetch=1,
+        grid=(groups, width // block, ways - 1),
+        in_specs=[
+            pl.BlockSpec((None, rows, depth), lambda g, j, k, idx: (other(k, idx), 0, 0)),
+            pl.BlockSpec((None, depth, block), lambda g, j, k, idx: (g, other(k, idx), j)),
+            pl.BlockSpec((None, rows, block), lambda g, j, k, idx: (g, 0, j)),
+        ],
+        out_specs=pl.BlockSpec((None, rows, block), lambda g, j, k, idx: (g, 0, j)),
+    )
+    return pl.pallas_call(
+        rest_project_kernel,
+        grid_spec=grid_spec,
+        out_shape=jax.ShapeDtypeStruct((groups, rows, width), jnp.float32),
+        compiler_params=pltpu.CompilerParams(vmem_limit_bytes=48 * 1024 * 1024),
+        cost_estimate=pl.CostEstimate(
+            flops=2 * rows * depth * width * groups * (ways - 1),
+            bytes_accessed=2 * (ways - 1) * (rows * depth + groups * depth * width)
+            + 8 * groups * rows * width,
+            transcendentals=0,
+        ),
+    )(index, xs, w, part)
 
 
 def shards(
@@ -268,15 +311,20 @@
         [jax.ShapeDtypeStruct((ways, row_count, channels), jnp.bfloat16)],
         block,
     )
+    tensor_index = lax.axis_index("tensor").astype(jnp.int32).reshape(1)
+    gains = norm_gain.reshape(ways, 1, channels)
+    weights3 = qkv_weight.transpose(1, 0, 2)
+    own_gain = lax.dynamic_index_in_dim(gains, tensor_index[0], 0, keepdims=False)
+    own = (hidden_out[0].astype(jnp.float32) * own_gain).astype(jnp.bfloat16)
+    part = project_own(tensor_index, own, weights3)
     gathered = lax.all_to_all(hidden_out, "tensor", 0, 0, tiled=True)
-    gathered = gathered.transpose(1, 0, 2).reshape(row_count, ways * channels)
     hidden_float = gathered.astype(jnp.float32)
-    mean_square = jnp.mean(hidden_float * hidden_float, axis=1, keepdims=True)
-    normed = (hidden_float * lax.rsqrt(mean_square + NORM_EPSILON) * norm_gain[None, :]).astype(
-        jnp.bfloat16
-    )
+    mean_square = jnp.sum(hidden_float * hidden_float, axis=(0, 2)) / (ways * channels)
+    scaled = (hidden_float * gains).astype(jnp.bfloat16)
+    total = project_rest(tensor_index, scaled, weights3, part)
+    row_scale = lax.rsqrt(mean_square + NORM_EPSILON)
     projected = (
-        project(normed, qkv_weight.transpose(1, 0, 2))
+        (total * row_scale[None, :, None])
         .transpose(1, 0, 2)
         .reshape(row_count, 3, heads_here, HEAD)
     )

time: 121 us -> 127 us (1.050)
  blocking collectives: 27 us -> 10.5 us
  Pallas kernels: 33.4 us -> 43.3 us
  starting transfers between devices: 19.4 us -> 28 us
  waiting for transfers between devices: 30 us -> 31.7 us
    all_to_all x1 -> x0, blocking collectives: 16.5 us -> none  [shards(): finals = lax.all_to_all(finals_out, 'context', 0, 0, tiled=True)]
    pallas_call x1 -> x2, Pallas kernels: 10.6 us -> 20.5 us  [the longest x1 15.3 us: project_rest(): pl.pallas_call(rest_project_kernel, grid_spec=grid_spec, out_shape=jax.Sh...]
    all_to_all x0 -> x1, waiting for transfers between devices: none -> 8.58 us  [shards(): finals = lax.all_to_all(finals_out, 'context', 0, 0, tiled=True)]
    all_to_all x0 -> x1, starting transfers between devices: none -> 6.94 us  [shards(): finals = lax.all_to_all(finals_out, 'context', 0, 0, tiled=True)]
    all_to_all x1, waiting for transfers between devices: 11 us -> 5.62 us  [shards(): gathered = lax.all_to_all(hidden_out, 'tensor', 0, 0, tiled=True)]
  transfers between devices with their start and end apart: 4 -> 5, of which waited for: 4 -> 4; matrix products, arithmetic and copies ran while one was open for 6% -> 6% of each run, Pallas kernels for 9% -> 16%
where the time goes in v9:
time: 127 us; the launch traced here: 126 us
  Pallas kernels  43.3 us (34%)
  waiting for transfers between devices  31.7 us (25%)
  starting transfers between devices  28 us (22%)
  blocking collectives  10.5 us (8%)
  local copies, waits for them, and re-layouts  6.19 us (5%)
  other arithmetic  5.22 us (4%)
    all_to_all x1, waiting for transfers between devices, shards(): lax.all_to_all(jnp.concatenate([query_parts, by_head(new_keys), by_head(n...  16.7 us
    pallas_call x1, Pallas kernels, project_rest(): pl.pallas_call(rest_project_kernel, grid_spec=grid_spec, out_shape=jax.Sh...  15.3 us
    pallas_call x2, Pallas kernels, channel_blocks(): pl.pallas_call(kernel, grid_spec=grid_spec, out_shape=outputs)  11.7 us
    pallas_call x1, Pallas kernels, attend(): pl.pallas_call(functools.partial(attention_kernel, 1.0 / math.sqrt(width)...  11.1 us
    all_to_all x1, blocking collectives, shards(): back = lax.all_to_all(mine, 'context', 0, 0, tiled=True)  10.5 us
    all_to_all x1, waiting for transfers between devices, shards(): finals = lax.all_to_all(finals_out, 'context', 0, 0, tiled=True)  8.58 us
    all_to_all x1, starting transfers between devices, shards(): finals = lax.all_to_all(finals_out, 'context', 0, 0, tiled=True)  6.94 us
    all_to_all x1, starting transfers between devices, shards(): lax.all_to_all(jnp.concatenate([by_head(cache_keys), by_head(cache_values...  6.64 us
  transfers between devices with their start and end apart: 5, of which 4 were waited for; matrix products, arithmetic and copies ran while one was open for 6% of the time, Pallas kernels for 16%

profile of v9, /device:TPU:1, one launch (start us, length us, event | category | flops | bytes accessed | tf_op | source)
XLA Modules:
  0.0 125.8 jit_solution(10152189596377329214)
XLA Ops:
  0.0 0.9 slice.43
  0.9 4.6 %collective-permute-start = (bf16[2,3,1024]{2,0,1:T(2,128)(2,1)S(1)}, bf16[2,3,1024]{2,0,1:T(2,128)(2,1)S(1)}, u32[]{:S(2)}, u32[]{:S(2)}) collective-permute-start(bf16[2,3,1024]{2,0,1:T(2,128)(2,1)S(1)} %slice.43), channel_id=1, source_target_pairs={{0,4},{4,8},{8,12},{12,16},{16,20},{20,24},{24,28},{28,32},{32,36}... | collective-permute-start | bytes 36872 | tf_op jit(solution)/shard_map/ppermute | solution.py:21
  5.5 0.8 collective-permute-done
  6.3 0.6 copy-done.4
  6.9 7.0 %shard_map.127 = (bf16[128,1024]{1,0:T(8,128)(2,1)}, f32[128,1024]{1,0:T(8,128)}, f32[128,1024]{1,0:T(8,128)}, bf16[16,16,1024]{2,1,0:T(8,128)(2,1)}) custom-call(s32[1]{0:T(128)} %bitcast.1.idx_ref, bf16[3,128,1024]{2,1,0:T(8,128)(2,1)} %bitcast.85, bf16[3,2,1024]{2,1,0:T(2,128)(2,1)} %bitcast.91, bf16[3,2,1024]{2,1,0:T(2,128)(2,1)} %bitcast.90, ...), custom_call_target="tpu_custom_call" | custom-call | tf_op jit(solution)/shard_map/pallas_call | solution.py:122
  13.9 6.9 %all-to-all-start = ((bf16[16,16,1024]{2,1,0:T(8,128)(2,1)}), bf16[16,16,1024]{2,1,0:T(8,128)(2,1)S(1)}, u32[]{:S(2)}, u32[]{:S(2)}) async-start(bf16[16,16,1024]{2,1,0:T(8,128)(2,1)} %get-tuple-element.10), calls=%async_computation | async-start | bytes 1048576 | tf_op jit(solution)/shard_map/all_to_all | solution.py:296
  21.7 8.6 %all-to-all-done.fin_ref = bf16[16,16,1024]{2,1,0:T(8,128)(2,1)S(1)} async-done(((bf16[16,16,1024]{2,1,0:T(8,128)(2,1)}), bf16[16,16,1024]{2,1,0:T(8,128)(2,1)S(1)}, u32[]{:S(2)}, u32[]{:S(2)}) %all-to-all-start) | async-done | bytes 524320 | tf_op jit(solution)/shard_map/all_to_all | solution.py:296
  30.3 0.8 copy-done
  31.1 4.7 %shard_map.128 = bf16[4,128,1024]{2,1,0:T(8,128)(2,1)} custom-call(s32[1]{0:T(128)} %bitcast.1.idx_ref, f32[128,1024]{1,0:T(8,128)} %get-tuple-element.9.local_ref, f32[16,1024]{1,0:T(8,128)} %rate_ref.3, f32[16,1024]{1,0:T(8,128)} %res_ref.3, bf16[16,16,1024]{2,1,0:T(8,128)(2,1)} %copy-done, f32[16,1024]{1,0:T(8,128)} %hs_ref.1, ...), custom_call_target="tpu_custom_call" | custom-call | tf_op jit(solution)/shard_map/pallas_call | solution.py:122
  35.8 4.0 %all-to-all-start.1 = ((bf16[4,128,1024]{2,1,0:T(8,128)(2,1)}), bf16[4,128,1024]{2,1,0:T(8,128)(2,1)S(1)}, u32[]{:S(2)}, u32[]{:S(2)}) async-start(bf16[4,128,1024]{2,1,0:T(8,128)(2,1)} %shard_map.128), calls=%async_computation.1 | async-start | bytes 2097152 | tf_op jit(solution)/shard_map/all_to_all | solution.py:320
  40.0 1.1 pad_maximum_fusion.1
  41.4 1.0 fusion.2.x_ref
  42.4 5.2 %shard_map.129.part_ref = f32[3,128,1024]{2,1,0:T(8,128)S(1)} custom-call(s32[1]{0:T(128)} %bitcast.idx_ref, bf16[128,1024]{1,0:T(8,128)(2,1)S(1)} %fusion.2.x_ref, bf16[3,4096,1024]{2,1,0:T(8,128)(2,1)} %bitcast.65), custom_call_target="tpu_custom_call" | custom-call | flops 805306368 | bytes 8126464 | tf_op jit(solution)/shard_map/pallas_call | solution.py:193
  47.7 5.6 %all-to-all-done.1 = bf16[4,128,1024]{2,1,0:T(8,128)(2,1)S(1)} async-done(((bf16[4,128,1024]{2,1,0:T(8,128)(2,1)}), bf16[4,128,1024]{2,1,0:T(8,128)(2,1)S(1)}, u32[]{:S(2)}, u32[]{:S(2)}) %all-to-all-start.1) | async-done | bytes 1048608 | tf_op jit(solution)/shard_map/all_to_all | solution.py:320
  53.3 6.6 %all-to-all-start.3 = ((bf16[16,256,128]{2,1,0:T(8,128)(2,1)}), bf16[16,256,128]{2,1,0:T(8,128)(2,1)}, u32[]{:S(2)}, u32[]{:S(2)}) async-start(bf16[16,256,128]{2,1,0:T(8,128)(2,1)} %pad_maximum_fusion.1), calls=%async_computation.3 | async-start | bytes 2097152 | tf_op jit(solution)/shard_map/all_to_all | solution.py:264
  60.4 15.3 %shard_map.130 = f32[3,128,1024]{2,1,0:T(8,128)S(1)} custom-call(s32[1]{0:T(128)} %bitcast.idx_ref, bf16[4,128,1024]{2,1,0:T(8,128)(2,1)S(1)} %get-tuple-element.20.x_ref, bf16[3,4096,1024]{2,1,0:T(8,128)(2,1)} %bitcast.66, f32[3,128,1024]{2,1,0:T(8,128)S(1)} %shard_map.129.part_ref), custom_call_target="tpu_custom_call" | custom-call | flops 2415919104 | bytes 22806528 | tf_op jit(solution)/shard_map/pallas_call | solution.py:223
  77.5 1.2 pad_maximum_fusion
  78.7 5.8 %all-to-all-start.2 = ((bf16[16,320,128]{2,1,0:T(8,128)(2,1)}), bf16[16,320,128]{2,1,0:T(8,128)(2,1)S(1)}, u32[]{:S(2)}, u32[]{:S(2)}) async-start(bf16[16,320,128]{2,1,0:T(8,128)(2,1)} %pad_maximum_fusion), calls=%async_computation.2 | async-start | bytes 2621440 | tf_op jit(solution)/shard_map/all_to_all | solution.py:342
  84.6 0.5 add.94.qpos_ref
  85.0 1.3 %fusion.5 = (bf16[16,128,128]{2,1,0:T(8,128)(2,1)S(1)}, bf16[16,128,128]{2,1,0:T(8,128)(2,1)S(1)}) fusion(bf16[16,256,128]{2,1,0:T(8,128)(2,1)} %all-to-all-done.3), kind=kLoop, calls=%fused_computation.32 | loop fusion | bytes 2097152 | tf_op jit(solution)/shard_map/slice | solution.py:268
  86.3 16.7 %all-to-all-done.2 = bf16[16,320,128]{2,1,0:T(8,128)(2,1)S(1)} async-done(((bf16[16,320,128]{2,1,0:T(8,128)(2,1)}), bf16[16,320,128]{2,1,0:T(8,128)(2,1)S(1)}, u32[]{:S(2)}, u32[]{:S(2)}) %all-to-all-start.2) | async-done | bytes 1310752 | tf_op jit(solution)/shard_map/all_to_all | solution.py:342
  103.3 11.1 %shard_map.131 = bf16[1024,128]{1,0:T(8,128)(2,1)S(1)} custom-call(bf16[1024,128]{1,0:T(8,128)(2,1)S(1)} %bitcast.63, bf16[4096,128]{1,0:T(8,128)(2,1)S(1)} %get-tuple-element.29.k_ref, bf16[4096,128]{1,0:T(8,128)(2,1)S(1)} %get-tuple-element.30.v_ref, s32[1024,1]{1,0:T(8,128)S(1)} %add.94.qpos_ref), custom_call_target="tpu_custom_call" | custom-call | tf_op jit(solution)/shard_map/pallas_call | solution.py:154
  114.4 10.5 %all_to_all.25 = bf16[16,64,128]{2,1,0:T(8,128)(2,1)S(1)} all-to-all(bf16[16,64,128]{2,1,0:T(8,128)(2,1)S(1)} %bitcast.64), channel_id=1, replica_groups=mesh['dp'=2,'context'=16,'tensor'=4] {'context'}, dimensions={0} | all-to-all | bytes 524288 | tf_op jit(solution)/shard_map/all_to_all | solution.py:358
  125.0 0.8 copy.34
  (41 shorter events, 3.4 us)
Async XLA Ops:
  0.0 20.8 %copy-start.3 = (f32[4096]{0:T(1024)S(1)}, f32[4096]{0:T(1024)}, u32[]{:S(2)}) copy-start(f32[4096]{0:T(1024)} %param.21) | copy-start | bytes 49156
  0.0 21.5 %copy-start.1 = (bf16[128,1024]{1,0:T(8,128)(2,1)S(1)}, bf16[128,1024]{1,0:T(8,128)(2,1)}, u32[]{:S(2)}) copy-start(bf16[128,1024]{1,0:T(8,128)(2,1)} %param.25) | copy-start | bytes 786436
  0.0 21.6 %copy-start.2 = (bf16[128,1024]{1,0:T(8,128)(2,1)S(1)}, bf16[128,1024]{1,0:T(8,128)(2,1)}, u32[]{:S(2)}) copy-start(bf16[128,1024]{1,0:T(8,128)(2,1)} %param.24) | copy-start | bytes 786436
  0.9 5.4 %collective-permute-start = (bf16[2,3,1024]{2,0,1:T(2,128)(2,1)S(1)}, bf16[2,3,1024]{2,0,1:T(2,128)(2,1)S(1)}, u32[]{:S(2)}, u32[]{:S(2)}) collective-permute-start(bf16[2,3,1024]{2,0,1:T(2,128)(2,1)S(1)} %slice.43), channel_id=1, source_target_pairs={{0,4},{4,8},{8,12},{12,16},{16,20},{20,24},{24,28},{28,32},{32,36}... | collective-permute-start | bytes 36872 | tf_op jit(solution)/shard_map/ppermute | solution.py:21
  6.3 0.6 copy-start.4
  13.9 16.4 %all-to-all-start = ((bf16[16,16,1024]{2,1,0:T(8,128)(2,1)}), bf16[16,16,1024]{2,1,0:T(8,128)(2,1)S(1)}, u32[]{:S(2)}, u32[]{:S(2)}) async-start(bf16[16,16,1024]{2,1,0:T(8,128)(2,1)} %get-tuple-element.10), calls=%async_computation | async-start | bytes 1048576 | tf_op jit(solution)/shard_map/all_to_all | solution.py:296
  30.3 0.8 copy-start
  35.8 17.5 %all-to-all-start.1 = ((bf16[4,128,1024]{2,1,0:T(8,128)(2,1)}), bf16[4,128,1024]{2,1,0:T(8,128)(2,1)S(1)}, u32[]{:S(2)}, u32[]{:S(2)}) async-start(bf16[4,128,1024]{2,1,0:T(8,128)(2,1)} %shard_map.128), calls=%async_computation.1 | async-start | bytes 2097152 | tf_op jit(solution)/shard_map/all_to_all | solution.py:320
  53.3 25.4 %all-to-all-start.3 = ((bf16[16,256,128]{2,1,0:T(8,128)(2,1)}), bf16[16,256,128]{2,1,0:T(8,128)(2,1)}, u32[]{:S(2)}, u32[]{:S(2)}) async-start(bf16[16,256,128]{2,1,0:T(8,128)(2,1)} %pad_maximum_fusion.1), calls=%async_computation.3 | async-start | bytes 2097152 | tf_op jit(solution)/shard_map/all_to_all | solution.py:264
  78.7 24.4 %all-to-all-start.2 = ((bf16[16,320,128]{2,1,0:T(8,128)(2,1)}), bf16[16,320,128]{2,1,0:T(8,128)(2,1)S(1)}, u32[]{:S(2)}, u32[]{:S(2)}) async-start(bf16[16,320,128]{2,1,0:T(8,128)(2,1)} %pad_maximum_fusion), calls=%async_computation.2 | async-start | bytes 2621440 | tf_op jit(solution)/shard_map/all_to_all | solution.py:342

commit v10 on v8

--- a/solution.py
+++ b/solution.py
@@ -148,7 +148,7 @@
     out_ref[...] = (numerator / weight_sum[:, :1]).astype(out_ref.dtype)
 
 
-def attend(queries, keys, values, query_pos, history, block=256):
+def attend(queries, keys, values, query_pos, history, block=512):
     rows, width = queries.shape
     key_rows = keys.shape[0]
     return pl.pallas_call(
@@ -170,7 +170,7 @@
     out_ref[...] = jnp.dot(x_ref[...], w_ref[...], preferred_element_type=jnp.float32)
 
 
-def project(x, w, block=512):
+def project(x, w, block=1024):
     rows, depth = x.shape
     groups, _, width = w.shape
     return pl.pallas_call(

time: 121 us -> 120 us (level)
  Pallas kernels: 33.4 us -> 31.8 us
  transfers between devices with their start and end apart: 4 -> 4, of which waited for: 4 -> 4; matrix products, arithmetic and copies ran while one was open for 6% -> 6% of each run, Pallas kernels for 9% -> 8%
where the time goes in v10:
time: 120 us
  Pallas kernels  31.8 us (26%)
  waiting for transfers between devices  31 us (26%)
  blocking collectives  27 us (22%)
  starting transfers between devices  19.1 us (16%)
  local copies, waits for them, and re-layouts  5.35 us (4%)
  other arithmetic  4.36 us (4%)
    all_to_all x1, waiting for transfers between devices, shards(): lax.all_to_all(jnp.concatenate([query_parts, by_head(new_keys), by_head(n...  17.2 us
    all_to_all x1, blocking collectives, shards(): finals = lax.all_to_all(finals_out, 'context', 0, 0, tiled=True)  16.5 us
    pallas_call x2, Pallas kernels, channel_blocks(): pl.pallas_call(kernel, grid_spec=grid_spec, out_shape=outputs)  11.7 us
    all_to_all x1, waiting for transfers between devices, shards(): gathered = lax.all_to_all(hidden_out, 'tensor', 0, 0, tiled=True)  11 us
    all_to_all x1, blocking collectives, shards(): back = lax.all_to_all(mine, 'context', 0, 0, tiled=True)  10.5 us
    pallas_call x1, Pallas kernels, attend(): pl.pallas_call(functools.partial(attention_kernel, 1.0 / math.sqrt(width)...  10.4 us
    pallas_call x1, Pallas kernels, project(): pl.pallas_call(project_kernel, grid=(groups, width // block), in_specs=[p...  9.69 us
    all_to_all x1, starting transfers between devices, shards(): lax.all_to_all(jnp.concatenate([by_head(cache_keys), by_head(cache_values...  6.07 us
  transfers between devices with their start and end apart: 4, of which 4 were waited for; matrix products, arithmetic and copies ran while one was open for 6% of the time, Pallas kernels for 8%

profile of v10, /device:TPU:1, one launch (start us, length us, event | category | flops | bytes accessed | tf_op | source)
XLA Modules:
  0.0 119.6 jit_solution(10399833645353746113)
XLA Ops:
  0.0 0.8 slice.40
  0.8 4.6 %collective-permute-start = (bf16[2,3,1024]{2,0,1:T(2,128)(2,1)S(1)}, bf16[2,3,1024]{2,0,1:T(2,128)(2,1)S(1)}, u32[]{:S(2)}, u32[]{:S(2)}) collective-permute-start(bf16[2,3,1024]{2,0,1:T(2,128)(2,1)S(1)} %slice.40), channel_id=1, source_target_pairs={{0,4},{4,8},{8,12},{12,16},{16,20},{20,24},{24,28},{28,32},{32,36}... | collective-permute-start | bytes 36872 | tf_op jit(solution)/shard_map/ppermute | solution.py:21
  5.4 0.8 collective-permute-done
  6.2 0.6 copy-done.4
  6.8 7.0 %shard_map.127 = (bf16[128,1024]{1,0:T(8,128)(2,1)}, f32[128,1024]{1,0:T(8,128)}, f32[128,1024]{1,0:T(8,128)}, bf16[16,16,1024]{2,1,0:T(8,128)(2,1)}) custom-call(s32[1]{0:T(128)} %bitcast.idx_ref, bf16[3,128,1024]{2,1,0:T(8,128)(2,1)} %bitcast.81, bf16[3,2,1024]{2,1,0:T(2,128)(2,1)} %bitcast.85, bf16[3,2,1024]{2,1,0:T(2,128)(2,1)} %bitcast.84, ...), custom_call_target="tpu_custom_call" | custom-call | tf_op jit(solution)/shard_map/pallas_call | solution.py:122
  13.8 16.5 %all_to_all.25.fin_ref = bf16[16,16,1024]{2,1,0:T(8,128)(2,1)} all-to-all(bf16[16,16,1024]{2,1,0:T(8,128)(2,1)} %get-tuple-element.10), channel_id=1, replica_groups=mesh['dp'=2,'context'=16,'tensor'=4] {'context'}, dimensions={0} | all-to-all | bytes 1048576 | tf_op jit(solution)/shard_map/all_to_all | solution.py:253
  30.3 4.7 %shard_map.128 = bf16[4,128,1024]{2,1,0:T(8,128)(2,1)} custom-call(s32[1]{0:T(128)} %bitcast.idx_ref, f32[128,1024]{1,0:T(8,128)} %get-tuple-element.9.local_ref, f32[16,1024]{1,0:T(8,128)} %rate_ref.3, f32[16,1024]{1,0:T(8,128)} %res_ref.3, bf16[16,16,1024]{2,1,0:T(8,128)(2,1)} %all_to_all.25.fin_ref, f32[16,1024]{1,0:T(8,128)} %hs_ref.1, ...), custom_call_target="tpu_custom_call" | custom-call | tf_op jit(solution)/shard_map/pallas_call | solution.py:122
  35.1 4.1 %all-to-all-start.1 = ((bf16[4,128,1024]{2,1,0:T(8,128)(2,1)}), bf16[4,128,1024]{2,1,0:T(8,128)(2,1)S(1)}, u32[]{:S(2)}, u32[]{:S(2)}) async-start(bf16[4,128,1024]{2,1,0:T(8,128)(2,1)} %shard_map.128), calls=%async_computation.1 | async-start | bytes 2097152 | tf_op jit(solution)/shard_map/all_to_all | solution.py:271
  40.3 1.1 pad_maximum_fusion.1
  41.4 0.3 multiply_cosine_fusion
  41.7 11.0 %all-to-all-done.1 = bf16[4,128,1024]{2,1,0:T(8,128)(2,1)S(1)} async-done(((bf16[4,128,1024]{2,1,0:T(8,128)(2,1)}), bf16[4,128,1024]{2,1,0:T(8,128)(2,1)S(1)}, u32[]{:S(2)}, u32[]{:S(2)}) %all-to-all-start.1) | async-done | bytes 1048608 | tf_op jit(solution)/shard_map/all_to_all | solution.py:271
  52.7 6.1 %all-to-all-start.3 = ((bf16[16,256,128]{2,1,0:T(8,128)(2,1)}), bf16[16,256,128]{2,1,0:T(8,128)(2,1)S(1)}, u32[]{:S(2)}, u32[]{:S(2)}) async-start(bf16[16,256,128]{2,1,0:T(8,128)(2,1)} %pad_maximum_fusion.1), calls=%async_computation.3 | async-start | bytes 2097152 | tf_op jit(solution)/shard_map/all_to_all | solution.py:221
  60.0 9.7 %shard_map.129 = f32[3,128,1024]{2,1,0:T(8,128)S(1)} custom-call(bf16[128,4096]{1,0:T(8,128)(2,1)S(1)} %multiply_convert_fusion.x_ref, bf16[3,4096,1024]{2,1,0:T(8,128)(2,1)} %bitcast.62), custom_call_target="tpu_custom_call" | custom-call | flops 3221225472 | bytes 27787264 | tf_op jit(solution)/shard_map/pallas_call | solution.py:176
  69.7 0.3 copy.32
  70.2 0.5 subtract_convert_fusion.1
  71.4 1.2 pad_maximum_fusion
  72.5 2.0 %all-to-all-done.3 = bf16[16,256,128]{2,1,0:T(8,128)(2,1)S(1)} async-done(((bf16[16,256,128]{2,1,0:T(8,128)(2,1)}), bf16[16,256,128]{2,1,0:T(8,128)(2,1)S(1)}, u32[]{:S(2)}, u32[]{:S(2)}) %all-to-all-start.3) | async-done | bytes 1048608 | tf_op jit(solution)/shard_map/all_to_all | solution.py:221
  74.6 4.3 %all-to-all-start.2 = ((bf16[16,320,128]{2,1,0:T(8,128)(2,1)}), bf16[16,320,128]{2,1,0:T(8,128)(2,1)S(1)}, u32[]{:S(2)}, u32[]{:S(2)}) async-start(bf16[16,320,128]{2,1,0:T(8,128)(2,1)} %pad_maximum_fusion), calls=%async_computation.2 | async-start | bytes 2621440 | tf_op jit(solution)/shard_map/all_to_all | solution.py:294
  78.9 0.5 add.90.qpos_ref
  79.4 0.9 fusion.3
  80.3 17.2 %all-to-all-done.2 = bf16[16,320,128]{2,1,0:T(8,128)(2,1)S(1)} async-done(((bf16[16,320,128]{2,1,0:T(8,128)(2,1)}), bf16[16,320,128]{2,1,0:T(8,128)(2,1)S(1)}, u32[]{:S(2)}, u32[]{:S(2)}) %all-to-all-start.2) | async-done | bytes 1310752 | tf_op jit(solution)/shard_map/all_to_all | solution.py:294
  97.8 10.4 %shard_map.130 = bf16[1024,128]{1,0:T(8,128)(2,1)S(1)} custom-call(bf16[1024,128]{1,0:T(8,128)(2,1)S(1)} %bitcast.60, bf16[4096,128]{1,0:T(8,128)(2,1)S(1)} %get-tuple-element.27.k_ref, bf16[4096,128]{1,0:T(8,128)(2,1)S(1)} %get-tuple-element.28.v_ref, s32[1024,1]{1,0:T(8,128)S(1)} %add.90.qpos_ref), custom_call_target="tpu_custom_call" | custom-call | tf_op jit(solution)/shard_map/pallas_call | solution.py:154
  108.2 10.5 %all_to_all.26 = bf16[16,64,128]{2,1,0:T(8,128)(2,1)S(1)} all-to-all(bf16[16,64,128]{2,1,0:T(8,128)(2,1)S(1)} %bitcast.61), channel_id=1, replica_groups=mesh['dp'=2,'context'=16,'tensor'=4] {'context'}, dimensions={0} | all-to-all | bytes 524288 | tf_op jit(solution)/shard_map/all_to_all | solution.py:310
  118.8 0.8 copy.37
  (38 shorter events, 2.9 us)
Async XLA Ops:
  0.8 5.4 %collective-permute-start = (bf16[2,3,1024]{2,0,1:T(2,128)(2,1)S(1)}, bf16[2,3,1024]{2,0,1:T(2,128)(2,1)S(1)}, u32[]{:S(2)}, u32[]{:S(2)}) collective-permute-start(bf16[2,3,1024]{2,0,1:T(2,128)(2,1)S(1)} %slice.40), channel_id=1, source_target_pairs={{0,4},{4,8},{8,12},{12,16},{16,20},{20,24},{24,28},{28,32},{32,36}... | collective-permute-start | bytes 36872 | tf_op jit(solution)/shard_map/ppermute | solution.py:21
  6.2 0.6 copy-start.4
  30.3 9.5 %copy-start.1 = (bf16[128,1024]{1,0:T(8,128)(2,1)S(1)}, bf16[128,1024]{1,0:T(8,128)(2,1)}, u32[]{:S(2)}) copy-start(bf16[128,1024]{1,0:T(8,128)(2,1)} %param.25) | copy-start | bytes 786436
  35.1 4.9 %copy-start.2 = (bf16[128,1024]{1,0:T(8,128)(2,1)S(1)}, bf16[128,1024]{1,0:T(8,128)(2,1)}, u32[]{:S(2)}) copy-start(bf16[128,1024]{1,0:T(8,128)(2,1)} %param.24) | copy-start | bytes 786436
  35.1 17.6 %all-to-all-start.1 = ((bf16[4,128,1024]{2,1,0:T(8,128)(2,1)}), bf16[4,128,1024]{2,1,0:T(8,128)(2,1)S(1)}, u32[]{:S(2)}, u32[]{:S(2)}) async-start(bf16[4,128,1024]{2,1,0:T(8,128)(2,1)} %shard_map.128), calls=%async_computation.1 | async-start | bytes 2097152 | tf_op jit(solution)/shard_map/all_to_all | solution.py:271
  52.7 21.9 %all-to-all-start.3 = ((bf16[16,256,128]{2,1,0:T(8,128)(2,1)}), bf16[16,256,128]{2,1,0:T(8,128)(2,1)S(1)}, u32[]{:S(2)}, u32[]{:S(2)}) async-start(bf16[16,256,128]{2,1,0:T(8,128)(2,1)} %pad_maximum_fusion.1), calls=%async_computation.3 | async-start | bytes 2097152 | tf_op jit(solution)/shard_map/all_to_all | solution.py:221
  59.0 0.7 copy-start.3
  74.6 22.9 %all-to-all-start.2 = ((bf16[16,320,128]{2,1,0:T(8,128)(2,1)}), bf16[16,320,128]{2,1,0:T(8,128)(2,1)S(1)}, u32[]{:S(2)}, u32[]{:S(2)}) async-start(bf16[16,320,128]{2,1,0:T(8,128)(2,1)} %pad_maximum_fusion), calls=%async_computation.2 | async-start | bytes 2621440 | tf_op jit(solution)/shard_map/all_to_all | solution.py:294
  80.3 17.3 %copy-start = (bf16[16,128,128]{2,1,0:T(8,128)(2,1)S(1)}, bf16[16,128,128]{2,1,0:T(8,128)(2,1)}, u32[]{:S(2)}) copy-start(bf16[16,128,128]{2,1,0:T(8,128)(2,1)} %get-tuple-element.18) | copy-start | bytes 1572868

commit v11 on v10

--- a/solution.py
+++ b/solution.py
@@ -122,63 +122,103 @@
     return pl.pallas_call(kernel, grid_spec=grid_spec, out_shape=outputs)(index, *inputs)
 
 
-def attention_kernel(scale, history, q_ref, k_ref, v_ref, qpos_ref, out_ref):
-    q = q_ref[...]
-    contract = (((1,), (1,)), ((), ()))
-    old_scores = (
-        lax.dot_general(q, k_ref[:history], contract, preferred_element_type=jnp.float32) * scale
-    )
-    new_scores = (
-        lax.dot_general(q, k_ref[history:], contract, preferred_element_type=jnp.float32) * scale
-    )
-    new_pos = lax.broadcasted_iota(jnp.int32, (1, new_scores.shape[1]), 1)
-    new_scores = jnp.where(new_pos <= qpos_ref[...], new_scores, -jnp.inf)
-    row_max = jnp.maximum(
-        jnp.max(old_scores, axis=1, keepdims=True), jnp.max(new_scores, axis=1, keepdims=True)
-    )
-    old_w = jnp.exp(old_scores - row_max).astype(jnp.bfloat16)
-    new_w = jnp.exp(new_scores - row_max).astype(jnp.bfloat16)
-    ones = jnp.ones((history, 128), jnp.bfloat16)
-    weight_sum = jnp.dot(old_w, ones, preferred_element_type=jnp.float32) + jnp.dot(
-        new_w, ones[: new_w.shape[1]], preferred_element_type=jnp.float32
-    )
-    numerator = jnp.dot(old_w, v_ref[:history], preferred_element_type=jnp.float32) + jnp.dot(
-        new_w, v_ref[history:], preferred_element_type=jnp.float32
-    )
-    out_ref[...] = (numerator / weight_sum[:, :1]).astype(out_ref.dtype)
-
-
-def attend(queries, keys, values, query_pos, history, block=512):
+def cache_attention_kernel(scale, q_ref, k_ref, v_ref, max_ref, sum_ref, num_ref):
+    scores = (
+        lax.dot_general(
+            q_ref[...], k_ref[...], (((1,), (1,)), ((), ())), preferred_element_type=jnp.float32
+        )
+        * scale
+    )
+    row_max = jnp.max(scores, axis=1, keepdims=True)
+    weights = jnp.exp(scores - row_max).astype(jnp.bfloat16)
+    ones = jnp.ones((weights.shape[1], 128), jnp.bfloat16)
+    max_ref[...] = jnp.broadcast_to(row_max, max_ref.shape)
+    sum_ref[...] = jnp.dot(weights, ones, preferred_element_type=jnp.float32)
+    num_ref[...] = jnp.dot(weights, v_ref[...], preferred_element_type=jnp.float32)
+
+
+def new_attention_kernel(scale, q_ref, k_ref, v_ref, qpos_ref, max_ref, sum_ref, num_ref, out_ref):
+    scores = (
+        lax.dot_general(
+            q_ref[...], k_ref[...], (((1,), (1,)), ((), ())), preferred_element_type=jnp.float32
+        )
+        * scale
+    )
+    key_pos = lax.broadcasted_iota(jnp.int32, (1, scores.shape[1]), 1)
+    scores = jnp.where(key_pos <= qpos_ref[...], scores, -jnp.inf)
+    old_max = max_ref[:, :1]
+    row_max = jnp.maximum(old_max, jnp.max(scores, axis=1, keepdims=True))
+    rescale = jnp.exp(old_max - row_max)
+    weights = jnp.exp(scores - row_max).astype(jnp.bfloat16)
+    ones = jnp.ones((weights.shape[1], 128), jnp.bfloat16)
+    weight_sum = sum_ref[:, :1] * rescale + jnp.dot(
+        weights, ones, preferred_element_type=jnp.float32
+    )[:, :1]
+    numerator = num_ref[...] * rescale + jnp.dot(
+        weights, v_ref[...], preferred_element_type=jnp.float32
+    )
+    out_ref[...] = (numerator / weight_sum).astype(out_ref.dtype)
+
+
+def attend_cache(queries, keys, values, block=512):
     rows, width = queries.shape
     key_rows = keys.shape[0]
+    piece = jax.ShapeDtypeStruct((rows, width), jnp.float32)
+    row_spec = pl.BlockSpec((block, width), lambda i: (i, 0))
     return pl.pallas_call(
-        functools.partial(attention_kernel, 1.0 / math.sqrt(width), history),
+        functools.partial(cache_attention_kernel, 1.0 / math.sqrt(width)),
         grid=(rows // block,),
         in_specs=[
-            pl.BlockSpec((block, width), lambda i: (i, 0)),
+            row_spec,
+            pl.BlockSpec((key_rows, width), lambda i: (0, 0)),
+            pl.BlockSpec((key_rows, width), lambda i: (0, 0)),
+        ],
+        out_specs=[row_spec, row_spec, row_spec],
+        out_shape=[piece, piece, piece],
+        compiler_params=pltpu.CompilerParams(vmem_limit_bytes=48 * 1024 * 1024),
+        cost_estimate=pl.CostEstimate(
+            flops=6 * rows * key_rows * width,
+            bytes_accessed=2 * rows * width + 4 * key_rows * width + 12 * rows * width,
+            transcendentals=rows * key_rows,
+        ),
+    )(queries, keys, values)
+
+
+def attend_new(queries, keys, values, query_pos, pieces, block=512):
+    rows, width = queries.shape
+    key_rows = keys.shape[0]
+    row_spec = pl.BlockSpec((block, width), lambda i: (i, 0))
+    return pl.pallas_call(
+        functools.partial(new_attention_kernel, 1.0 / math.sqrt(width)),
+        grid=(rows // block,),
+        in_specs=[
+            row_spec,
             pl.BlockSpec((key_rows, width), lambda i: (0, 0)),
             pl.BlockSpec((key_rows, width), lambda i: (0, 0)),
             pl.BlockSpec((block, 1), lambda i: (i, 0)),
-        ],
-        out_specs=pl.BlockSpec((block, width), lambda i: (i, 0)),
+            row_spec,
+            row_spec,
+            row_spec,
+        ],
+        out_specs=row_spec,
         out_shape=jax.ShapeDtypeStruct((rows, width), jnp.bfloat16),
         compiler_params=pltpu.CompilerParams(vmem_limit_bytes=48 * 1024 * 1024),
-    )(queries, keys, values, query_pos.reshape(rows, 1))
+    )(queries, keys, values, query_pos.reshape(rows, 1), *pieces)
 
 
 def project_kernel(x_ref, w_ref, out_ref):
     out_ref[...] = jnp.dot(x_ref[...], w_ref[...], preferred_element_type=jnp.float32)
 
 
-def project(x, w, block=1024):
+def project(x, w, first, groups, block=1024):
     rows, depth = x.shape
-    groups, _, width = w.shape
+    width = w.shape[2]
     return pl.pallas_call(
         project_kernel,
         grid=(groups, width // block),
         in_specs=[
             pl.BlockSpec((rows, depth), lambda g, j: (0, 0)),
-            pl.BlockSpec((None, depth, block), lambda g, j: (g, 0, j)),
+            pl.BlockSpec((None, depth, block), lambda g, j: (g + first, 0, j)),
         ],
         out_specs=pl.BlockSpec((None, rows, block), lambda g, j: (g, 0, j)),
         out_shape=jax.ShapeDtypeStruct((groups, rows, width), jnp.float32),
@@ -275,38 +315,36 @@
     normed = (hidden_float * lax.rsqrt(mean_square + NORM_EPSILON) * norm_gain[None, :]).astype(
         jnp.bfloat16
     )
-    projected = (
-        project(normed, qkv_weight.transpose(1, 0, 2))
-        .transpose(1, 0, 2)
-        .reshape(row_count, 3, heads_here, HEAD)
-    )
+    weights3 = qkv_weight.transpose(1, 0, 2)
     query_index = device_index * row_count + jnp.arange(row_count, dtype=jnp.int32)
     positions = (start_offset[0] + query_index).astype(jnp.float32)
-    queries = rotate(projected[:, 0], positions).astype(jnp.bfloat16)
-    new_keys = rotate(projected[:, 1], positions).astype(jnp.bfloat16)
-    new_values = projected[:, 2].astype(jnp.bfloat16)
-
+    query_proj = project(normed, weights3, 0, 1)[0].reshape(row_count, heads_here, HEAD)
+    queries = rotate(query_proj, positions).astype(jnp.bfloat16)
     query_parts = (
         queries.reshape(2, half_rows, heads_here, HEAD)
         .transpose(2, 0, 1, 3)
         .reshape(devices, half_rows, HEAD)
     )
-    sent = lax.all_to_all(
-        jnp.concatenate([query_parts, by_head(new_keys), by_head(new_values)], axis=1),
+    my_queries = lax.all_to_all(query_parts, "context", 0, 0, tiled=True)
+    kv_proj = project(normed, weights3, 1, 2).reshape(2, row_count, heads_here, HEAD)
+    new_keys = rotate(kv_proj[0], positions).astype(jnp.bfloat16)
+    new_values = kv_proj[1].astype(jnp.bfloat16)
+    new_kv = lax.all_to_all(
+        jnp.concatenate([by_head(new_keys), by_head(new_values)], axis=1),
         "context", 0, 0, tiled=True,
     )
-    my_queries = sent[:, :half_rows]
-    new_k = sent[:, half_rows : half_rows + row_count]
-    new_v = sent[:, half_rows + row_count :]
-
-    hist_rows = cache_k.shape[0] * cache_k.shape[1]
-    all_k = jnp.concatenate([cache_k.reshape(-1, HEAD), new_k.reshape(-1, HEAD)], axis=0)
-    all_v = jnp.concatenate([cache_v.reshape(-1, HEAD), new_v.reshape(-1, HEAD)], axis=0)
     q_flat = my_queries.reshape(-1, HEAD)
+    pieces = attend_cache(q_flat, cache_k.reshape(-1, HEAD), cache_v.reshape(-1, HEAD))
     src = jnp.arange(devices, dtype=jnp.int32)[:, None]
     row = jnp.arange(half_rows, dtype=jnp.int32)[None, :]
     query_pos = (src * row_count + (device_index % 2) * half_rows + row).reshape(-1)
-    mine = attend(q_flat, all_k, all_v, query_pos, hist_rows).reshape(devices, half_rows, HEAD)
+    mine = attend_new(
+        q_flat,
+        new_kv[:, :row_count].reshape(-1, HEAD),
+        new_kv[:, row_count:].reshape(-1, HEAD),
+        query_pos,
+        pieces,
+    ).reshape(devices, half_rows, HEAD)
     back = lax.all_to_all(mine, "context", 0, 0, tiled=True)
     attended = (
         back.reshape(heads_here, 2, half_rows, HEAD)

time: 120 us -> 124 us (1.033)
  starting transfers between devices: 19.1 us -> 23.6 us
    all_to_all x1 -> x2, starting transfers between devices: 4.26 us -> 8.79 us  [the longest x1 4.61 us: shards(): my_queries = lax.all_to_all(query_parts, 'context', 0, 0, tiled=True)]
    pallas_call x1 -> x2, Pallas kernels: 9.69 us -> 11.7 us  [project(): pl.pallas_call(project_kernel, grid=(groups, width // block), in_specs=[p...]
    pallas_call x1 -> x2, Pallas kernels: 10.4 us -> 9.01 us  [the longest x1 5.01 us: attend_new(): pl.pallas_call(functools.partial(new_attention_kernel, 1.0 / math.sqrt(wi...]
    all_to_all x1 -> x2, waiting for transfers between devices: 17.2 us -> 16.9 us  [the longest x1 11.2 us: shards(): lax.all_to_all(jnp.concatenate([by_head(new_keys), by_head(new_values)],...]
  transfers between devices with their start and end apart: 4 -> 5, of which waited for: 4 -> 5; matrix products, arithmetic and copies ran while one was open for 6% -> 5% of each run, Pallas kernels for 8% -> 13%
where the time goes in v11:
time: 124 us; the launch traced here: 123 us
  Pallas kernels  32.4 us (26%)
  waiting for transfers between devices  29.8 us (24%)
  blocking collectives  27 us (22%)
  starting transfers between devices  23.6 us (19%)
  other arithmetic  4.79 us (4%)
  local copies, waits for them, and re-layouts  4.37 us (4%)
    all_to_all x1, blocking collectives, shards(): finals = lax.all_to_all(finals_out, 'context', 0, 0, tiled=True)  16.5 us
    pallas_call x2, Pallas kernels, channel_blocks(): pl.pallas_call(kernel, grid_spec=grid_spec, out_shape=outputs)  11.7 us
    pallas_call x2, Pallas kernels, project(): pl.pallas_call(project_kernel, grid=(groups, width // block), in_specs=[p...  11.7 us
    all_to_all x1, waiting for transfers between devices, shards(): lax.all_to_all(jnp.concatenate([by_head(new_keys), by_head(new_values)],...  11.2 us
    all_to_all x1, waiting for transfers between devices, shards(): gathered = lax.all_to_all(hidden_out, 'tensor', 0, 0, tiled=True)  11 us
    all_to_all x1, blocking collectives, shards(): back = lax.all_to_all(mine, 'context', 0, 0, tiled=True)  10.4 us
    all_to_all x1, starting transfers between devices, shards(): lax.all_to_all(jnp.concatenate([by_head(cache_keys), by_head(cache_values...  6.07 us
    all_to_all x1, waiting for transfers between devices, shards(): my_queries = lax.all_to_all(query_parts, 'context', 0, 0, tiled=True)  5.63 us
  transfers between devices with their start and end apart: 5, of which 5 were waited for; matrix products, arithmetic and copies ran while one was open for 5% of the time, Pallas kernels for 13%

profile of v11, /device:TPU:1, one launch (start us, length us, event | category | flops | bytes accessed | tf_op | source)
XLA Modules:
  0.0 122.9 jit_solution(12070224824846626387)
XLA Ops:
  0.0 0.8 slice.36
  0.8 4.6 %collective-permute-start = (bf16[2,3,1024]{2,0,1:T(2,128)(2,1)S(1)}, bf16[2,3,1024]{2,0,1:T(2,128)(2,1)S(1)}, u32[]{:S(2)}, u32[]{:S(2)}) collective-permute-start(bf16[2,3,1024]{2,0,1:T(2,128)(2,1)S(1)} %slice.36), channel_id=1, source_target_pairs={{0,4},{4,8},{8,12},{12,16},{16,20},{20,24},{24,28},{28,32},{32,36}... | collective-permute-start | bytes 36872 | tf_op jit(solution)/shard_map/ppermute | solution.py:21
  5.4 0.8 collective-permute-done
  6.2 0.6 copy-done.3
  6.8 7.0 %shard_map.127 = (bf16[128,1024]{1,0:T(8,128)(2,1)}, f32[128,1024]{1,0:T(8,128)}, f32[128,1024]{1,0:T(8,128)}, bf16[16,16,1024]{2,1,0:T(8,128)(2,1)}) custom-call(s32[1]{0:T(128)} %bitcast.idx_ref, bf16[3,128,1024]{2,1,0:T(8,128)(2,1)} %bitcast.81, bf16[3,2,1024]{2,1,0:T(2,128)(2,1)} %bitcast.85, bf16[3,2,1024]{2,1,0:T(2,128)(2,1)} %bitcast.84, ...), custom_call_target="tpu_custom_call" | custom-call | tf_op jit(solution)/shard_map/pallas_call | solution.py:122
  13.8 16.5 %all_to_all.30.fin_ref = bf16[16,16,1024]{2,1,0:T(8,128)(2,1)} all-to-all(bf16[16,16,1024]{2,1,0:T(8,128)(2,1)} %get-tuple-element.13), channel_id=1, replica_groups=mesh['dp'=2,'context'=16,'tensor'=4] {'context'}, dimensions={0} | all-to-all | bytes 1048576 | tf_op jit(solution)/shard_map/all_to_all | solution.py:293
  30.3 4.7 %shard_map.128 = bf16[4,128,1024]{2,1,0:T(8,128)(2,1)} custom-call(s32[1]{0:T(128)} %bitcast.idx_ref, f32[128,1024]{1,0:T(8,128)} %get-tuple-element.12.local_ref, f32[16,1024]{1,0:T(8,128)} %rate_ref.3, f32[16,1024]{1,0:T(8,128)} %res_ref.3, bf16[16,16,1024]{2,1,0:T(8,128)(2,1)} %all_to_all.30.fin_ref, f32[16,1024]{1,0:T(8,128)} %hs_ref.1, ...), custom_call_target="tpu_custom_call" | custom-call | tf_op jit(solution)/shard_map/pallas_call | solution.py:122
  35.1 4.1 %all-to-all-start.1 = ((bf16[4,128,1024]{2,1,0:T(8,128)(2,1)}), bf16[4,128,1024]{2,1,0:T(8,128)(2,1)S(1)}, u32[]{:S(2)}, u32[]{:S(2)}) async-start(bf16[4,128,1024]{2,1,0:T(8,128)(2,1)} %shard_map.128), calls=%async_computation.1 | async-start | bytes 2097152 | tf_op jit(solution)/shard_map/all_to_all | solution.py:311
  40.3 1.1 pad_maximum_fusion.1
  41.7 11.0 %all-to-all-done.1 = bf16[4,128,1024]{2,1,0:T(8,128)(2,1)S(1)} async-done(((bf16[4,128,1024]{2,1,0:T(8,128)(2,1)}), bf16[4,128,1024]{2,1,0:T(8,128)(2,1)S(1)}, u32[]{:S(2)}, u32[]{:S(2)}) %all-to-all-start.1) | async-done | bytes 1048608 | tf_op jit(solution)/shard_map/all_to_all | solution.py:311
  52.7 6.1 %all-to-all-start.4 = ((bf16[16,256,128]{2,1,0:T(8,128)(2,1)}), bf16[16,256,128]{2,1,0:T(8,128)(2,1)S(1)}, u32[]{:S(2)}, u32[]{:S(2)}) async-start(bf16[16,256,128]{2,1,0:T(8,128)(2,1)} %pad_maximum_fusion.1), calls=%async_computation.4 | async-start | bytes 2097152 | tf_op jit(solution)/shard_map/all_to_all | solution.py:261
  60.0 7.1 %shard_map.130 = f32[2,128,1024]{2,1,0:T(8,128)S(1)} custom-call(bf16[128,4096]{1,0:T(8,128)(2,1)S(1)} %multiply_convert_fusion.x_ref, bf16[3,4096,1024]{2,1,0:T(8,128)(2,1)} %bitcast.65), custom_call_target="tpu_custom_call" | custom-call | flops 2147483648 | bytes 18874368 | tf_op jit(solution)/shard_map/pallas_call | solution.py:216
  67.2 4.6 %shard_map.129 = f32[1,128,1024]{2,1,0:T(8,128)S(1)} custom-call(bf16[128,4096]{1,0:T(8,128)(2,1)S(1)} %multiply_convert_fusion.x_ref, bf16[3,4096,1024]{2,1,0:T(8,128)(2,1)} %bitcast.66), custom_call_target="tpu_custom_call" | custom-call | flops 1073741824 | bytes 9961472 | tf_op jit(solution)/shard_map/pallas_call | solution.py:216
  72.5 0.9 pad_maximum_fusion.2
  73.4 1.2 all-to-all-done.4
  74.6 4.6 %all-to-all-start.2 = ((bf16[16,64,128]{2,1,0:T(8,128)(2,1)}), bf16[16,64,128]{2,1,0:T(8,128)(2,1)S(1)}, u32[]{:S(2)}, u32[]{:S(2)}) async-start(bf16[16,64,128]{2,1,0:T(8,128)(2,1)} %bitcast.11), calls=%async_computation.2 | async-start | bytes 524288 | tf_op jit(solution)/shard_map/all_to_all | solution.py:328
  79.7 1.1 pad_maximum_fusion
  80.7 5.6 %all-to-all-done.2 = bf16[16,64,128]{2,1,0:T(8,128)(2,1)S(1)} async-done(((bf16[16,64,128]{2,1,0:T(8,128)(2,1)}), bf16[16,64,128]{2,1,0:T(8,128)(2,1)S(1)}, u32[]{:S(2)}, u32[]{:S(2)}) %all-to-all-start.2) | async-done | bytes 262176 | tf_op jit(solution)/shard_map/all_to_all | solution.py:328
  86.4 4.2 %all-to-all-start.3 = ((bf16[16,256,128]{2,1,0:T(8,128)(2,1)}), bf16[16,256,128]{2,1,0:T(8,128)(2,1)S(1)}, u32[]{:S(2)}, u32[]{:S(2)}) async-start(bf16[16,256,128]{2,1,0:T(8,128)(2,1)} %pad_maximum_fusion), calls=%async_computation.3 | async-start | bytes 2097152 | tf_op jit(solution)/shard_map/all_to_all | solution.py:332
  91.2 4.0 %shard_map.131 = (f32[1024,128]{1,0:T(8,128)S(1)}, f32[1024,128]{1,0:T(8,128)S(1)}, f32[1024,128]{1,0:T(8,128)S(1)}) custom-call(bf16[1024,128]{1,0:T(8,128)(2,1)S(1)} %bitcast.60, bf16[2048,128]{1,0:T(8,128)(2,1)S(1)} %bitcast.64, bf16[2048,128]{1,0:T(8,128)(2,1)S(1)} %bitcast.63), custom_call_target="tpu_custom_call" | custom-call | flops 1610612736 | bytes 2883584 | tf_op jit(solution)/shard_map/pallas_call | solution.py:168
  95.2 11.2 %all-to-all-done.3 = bf16[16,256,128]{2,1,0:T(8,128)(2,1)S(1)} async-done(((bf16[16,256,128]{2,1,0:T(8,128)(2,1)}), bf16[16,256,128]{2,1,0:T(8,128)(2,1)S(1)}, u32[]{:S(2)}, u32[]{:S(2)}) %all-to-all-start.3) | async-done | bytes 1048608 | tf_op jit(solution)/shard_map/all_to_all | solution.py:332
  106.5 5.0 %shard_map.132 = bf16[1024,128]{1,0:T(8,128)(2,1)S(1)} custom-call(bf16[1024,128]{1,0:T(8,128)(2,1)S(1)} %bitcast.61, bf16[2048,128]{1,0:T(8,128)(2,1)S(1)} %bitcast.59, bf16[2048,128]{1,0:T(8,128)(2,1)S(1)} %bitcast.58, s32[1024,1]{1,0:T(8,128)S(1)} %add.90.qpos_ref, f32[1024,128]{1,0:T(8,128)S(1)} %get-tuple-element.16.max_ref, ...), custom_call_target="tpu_custom_call" | custom-call | tf_op jit(solution)/shard_map/pallas_call | solution.py:191
  111.5 10.4 %all_to_all.31 = bf16[16,64,128]{2,1,0:T(8,128)(2,1)S(1)} all-to-all(bf16[16,64,128]{2,1,0:T(8,128)(2,1)S(1)} %bitcast.62), channel_id=1, replica_groups=mesh['dp'=2,'context'=16,'tensor'=4] {'context'}, dimensions={0} | all-to-all | bytes 524288 | tf_op jit(solution)/shard_map/all_to_all | solution.py:348
  122.1 0.8 copy.39
  (40 shorter events, 4.0 us)
Async XLA Ops:
  0.8 5.4 %collective-permute-start = (bf16[2,3,1024]{2,0,1:T(2,128)(2,1)S(1)}, bf16[2,3,1024]{2,0,1:T(2,128)(2,1)S(1)}, u32[]{:S(2)}, u32[]{:S(2)}) collective-permute-start(bf16[2,3,1024]{2,0,1:T(2,128)(2,1)S(1)} %slice.36), channel_id=1, source_target_pairs={{0,4},{4,8},{8,12},{12,16},{16,20},{20,24},{24,28},{28,32},{32,36}... | collective-permute-start | bytes 36872 | tf_op jit(solution)/shard_map/ppermute | solution.py:21
  6.2 0.6 copy-start.3
  30.3 9.5 %copy-start = (bf16[128,1024]{1,0:T(8,128)(2,1)S(1)}, bf16[128,1024]{1,0:T(8,128)(2,1)}, u32[]{:S(2)}) copy-start(bf16[128,1024]{1,0:T(8,128)(2,1)} %param.24) | copy-start | bytes 786436
  35.1 4.9 %copy-start.1 = (bf16[128,1024]{1,0:T(8,128)(2,1)S(1)}, bf16[128,1024]{1,0:T(8,128)(2,1)}, u32[]{:S(2)}) copy-start(bf16[128,1024]{1,0:T(8,128)(2,1)} %param.25) | copy-start | bytes 786436
  35.1 17.6 %all-to-all-start.1 = ((bf16[4,128,1024]{2,1,0:T(8,128)(2,1)}), bf16[4,128,1024]{2,1,0:T(8,128)(2,1)S(1)}, u32[]{:S(2)}, u32[]{:S(2)}) async-start(bf16[4,128,1024]{2,1,0:T(8,128)(2,1)} %shard_map.128), calls=%async_computation.1 | async-start | bytes 2097152 | tf_op jit(solution)/shard_map/all_to_all | solution.py:311
  52.7 21.9 %all-to-all-start.4 = ((bf16[16,256,128]{2,1,0:T(8,128)(2,1)}), bf16[16,256,128]{2,1,0:T(8,128)(2,1)S(1)}, u32[]{:S(2)}, u32[]{:S(2)}) async-start(bf16[16,256,128]{2,1,0:T(8,128)(2,1)} %pad_maximum_fusion.1), calls=%async_computation.4 | async-start | bytes 2097152 | tf_op jit(solution)/shard_map/all_to_all | solution.py:261
  59.0 0.7 copy-start.2
  74.6 11.8 %all-to-all-start.2 = ((bf16[16,64,128]{2,1,0:T(8,128)(2,1)}), bf16[16,64,128]{2,1,0:T(8,128)(2,1)S(1)}, u32[]{:S(2)}, u32[]{:S(2)}) async-start(bf16[16,64,128]{2,1,0:T(8,128)(2,1)} %bitcast.11), calls=%async_computation.2 | async-start | bytes 524288 | tf_op jit(solution)/shard_map/all_to_all | solution.py:328
  86.4 20.0 %all-to-all-start.3 = ((bf16[16,256,128]{2,1,0:T(8,128)(2,1)}), bf16[16,256,128]{2,1,0:T(8,128)(2,1)S(1)}, u32[]{:S(2)}, u32[]{:S(2)}) async-start(bf16[16,256,128]{2,1,0:T(8,128)(2,1)} %pad_maximum_fusion), calls=%async_computation.3 | async-start | bytes 2097152 | tf_op jit(solution)/shard_map/all_to_all | solution.py:332

commit v12 on v11

--- a/solution.py
+++ b/solution.py
@@ -210,16 +210,21 @@
     out_ref[...] = jnp.dot(x_ref[...], w_ref[...], preferred_element_type=jnp.float32)
 
 
-def project(x, w, first, groups, block=1024):
+def project_after_kernel(x_ref, w_ref, after_ref, out_ref):
+    project_kernel(x_ref, w_ref, out_ref)
+
+
+def project(x, w, first, groups, block=1024, after=None):
     rows, depth = x.shape
     width = w.shape[2]
     return pl.pallas_call(
-        project_kernel,
+        project_kernel if after is None else project_after_kernel,
         grid=(groups, width // block),
         in_specs=[
             pl.BlockSpec((rows, depth), lambda g, j: (0, 0)),
             pl.BlockSpec((None, depth, block), lambda g, j: (g + first, 0, j)),
-        ],
+        ]
+        + ([] if after is None else [pl.BlockSpec(after.shape, lambda g, j: (0,) * after.ndim)]),
         out_specs=pl.BlockSpec((None, rows, block), lambda g, j: (g, 0, j)),
         out_shape=jax.ShapeDtypeStruct((groups, rows, width), jnp.float32),
         compiler_params=pltpu.CompilerParams(vmem_limit_bytes=48 * 1024 * 1024),
@@ -228,7 +233,7 @@
             bytes_accessed=2 * (rows * depth + groups * depth * width) + 4 * groups * rows * width,
             transcendentals=0,
         ),
-    )(x, w)
+    )(x, w, *([] if after is None else [after]))
 
 
 def shards(
@@ -258,11 +263,6 @@
         per_head = block.reshape(row_count, heads_here, HEAD).transpose(1, 0, 2)
         return jnp.repeat(per_head, devices // heads_here, axis=0)
 
-    cache_kv = lax.all_to_all(
-        jnp.concatenate([by_head(cache_keys), by_head(cache_values)], axis=1),
-        "context", 0, 0, tiled=True,
-    )
-    cache_k, cache_v = cache_kv[:, :row_count], cache_kv[:, row_count:]
 
     received = shifted(streams[row_count - (tap_count - 1) :], "context", 1)
     channels = streams.shape[2]
@@ -325,10 +325,21 @@
         .transpose(2, 0, 1, 3)
         .reshape(devices, half_rows, HEAD)
     )
-    my_queries = lax.all_to_all(query_parts, "context", 0, 0, tiled=True)
-    kv_proj = project(normed, weights3, 1, 2).reshape(2, row_count, heads_here, HEAD)
+    first_sent = lax.all_to_all(
+        jnp.concatenate([by_head(cache_keys), by_head(cache_values), query_parts], axis=1),
+        "context", 0, 0, tiled=True,
+    )
+    kv_proj = project(normed, weights3, 1, 2, after=query_parts).reshape(
+        2, row_count, heads_here, HEAD
+    )
     new_keys = rotate(kv_proj[0], positions).astype(jnp.bfloat16)
     new_values = kv_proj[1].astype(jnp.bfloat16)
+    new_keys, new_values, first_sent = lax.optimization_barrier(
+        (new_keys, new_values, first_sent)
+    )
+    cache_k = first_sent[:, :row_count]
+    cache_v = first_sent[:, row_count : 2 * row_count]
+    my_queries = first_sent[:, 2 * row_count :]
     new_kv = lax.all_to_all(
         jnp.concatenate([by_head(new_keys), by_head(new_values)], axis=1),
         "context", 0, 0, tiled=True,

time: 124 us -> 126 us (1.016)
  waiting for transfers between devices: 29.8 us -> 35.3 us
  starting transfers between devices: 23.6 us -> 19.6 us
    all_to_all x1, waiting for transfers between devices: 1.15 us -> 10.9 us  [shards(): lax.all_to_all(jnp.concatenate([by_head(cache_keys), by_head(cache_values...]
    all_to_all x1 -> x0, waiting for transfers between devices: 5.63 us -> none  [shards(): my_queries = lax.all_to_all(query_parts, 'context', 0, 0, tiled=True)]
    all_to_all x1 -> x0, starting transfers between devices: 4.61 us -> none  [shards(): my_queries = lax.all_to_all(query_parts, 'context', 0, 0, tiled=True)]
    all_to_all x1, waiting for transfers between devices: 11 us -> 12.3 us  [shards(): gathered = lax.all_to_all(hidden_out, 'tensor', 0, 0, tiled=True)]
  transfers between devices with their start and end apart: 5 -> 4, of which waited for: 5 -> 4; matrix products, arithmetic and copies ran while one was open for 5% -> 1% of each run, Pallas kernels for 13% -> 9%
where the time goes in v12:
time: 126 us; the launch traced here: 125 us
  waiting for transfers between devices  35.3 us (28%)
  Pallas kernels  32.4 us (26%)
  blocking collectives  27 us (21%)
  starting transfers between devices  19.6 us (16%)
  local copies, waits for them, and re-layouts  5.61 us (4%)
  other arithmetic  4.32 us (3%)
    all_to_all x1, blocking collectives, shards(): finals = lax.all_to_all(finals_out, 'context', 0, 0, tiled=True)  16.5 us
    all_to_all x1, waiting for transfers between devices, shards(): gathered = lax.all_to_all(hidden_out, 'tensor', 0, 0, tiled=True)  12.3 us
    pallas_call x2, Pallas kernels, channel_blocks(): pl.pallas_call(kernel, grid_spec=grid_spec, out_shape=outputs)  11.7 us
    pallas_call x2, Pallas kernels, project(): pl.pallas_call(project_kernel if after is None else project_after_kernel,...  11.7 us
    all_to_all x1, waiting for transfers between devices, shards(): lax.all_to_all(jnp.concatenate([by_head(new_keys), by_head(new_values)],...  11.3 us
    all_to_all x1, waiting for transfers between devices, shards(): lax.all_to_all(jnp.concatenate([by_head(cache_keys), by_head(cache_values...  10.9 us
    all_to_all x1, blocking collectives, shards(): back = lax.all_to_all(mine, 'context', 0, 0, tiled=True)  10.4 us
    all_to_all x1, starting transfers between devices, shards(): lax.all_to_all(jnp.concatenate([by_head(cache_keys), by_head(cache_values...  6.07 us
  transfers between devices with their start and end apart: 4, of which 4 were waited for; matrix products, arithmetic and copies ran while one was open for 1% of the time, Pallas kernels for 9%

profile of v12, /device:TPU:1, one launch (start us, length us, event | category | flops | bytes accessed | tf_op | source)
XLA Modules:
  0.0 125.2 jit_solution(14852705535747828687)
XLA Ops:
  0.0 0.8 slice.39
  0.8 4.6 %collective-permute-start = (bf16[2,3,1024]{2,0,1:T(2,128)(2,1)S(1)}, bf16[2,3,1024]{2,0,1:T(2,128)(2,1)S(1)}, u32[]{:S(2)}, u32[]{:S(2)}) collective-permute-start(bf16[2,3,1024]{2,0,1:T(2,128)(2,1)S(1)} %slice.39), channel_id=1, source_target_pairs={{0,4},{4,8},{8,12},{12,16},{16,20},{20,24},{24,28},{28,32},{32,36}... | collective-permute-start | bytes 36872 | tf_op jit(solution)/shard_map/ppermute | solution.py:21
  5.4 0.8 collective-permute-done
  6.2 0.6 copy-done.3
  6.8 7.0 %shard_map.127 = (bf16[128,1024]{1,0:T(8,128)(2,1)}, f32[128,1024]{1,0:T(8,128)}, f32[128,1024]{1,0:T(8,128)}, bf16[16,16,1024]{2,1,0:T(8,128)(2,1)}) custom-call(s32[1]{0:T(128)} %bitcast.idx_ref, bf16[3,128,1024]{2,1,0:T(8,128)(2,1)} %bitcast.82, bf16[3,2,1024]{2,1,0:T(2,128)(2,1)} %bitcast.86, bf16[3,2,1024]{2,1,0:T(2,128)(2,1)} %bitcast.85, ...), custom_call_target="tpu_custom_call" | custom-call | tf_op jit(solution)/shard_map/pallas_call | solution.py:122
  13.8 16.5 %all_to_all.25.fin_ref = bf16[16,16,1024]{2,1,0:T(8,128)(2,1)} all-to-all(bf16[16,16,1024]{2,1,0:T(8,128)(2,1)} %get-tuple-element.16), channel_id=1, replica_groups=mesh['dp'=2,'context'=16,'tensor'=4] {'context'}, dimensions={0} | all-to-all | bytes 1048576 | tf_op jit(solution)/shard_map/all_to_all | solution.py:293
  30.3 4.7 %shard_map.128 = bf16[4,128,1024]{2,1,0:T(8,128)(2,1)} custom-call(s32[1]{0:T(128)} %bitcast.idx_ref, f32[128,1024]{1,0:T(8,128)} %get-tuple-element.15.local_ref, f32[16,1024]{1,0:T(8,128)} %rate_ref.3, f32[16,1024]{1,0:T(8,128)} %res_ref.3, bf16[16,16,1024]{2,1,0:T(8,128)(2,1)} %all_to_all.25.fin_ref, f32[16,1024]{1,0:T(8,128)} %hs_ref.1, ...), custom_call_target="tpu_custom_call" | custom-call | tf_op jit(solution)/shard_map/pallas_call | solution.py:122
  35.1 4.2 %all-to-all-start.1 = ((bf16[4,128,1024]{2,1,0:T(8,128)(2,1)}), bf16[4,128,1024]{2,1,0:T(8,128)(2,1)S(1)}, u32[]{:S(2)}, u32[]{:S(2)}) async-start(bf16[4,128,1024]{2,1,0:T(8,128)(2,1)} %shard_map.128), calls=%async_computation.1 | async-start | bytes 2097152 | tf_op jit(solution)/shard_map/all_to_all | solution.py:311
  40.1 0.3 multiply_cosine_fusion
  40.4 12.3 %all-to-all-done.1 = bf16[4,128,1024]{2,1,0:T(8,128)(2,1)S(1)} async-done(((bf16[4,128,1024]{2,1,0:T(8,128)(2,1)}), bf16[4,128,1024]{2,1,0:T(8,128)(2,1)S(1)}, u32[]{:S(2)}, u32[]{:S(2)}) %all-to-all-start.1) | async-done | bytes 1048608 | tf_op jit(solution)/shard_map/all_to_all | solution.py:311
  54.0 4.6 %shard_map.129 = f32[1,128,1024]{2,1,0:T(8,128)S(1)} custom-call(bf16[128,4096]{1,0:T(8,128)(2,1)S(1)} %multiply_convert_fusion.x_ref, bf16[3,4096,1024]{2,1,0:T(8,128)(2,1)} %bitcast.65), custom_call_target="tpu_custom_call" | custom-call | flops 1073741824 | bytes 9961472 | tf_op jit(solution)/shard_map/pallas_call | solution.py:220
  59.4 1.2 pad_maximum_fusion
  60.6 6.1 %all-to-all-start.2 = ((bf16[16,320,128]{2,1,0:T(8,128)(2,1)}), bf16[16,320,128]{2,1,0:T(8,128)(2,1)S(1)}, u32[]{:S(2)}, u32[]{:S(2)}) async-start(bf16[16,320,128]{2,1,0:T(8,128)(2,1)} %pad_maximum_fusion), calls=%async_computation.2 | async-start | bytes 2621440 | tf_op jit(solution)/shard_map/all_to_all | solution.py:328
  66.7 7.1 %shard_map.130 = f32[2,128,1024]{2,1,0:T(8,128)S(1)} custom-call(bf16[128,4096]{1,0:T(8,128)(2,1)S(1)} %multiply_convert_fusion.x_ref, bf16[3,4096,1024]{2,1,0:T(8,128)(2,1)} %bitcast.66, bf16[16,64,128]{2,1,0:T(8,128)(2,1)S(1)} %bitcast.56), custom_call_target="tpu_custom_call" | custom-call | flops 2147483648 | bytes 18874368 | tf_op jit(solution)/shard_map/pallas_call | solution.py:220
  74.4 10.9 %all-to-all-done.2 = bf16[16,320,128]{2,1,0:T(8,128)(2,1)S(1)} async-done(((bf16[16,320,128]{2,1,0:T(8,128)(2,1)}), bf16[16,320,128]{2,1,0:T(8,128)(2,1)S(1)}, u32[]{:S(2)}, u32[]{:S(2)}) %all-to-all-start.2) | async-done | bytes 1310752 | tf_op jit(solution)/shard_map/all_to_all | solution.py:328
  85.6 1.1 pad_maximum_fusion.1
  86.7 4.8 %all-to-all-start.3 = ((bf16[16,256,128]{2,1,0:T(8,128)(2,1)}), bf16[16,256,128]{2,1,0:T(8,128)(2,1)}, u32[]{:S(2)}, u32[]{:S(2)}) async-start(bf16[16,256,128]{2,1,0:T(8,128)(2,1)} %pad_maximum_fusion.1), calls=%async_computation.3 | async-start | bytes 2097152 | tf_op jit(solution)/shard_map/all_to_all | solution.py:343
  91.6 0.5 add.90.qpos_ref
  92.2 4.0 %shard_map.131 = (f32[1024,128]{1,0:T(8,128)S(1)}, f32[1024,128]{1,0:T(8,128)S(1)}, f32[1024,128]{1,0:T(8,128)S(1)}) custom-call(bf16[1024,128]{1,0:T(8,128)(2,1)S(1)} %bitcast.60, bf16[2048,128]{1,0:T(8,128)(2,1)S(1)} %bitcast.64, bf16[2048,128]{1,0:T(8,128)(2,1)S(1)} %bitcast.63), custom_call_target="tpu_custom_call" | custom-call | flops 1610612736 | bytes 2883584 | tf_op jit(solution)/shard_map/pallas_call | solution.py:168
  96.2 11.3 %all-to-all-done.3 = bf16[16,256,128]{2,1,0:T(8,128)(2,1)} async-done(((bf16[16,256,128]{2,1,0:T(8,128)(2,1)}), bf16[16,256,128]{2,1,0:T(8,128)(2,1)}, u32[]{:S(2)}, u32[]{:S(2)}) %all-to-all-start.3) | async-done | bytes 1048608 | tf_op jit(solution)/shard_map/all_to_all | solution.py:343
  107.5 1.3 %fusion.3 = (bf16[16,128,128]{2,1,0:T(8,128)(2,1)S(1)}, bf16[16,128,128]{2,1,0:T(8,128)(2,1)S(1)}) fusion(bf16[16,256,128]{2,1,0:T(8,128)(2,1)} %all-to-all-done.3), kind=kLoop, calls=%fused_computation.24 | loop fusion | bytes 2097152 | tf_op jit(solution)/shard_map/slice | solution.py:355
  108.8 5.0 %shard_map.132 = bf16[1024,128]{1,0:T(8,128)(2,1)S(1)} custom-call(bf16[1024,128]{1,0:T(8,128)(2,1)S(1)} %bitcast.61, bf16[2048,128]{1,0:T(8,128)(2,1)S(1)} %bitcast.59, bf16[2048,128]{1,0:T(8,128)(2,1)S(1)} %bitcast.58, s32[1024,1]{1,0:T(8,128)S(1)} %add.90.qpos_ref, f32[1024,128]{1,0:T(8,128)S(1)} %get-tuple-element.22.max_ref, ...), custom_call_target="tpu_custom_call" | custom-call | tf_op jit(solution)/shard_map/pallas_call | solution.py:191
  113.8 10.4 %all_to_all.26 = bf16[16,64,128]{2,1,0:T(8,128)(2,1)S(1)} all-to-all(bf16[16,64,128]{2,1,0:T(8,128)(2,1)S(1)} %bitcast.62), channel_id=1, replica_groups=mesh['dp'=2,'context'=16,'tensor'=4] {'context'}, dimensions={0} | all-to-all | bytes 524288 | tf_op jit(solution)/shard_map/all_to_all | solution.py:359
  124.5 0.8 copy.39
  (40 shorter events, 3.4 us)
Async XLA Ops:
  0.8 5.4 %collective-permute-start = (bf16[2,3,1024]{2,0,1:T(2,128)(2,1)S(1)}, bf16[2,3,1024]{2,0,1:T(2,128)(2,1)S(1)}, u32[]{:S(2)}, u32[]{:S(2)}) collective-permute-start(bf16[2,3,1024]{2,0,1:T(2,128)(2,1)S(1)} %slice.39), channel_id=1, source_target_pairs={{0,4},{4,8},{8,12},{12,16},{16,20},{20,24},{24,28},{28,32},{32,36}... | collective-permute-start | bytes 36872 | tf_op jit(solution)/shard_map/ppermute | solution.py:21
  6.2 0.6 copy-start.3
  30.3 9.5 %copy-start = (bf16[128,1024]{1,0:T(8,128)(2,1)S(1)}, bf16[128,1024]{1,0:T(8,128)(2,1)}, u32[]{:S(2)}) copy-start(bf16[128,1024]{1,0:T(8,128)(2,1)} %param.24) | copy-start | bytes 786436
  35.1 4.9 %copy-start.1 = (bf16[128,1024]{1,0:T(8,128)(2,1)S(1)}, bf16[128,1024]{1,0:T(8,128)(2,1)}, u32[]{:S(2)}) copy-start(bf16[128,1024]{1,0:T(8,128)(2,1)} %param.25) | copy-start | bytes 786436
  35.1 17.6 %all-to-all-start.1 = ((bf16[4,128,1024]{2,1,0:T(8,128)(2,1)}), bf16[4,128,1024]{2,1,0:T(8,128)(2,1)S(1)}, u32[]{:S(2)}, u32[]{:S(2)}) async-start(bf16[4,128,1024]{2,1,0:T(8,128)(2,1)} %shard_map.128), calls=%async_computation.1 | async-start | bytes 2097152 | tf_op jit(solution)/shard_map/all_to_all | solution.py:311
  52.9 0.7 copy-start.2
  60.6 24.7 %all-to-all-start.2 = ((bf16[16,320,128]{2,1,0:T(8,128)(2,1)}), bf16[16,320,128]{2,1,0:T(8,128)(2,1)S(1)}, u32[]{:S(2)}, u32[]{:S(2)}) async-start(bf16[16,320,128]{2,1,0:T(8,128)(2,1)} %pad_maximum_fusion), calls=%async_computation.2 | async-start | bytes 2621440 | tf_op jit(solution)/shard_map/all_to_all | solution.py:328
  86.7 20.8 %all-to-all-start.3 = ((bf16[16,256,128]{2,1,0:T(8,128)(2,1)}), bf16[16,256,128]{2,1,0:T(8,128)(2,1)}, u32[]{:S(2)}, u32[]{:S(2)}) async-start(bf16[16,256,128]{2,1,0:T(8,128)(2,1)} %pad_maximum_fusion.1), calls=%async_computation.3 | async-start | bytes 2097152 | tf_op jit(solution)/shard_map/all_to_all | solution.py:343

commit v13 on v11

--- a/solution.py
+++ b/solution.py
@@ -210,15 +210,15 @@
     out_ref[...] = jnp.dot(x_ref[...], w_ref[...], preferred_element_type=jnp.float32)
 
 
-def project(x, w, first, groups, block=1024):
+def project(x, w, block=1024):
     rows, depth = x.shape
-    width = w.shape[2]
+    groups, _, width = w.shape
     return pl.pallas_call(
         project_kernel,
         grid=(groups, width // block),
         in_specs=[
             pl.BlockSpec((rows, depth), lambda g, j: (0, 0)),
-            pl.BlockSpec((None, depth, block), lambda g, j: (g + first, 0, j)),
+            pl.BlockSpec((None, depth, block), lambda g, j: (g, 0, j)),
         ],
         out_specs=pl.BlockSpec((None, rows, block), lambda g, j: (g, 0, j)),
         out_shape=jax.ShapeDtypeStruct((groups, rows, width), jnp.float32),
@@ -315,35 +315,37 @@
     normed = (hidden_float * lax.rsqrt(mean_square + NORM_EPSILON) * norm_gain[None, :]).astype(
         jnp.bfloat16
     )
-    weights3 = qkv_weight.transpose(1, 0, 2)
+    projected = (
+        project(normed, qkv_weight.transpose(1, 0, 2))
+        .transpose(1, 0, 2)
+        .reshape(row_count, 3, heads_here, HEAD)
+    )
     query_index = device_index * row_count + jnp.arange(row_count, dtype=jnp.int32)
     positions = (start_offset[0] + query_index).astype(jnp.float32)
-    query_proj = project(normed, weights3, 0, 1)[0].reshape(row_count, heads_here, HEAD)
-    queries = rotate(query_proj, positions).astype(jnp.bfloat16)
+    queries = rotate(projected[:, 0], positions).astype(jnp.bfloat16)
+    new_keys = rotate(projected[:, 1], positions).astype(jnp.bfloat16)
+    new_values = projected[:, 2].astype(jnp.bfloat16)
+
     query_parts = (
         queries.reshape(2, half_rows, heads_here, HEAD)
         .transpose(2, 0, 1, 3)
         .reshape(devices, half_rows, HEAD)
     )
-    my_queries = lax.all_to_all(query_parts, "context", 0, 0, tiled=True)
-    kv_proj = project(normed, weights3, 1, 2).reshape(2, row_count, heads_here, HEAD)
-    new_keys = rotate(kv_proj[0], positions).astype(jnp.bfloat16)
-    new_values = kv_proj[1].astype(jnp.bfloat16)
-    new_kv = lax.all_to_all(
-        jnp.concatenate([by_head(new_keys), by_head(new_values)], axis=1),
+    sent = lax.all_to_all(
+        jnp.concatenate([query_parts, by_head(new_keys), by_head(new_values)], axis=1),
         "context", 0, 0, tiled=True,
     )
+    my_queries = sent[:, :half_rows]
+    new_k = sent[:, half_rows : half_rows + row_count]
+    new_v = sent[:, half_rows + row_count :]
+
     q_flat = my_queries.reshape(-1, HEAD)
-    pieces = attend_cache(q_flat, cache_k.reshape(-1, HEAD), cache_v.reshape(-1, HEAD))
     src = jnp.arange(devices, dtype=jnp.int32)[:, None]
     row = jnp.arange(half_rows, dtype=jnp.int32)[None, :]
     query_pos = (src * row_count + (device_index % 2) * half_rows + row).reshape(-1)
+    pieces = attend_cache(q_flat, cache_k.reshape(-1, HEAD), cache_v.reshape(-1, HEAD))
     mine = attend_new(
-        q_flat,
-        new_kv[:, :row_count].reshape(-1, HEAD),
-        new_kv[:, row_count:].reshape(-1, HEAD),
-        query_pos,
-        pieces,
+        q_flat, new_k.reshape(-1, HEAD), new_v.reshape(-1, HEAD), query_pos, pieces
     ).reshape(devices, half_rows, HEAD)
     back = lax.all_to_all(mine, "context", 0, 0, tiled=True)
     attended = (

time: 124 us -> 120 us (0.968)
  starting transfers between devices: 23.6 us -> 19.1 us
  local copies, waits for them, and re-layouts: 4.37 us -> 6.7 us
  Pallas kernels: 32.4 us -> 30.4 us
    all_to_all x2 -> x1, starting transfers between devices: 8.79 us -> 4.26 us  [shards(): lax.all_to_all(jnp.concatenate([query_parts, by_head(new_keys), by_head(n...]
    pallas_call x2 -> x1, Pallas kernels: 11.7 us -> 9.69 us  [project(): pl.pallas_call(project_kernel, grid=(groups, width // block), in_specs=[p...]
    unnamed x16 -> x14, local copies, waits for them, and re-layouts: 1.92 us -> 2.91 us
    all_to_all x2 -> x1, waiting for transfers between devices: 16.9 us -> 16.8 us  [shards(): lax.all_to_all(jnp.concatenate([query_parts, by_head(new_keys), by_head(n...]
  transfers between devices with their start and end apart: 5 -> 4, of which waited for: 5 -> 4; matrix products, arithmetic and copies ran while one was open for 5% -> 6% of each run, Pallas kernels for 13% -> 8%
where the time goes in v13:
time: 120 us; the launch traced here: 119 us
  waiting for transfers between devices  30.7 us (26%)
  Pallas kernels  30.4 us (25%)
  blocking collectives  27 us (22%)
  starting transfers between devices  19.1 us (16%)
  local copies, waits for them, and re-layouts  6.7 us (6%)
  other arithmetic  4.22 us (4%)
    all_to_all x1, waiting for transfers between devices, shards(): lax.all_to_all(jnp.concatenate([query_parts, by_head(new_keys), by_head(n...  16.8 us
    all_to_all x1, blocking collectives, shards(): finals = lax.all_to_all(finals_out, 'context', 0, 0, tiled=True)  16.5 us
    pallas_call x2, Pallas kernels, channel_blocks(): pl.pallas_call(kernel, grid_spec=grid_spec, out_shape=outputs)  11.7 us
    all_to_all x1, waiting for transfers between devices, shards(): gathered = lax.all_to_all(hidden_out, 'tensor', 0, 0, tiled=True)  11 us
    all_to_all x1, blocking collectives, shards(): back = lax.all_to_all(mine, 'context', 0, 0, tiled=True)  10.5 us
    pallas_call x1, Pallas kernels, project(): pl.pallas_call(project_kernel, grid=(groups, width // block), in_specs=[p...  9.69 us
    all_to_all x1, starting transfers between devices, shards(): lax.all_to_all(jnp.concatenate([by_head(cache_keys), by_head(cache_values...  6.07 us
    pallas_call x1, Pallas kernels, attend_new(): pl.pallas_call(functools.partial(new_attention_kernel, 1.0 / math.sqrt(wi...  5 us
  transfers between devices with their start and end apart: 4, of which 4 were waited for; matrix products, arithmetic and copies ran while one was open for 6% of the time, Pallas kernels for 8%

profile of v13, /device:TPU:1, one launch (start us, length us, event | category | flops | bytes accessed | tf_op | source)
XLA Modules:
  0.0 119.0 jit_solution(12182063641868447359)
XLA Ops:
  0.0 0.8 slice.40
  0.8 4.6 %collective-permute-start = (bf16[2,3,1024]{2,0,1:T(2,128)(2,1)S(1)}, bf16[2,3,1024]{2,0,1:T(2,128)(2,1)S(1)}, u32[]{:S(2)}, u32[]{:S(2)}) collective-permute-start(bf16[2,3,1024]{2,0,1:T(2,128)(2,1)S(1)} %slice.40), channel_id=1, source_target_pairs={{0,4},{4,8},{8,12},{12,16},{16,20},{20,24},{24,28},{28,32},{32,36}... | collective-permute-start | bytes 36872 | tf_op jit(solution)/shard_map/ppermute | solution.py:21
  5.4 0.8 collective-permute-done
  6.2 0.6 copy-done.4
  6.8 7.0 %shard_map.127 = (bf16[128,1024]{1,0:T(8,128)(2,1)}, f32[128,1024]{1,0:T(8,128)}, f32[128,1024]{1,0:T(8,128)}, bf16[16,16,1024]{2,1,0:T(8,128)(2,1)}) custom-call(s32[1]{0:T(128)} %bitcast.idx_ref, bf16[3,128,1024]{2,1,0:T(8,128)(2,1)} %bitcast.82, bf16[3,2,1024]{2,1,0:T(2,128)(2,1)} %bitcast.86, bf16[3,2,1024]{2,1,0:T(2,128)(2,1)} %bitcast.85, ...), custom_call_target="tpu_custom_call" | custom-call | tf_op jit(solution)/shard_map/pallas_call | solution.py:122
  13.8 16.5 %all_to_all.25.fin_ref = bf16[16,16,1024]{2,1,0:T(8,128)(2,1)} all-to-all(bf16[16,16,1024]{2,1,0:T(8,128)(2,1)} %get-tuple-element.13), channel_id=1, replica_groups=mesh['dp'=2,'context'=16,'tensor'=4] {'context'}, dimensions={0} | all-to-all | bytes 1048576 | tf_op jit(solution)/shard_map/all_to_all | solution.py:293
  30.3 4.7 %shard_map.128 = bf16[4,128,1024]{2,1,0:T(8,128)(2,1)} custom-call(s32[1]{0:T(128)} %bitcast.idx_ref, f32[128,1024]{1,0:T(8,128)} %get-tuple-element.12.local_ref, f32[16,1024]{1,0:T(8,128)} %rate_ref.3, f32[16,1024]{1,0:T(8,128)} %res_ref.3, bf16[16,16,1024]{2,1,0:T(8,128)(2,1)} %all_to_all.25.fin_ref, f32[16,1024]{1,0:T(8,128)} %hs_ref.1, ...), custom_call_target="tpu_custom_call" | custom-call | tf_op jit(solution)/shard_map/pallas_call | solution.py:122
  35.1 4.1 %all-to-all-start.1 = ((bf16[4,128,1024]{2,1,0:T(8,128)(2,1)}), bf16[4,128,1024]{2,1,0:T(8,128)(2,1)S(1)}, u32[]{:S(2)}, u32[]{:S(2)}) async-start(bf16[4,128,1024]{2,1,0:T(8,128)(2,1)} %shard_map.128), calls=%async_computation.1 | async-start | bytes 2097152 | tf_op jit(solution)/shard_map/all_to_all | solution.py:311
  40.3 1.1 pad_maximum_fusion.1
  41.7 11.0 %all-to-all-done.1 = bf16[4,128,1024]{2,1,0:T(8,128)(2,1)S(1)} async-done(((bf16[4,128,1024]{2,1,0:T(8,128)(2,1)}), bf16[4,128,1024]{2,1,0:T(8,128)(2,1)S(1)}, u32[]{:S(2)}, u32[]{:S(2)}) %all-to-all-start.1) | async-done | bytes 1048608 | tf_op jit(solution)/shard_map/all_to_all | solution.py:311
  52.7 6.1 %all-to-all-start.3 = ((bf16[16,256,128]{2,1,0:T(8,128)(2,1)}), bf16[16,256,128]{2,1,0:T(8,128)(2,1)S(1)}, u32[]{:S(2)}, u32[]{:S(2)}) async-start(bf16[16,256,128]{2,1,0:T(8,128)(2,1)} %pad_maximum_fusion.1), calls=%async_computation.3 | async-start | bytes 2097152 | tf_op jit(solution)/shard_map/all_to_all | solution.py:261
  60.0 9.7 %shard_map.129 = f32[3,128,1024]{2,1,0:T(8,128)S(1)} custom-call(bf16[128,4096]{1,0:T(8,128)(2,1)S(1)} %multiply_convert_fusion.x_ref, bf16[3,4096,1024]{2,1,0:T(8,128)(2,1)} %bitcast.67), custom_call_target="tpu_custom_call" | custom-call | flops 3221225472 | bytes 27787264 | tf_op jit(solution)/shard_map/pallas_call | solution.py:216
  70.1 0.5 subtract_convert_fusion.1
  71.4 1.2 pad_maximum_fusion
  72.5 2.0 %all-to-all-done.3 = bf16[16,256,128]{2,1,0:T(8,128)(2,1)S(1)} async-done(((bf16[16,256,128]{2,1,0:T(8,128)(2,1)}), bf16[16,256,128]{2,1,0:T(8,128)(2,1)S(1)}, u32[]{:S(2)}, u32[]{:S(2)}) %all-to-all-start.3) | async-done | bytes 1048608 | tf_op jit(solution)/shard_map/all_to_all | solution.py:261
  74.6 1.0 copy-done
  75.5 4.3 %all-to-all-start.2 = ((bf16[16,320,128]{2,1,0:T(8,128)(2,1)}), bf16[16,320,128]{2,1,0:T(8,128)(2,1)S(1)}, u32[]{:S(2)}, u32[]{:S(2)}) async-start(bf16[16,320,128]{2,1,0:T(8,128)(2,1)} %pad_maximum_fusion), calls=%async_computation.2 | async-start | bytes 2621440 | tf_op jit(solution)/shard_map/all_to_all | solution.py:334
  79.9 0.5 add.90.qpos_ref
  80.3 1.3 %fusion.3 = (bf16[16,128,128]{2,1,0:T(8,128)(2,1)S(1)}, bf16[16,128,128]{2,1,0:T(8,128)(2,1)S(1)}) fusion(bf16[16,256,128]{2,1,0:T(8,128)(2,1)} %copy-done), kind=kLoop, calls=%fused_computation.25 | loop fusion | bytes 2097152 | tf_op jit(solution)/shard_map/slice | solution.py:265
  81.6 16.8 %all-to-all-done.2 = bf16[16,320,128]{2,1,0:T(8,128)(2,1)S(1)} async-done(((bf16[16,320,128]{2,1,0:T(8,128)(2,1)}), bf16[16,320,128]{2,1,0:T(8,128)(2,1)S(1)}, u32[]{:S(2)}, u32[]{:S(2)}) %all-to-all-start.2) | async-done | bytes 1310752 | tf_op jit(solution)/shard_map/all_to_all | solution.py:334
  98.5 4.0 %shard_map.130 = (f32[1024,128]{1,0:T(8,128)S(1)}, f32[1024,128]{1,0:T(8,128)S(1)}, f32[1024,128]{1,0:T(8,128)S(1)}) custom-call(bf16[1024,128]{1,0:T(8,128)(2,1)S(1)} %bitcast.62, bf16[2048,128]{1,0:T(8,128)(2,1)S(1)} %bitcast.66, bf16[2048,128]{1,0:T(8,128)(2,1)S(1)} %bitcast.65), custom_call_target="tpu_custom_call" | custom-call | flops 1610612736 | bytes 2883584 | tf_op jit(solution)/shard_map/pallas_call | solution.py:168
  102.6 5.0 %shard_map.131 = bf16[1024,128]{1,0:T(8,128)(2,1)S(1)} custom-call(bf16[1024,128]{1,0:T(8,128)(2,1)S(1)} %bitcast.63, bf16[2048,128]{1,0:T(8,128)(2,1)S(1)} %bitcast.61, bf16[2048,128]{1,0:T(8,128)(2,1)S(1)} %bitcast.60, s32[1024,1]{1,0:T(8,128)S(1)} %add.90.qpos_ref, f32[1024,128]{1,0:T(8,128)S(1)} %get-tuple-element.16.max_ref, ...), custom_call_target="tpu_custom_call" | custom-call | tf_op jit(solution)/shard_map/pallas_call | solution.py:191
  107.6 10.5 %all_to_all.26 = bf16[16,64,128]{2,1,0:T(8,128)(2,1)S(1)} all-to-all(bf16[16,64,128]{2,1,0:T(8,128)(2,1)S(1)} %bitcast.64), channel_id=1, replica_groups=mesh['dp'=2,'context'=16,'tensor'=4] {'context'}, dimensions={0} | all-to-all | bytes 524288 | tf_op jit(solution)/shard_map/all_to_all | solution.py:350
  118.2 0.8 copy.37
  (38 shorter events, 3.3 us)
Async XLA Ops:
  0.8 5.4 %collective-permute-start = (bf16[2,3,1024]{2,0,1:T(2,128)(2,1)S(1)}, bf16[2,3,1024]{2,0,1:T(2,128)(2,1)S(1)}, u32[]{:S(2)}, u32[]{:S(2)}) collective-permute-start(bf16[2,3,1024]{2,0,1:T(2,128)(2,1)S(1)} %slice.40), channel_id=1, source_target_pairs={{0,4},{4,8},{8,12},{12,16},{16,20},{20,24},{24,28},{28,32},{32,36}... | collective-permute-start | bytes 36872 | tf_op jit(solution)/shard_map/ppermute | solution.py:21
  6.2 0.6 copy-start.4
  30.3 9.5 %copy-start.1 = (bf16[128,1024]{1,0:T(8,128)(2,1)S(1)}, bf16[128,1024]{1,0:T(8,128)(2,1)}, u32[]{:S(2)}) copy-start(bf16[128,1024]{1,0:T(8,128)(2,1)} %param.24) | copy-start | bytes 786436
  35.1 4.9 %copy-start.2 = (bf16[128,1024]{1,0:T(8,128)(2,1)S(1)}, bf16[128,1024]{1,0:T(8,128)(2,1)}, u32[]{:S(2)}) copy-start(bf16[128,1024]{1,0:T(8,128)(2,1)} %param.25) | copy-start | bytes 786436
  35.1 17.6 %all-to-all-start.1 = ((bf16[4,128,1024]{2,1,0:T(8,128)(2,1)}), bf16[4,128,1024]{2,1,0:T(8,128)(2,1)S(1)}, u32[]{:S(2)}, u32[]{:S(2)}) async-start(bf16[4,128,1024]{2,1,0:T(8,128)(2,1)} %shard_map.128), calls=%async_computation.1 | async-start | bytes 2097152 | tf_op jit(solution)/shard_map/all_to_all | solution.py:311
  52.7 21.9 %all-to-all-start.3 = ((bf16[16,256,128]{2,1,0:T(8,128)(2,1)}), bf16[16,256,128]{2,1,0:T(8,128)(2,1)S(1)}, u32[]{:S(2)}, u32[]{:S(2)}) async-start(bf16[16,256,128]{2,1,0:T(8,128)(2,1)} %pad_maximum_fusion.1), calls=%async_computation.3 | async-start | bytes 2097152 | tf_op jit(solution)/shard_map/all_to_all | solution.py:261
  59.0 0.7 copy-start.3
  74.6 1.0 copy-start
  75.5 22.9 %all-to-all-start.2 = ((bf16[16,320,128]{2,1,0:T(8,128)(2,1)}), bf16[16,320,128]{2,1,0:T(8,128)(2,1)S(1)}, u32[]{:S(2)}, u32[]{:S(2)}) async-start(bf16[16,320,128]{2,1,0:T(8,128)(2,1)} %pad_maximum_fusion), calls=%async_computation.2 | async-start | bytes 2621440 | tf_op jit(solution)/shard_map/all_to_all | solution.py:334

commit v14 on v13

--- a/solution.py
+++ b/solution.py
@@ -137,27 +137,40 @@
     num_ref[...] = jnp.dot(weights, v_ref[...], preferred_element_type=jnp.float32)
 
 
-def new_attention_kernel(scale, q_ref, k_ref, v_ref, qpos_ref, max_ref, sum_ref, num_ref, out_ref):
-    scores = (
-        lax.dot_general(
-            q_ref[...], k_ref[...], (((1,), (1,)), ((), ())), preferred_element_type=jnp.float32
-        )
-        * scale
-    )
-    key_pos = lax.broadcasted_iota(jnp.int32, (1, scores.shape[1]), 1)
-    scores = jnp.where(key_pos <= qpos_ref[...], scores, -jnp.inf)
-    old_max = max_ref[:, :1]
-    row_max = jnp.maximum(old_max, jnp.max(scores, axis=1, keepdims=True))
-    rescale = jnp.exp(old_max - row_max)
-    weights = jnp.exp(scores - row_max).astype(jnp.bfloat16)
-    ones = jnp.ones((weights.shape[1], 128), jnp.bfloat16)
-    weight_sum = sum_ref[:, :1] * rescale + jnp.dot(
-        weights, ones, preferred_element_type=jnp.float32
-    )[:, :1]
-    numerator = num_ref[...] * rescale + jnp.dot(
-        weights, v_ref[...], preferred_element_type=jnp.float32
-    )
-    out_ref[...] = (numerator / weight_sum).astype(out_ref.dtype)
+def new_attention_kernel(
+    scale, reach, q_ref, k_ref, v_ref, qpos_ref, max_ref, sum_ref, num_ref, out_ref
+):
+    def block_with(keys):
+        scores = (
+            lax.dot_general(
+                q_ref[...], k_ref[:keys], (((1,), (1,)), ((), ())),
+                preferred_element_type=jnp.float32,
+            )
+            * scale
+        )
+        key_pos = lax.broadcasted_iota(jnp.int32, (1, keys), 1)
+        scores = jnp.where(key_pos <= qpos_ref[...], scores, -jnp.inf)
+        old_max = max_ref[:, :1]
+        row_max = jnp.maximum(old_max, jnp.max(scores, axis=1, keepdims=True))
+        rescale = jnp.exp(old_max - row_max)
+        weights = jnp.exp(scores - row_max).astype(jnp.bfloat16)
+        ones = jnp.ones((keys, 128), jnp.bfloat16)
+        weight_sum = sum_ref[:, :1] * rescale + jnp.dot(
+            weights, ones, preferred_element_type=jnp.float32
+        )[:, :1]
+        numerator = num_ref[...] * rescale + jnp.dot(
+            weights, v_ref[:keys], preferred_element_type=jnp.float32
+        )
+        out_ref[...] = (numerator / weight_sum).astype(out_ref.dtype)
+
+    key_rows = k_ref.shape[0]
+    for i in range(pl.cdiv(key_rows, reach)):
+        keys = min(key_rows, reach * (i + 1))
+        last = keys == key_rows
+
+        @pl.when((pl.program_id(0) >= i) if last else (pl.program_id(0) == i))
+        def _():
+            block_with(keys)
 
 
 def attend_cache(queries, keys, values, block=512):
@@ -184,12 +197,12 @@
     )(queries, keys, values)
 
 
-def attend_new(queries, keys, values, query_pos, pieces, block=512):
+def attend_new(queries, keys, values, query_pos, pieces, spread, block=512):
     rows, width = queries.shape
     key_rows = keys.shape[0]
     row_spec = pl.BlockSpec((block, width), lambda i: (i, 0))
     return pl.pallas_call(
-        functools.partial(new_attention_kernel, 1.0 / math.sqrt(width)),
+        functools.partial(new_attention_kernel, 1.0 / math.sqrt(width), block * spread),
         grid=(rows // block,),
         in_specs=[
             row_spec,
@@ -345,7 +358,8 @@
     query_pos = (src * row_count + (device_index % 2) * half_rows + row).reshape(-1)
     pieces = attend_cache(q_flat, cache_k.reshape(-1, HEAD), cache_v.reshape(-1, HEAD))
     mine = attend_new(
-        q_flat, new_k.reshape(-1, HEAD), new_v.reshape(-1, HEAD), query_pos, pieces
+        q_flat, new_k.reshape(-1, HEAD), new_v.reshape(-1, HEAD), query_pos, pieces,
+        row_count // half_rows,
     ).reshape(devices, half_rows, HEAD)
     back = lax.all_to_all(mine, "context", 0, 0, tiled=True)
     attended = (

time: 120 us -> 119 us (level)
  no operation moved by 1% of the time
where the time goes in v14:
time: 119 us; the launch traced here: 118 us
  waiting for transfers between devices  30.7 us (26%)
  Pallas kernels  29.4 us (25%)
  blocking collectives  27 us (23%)
  starting transfers between devices  19.1 us (16%)
  local copies, waits for them, and re-layouts  6.7 us (6%)
  other arithmetic  4.22 us (4%)
    all_to_all x1, waiting for transfers between devices, shards(): lax.all_to_all(jnp.concatenate([query_parts, by_head(new_keys), by_head(n...  16.8 us
    all_to_all x1, blocking collectives, shards(): finals = lax.all_to_all(finals_out, 'context', 0, 0, tiled=True)  16.5 us
    pallas_call x2, Pallas kernels, channel_blocks(): pl.pallas_call(kernel, grid_spec=grid_spec, out_shape=outputs)  11.7 us
    all_to_all x1, waiting for transfers between devices, shards(): gathered = lax.all_to_all(hidden_out, 'tensor', 0, 0, tiled=True)  11 us
    all_to_all x1, blocking collectives, shards(): back = lax.all_to_all(mine, 'context', 0, 0, tiled=True)  10.5 us
    pallas_call x1, Pallas kernels, project(): pl.pallas_call(project_kernel, grid=(groups, width // block), in_specs=[p...  9.69 us
    all_to_all x1, starting transfers between devices, shards(): lax.all_to_all(jnp.concatenate([by_head(cache_keys), by_head(cache_values...  6.07 us
    ppermute x1, starting transfers between devices, shifted(): return lax.ppermute(x, axis, pairs)  4.58 us
  transfers between devices with their start and end apart: 4, of which 4 were waited for; matrix products, arithmetic and copies ran while one was open for 6% of the time, Pallas kernels for 8%

profile of v14, /device:TPU:1, one launch (start us, length us, event | category | flops | bytes accessed | tf_op | source)
XLA Modules:
  0.0 118.0 jit_solution(15381212020869716438)
XLA Ops:
  0.0 0.8 slice.40
  0.8 4.6 %collective-permute-start = (bf16[2,3,1024]{2,0,1:T(2,128)(2,1)S(1)}, bf16[2,3,1024]{2,0,1:T(2,128)(2,1)S(1)}, u32[]{:S(2)}, u32[]{:S(2)}) collective-permute-start(bf16[2,3,1024]{2,0,1:T(2,128)(2,1)S(1)} %slice.40), channel_id=1, source_target_pairs={{0,4},{4,8},{8,12},{12,16},{16,20},{20,24},{24,28},{28,32},{32,36}... | collective-permute-start | bytes 36872 | tf_op jit(solution)/shard_map/ppermute | solution.py:21
  5.4 0.8 collective-permute-done
  6.2 0.6 copy-done.4
  6.8 7.0 %shard_map.127 = (bf16[128,1024]{1,0:T(8,128)(2,1)}, f32[128,1024]{1,0:T(8,128)}, f32[128,1024]{1,0:T(8,128)}, bf16[16,16,1024]{2,1,0:T(8,128)(2,1)}) custom-call(s32[1]{0:T(128)} %bitcast.idx_ref, bf16[3,128,1024]{2,1,0:T(8,128)(2,1)} %bitcast.82, bf16[3,2,1024]{2,1,0:T(2,128)(2,1)} %bitcast.86, bf16[3,2,1024]{2,1,0:T(2,128)(2,1)} %bitcast.85, ...), custom_call_target="tpu_custom_call" | custom-call | tf_op jit(solution)/shard_map/pallas_call | solution.py:122
  13.8 16.5 %all_to_all.25.fin_ref = bf16[16,16,1024]{2,1,0:T(8,128)(2,1)} all-to-all(bf16[16,16,1024]{2,1,0:T(8,128)(2,1)} %get-tuple-element.13), channel_id=1, replica_groups=mesh['dp'=2,'context'=16,'tensor'=4] {'context'}, dimensions={0} | all-to-all | bytes 1048576 | tf_op jit(solution)/shard_map/all_to_all | solution.py:306
  30.3 4.7 %shard_map.128 = bf16[4,128,1024]{2,1,0:T(8,128)(2,1)} custom-call(s32[1]{0:T(128)} %bitcast.idx_ref, f32[128,1024]{1,0:T(8,128)} %get-tuple-element.12.local_ref, f32[16,1024]{1,0:T(8,128)} %rate_ref.3, f32[16,1024]{1,0:T(8,128)} %res_ref.3, bf16[16,16,1024]{2,1,0:T(8,128)(2,1)} %all_to_all.25.fin_ref, f32[16,1024]{1,0:T(8,128)} %hs_ref.1, ...), custom_call_target="tpu_custom_call" | custom-call | tf_op jit(solution)/shard_map/pallas_call | solution.py:122
  35.1 4.1 %all-to-all-start.1 = ((bf16[4,128,1024]{2,1,0:T(8,128)(2,1)}), bf16[4,128,1024]{2,1,0:T(8,128)(2,1)S(1)}, u32[]{:S(2)}, u32[]{:S(2)}) async-start(bf16[4,128,1024]{2,1,0:T(8,128)(2,1)} %shard_map.128), calls=%async_computation.1 | async-start | bytes 2097152 | tf_op jit(solution)/shard_map/all_to_all | solution.py:324
  40.3 1.1 pad_maximum_fusion.1
  41.7 11.0 %all-to-all-done.1 = bf16[4,128,1024]{2,1,0:T(8,128)(2,1)S(1)} async-done(((bf16[4,128,1024]{2,1,0:T(8,128)(2,1)}), bf16[4,128,1024]{2,1,0:T(8,128)(2,1)S(1)}, u32[]{:S(2)}, u32[]{:S(2)}) %all-to-all-start.1) | async-done | bytes 1048608 | tf_op jit(solution)/shard_map/all_to_all | solution.py:324
  52.7 6.1 %all-to-all-start.3 = ((bf16[16,256,128]{2,1,0:T(8,128)(2,1)}), bf16[16,256,128]{2,1,0:T(8,128)(2,1)S(1)}, u32[]{:S(2)}, u32[]{:S(2)}) async-start(bf16[16,256,128]{2,1,0:T(8,128)(2,1)} %pad_maximum_fusion.1), calls=%async_computation.3 | async-start | bytes 2097152 | tf_op jit(solution)/shard_map/all_to_all | solution.py:274
  60.0 9.7 %shard_map.129 = f32[3,128,1024]{2,1,0:T(8,128)S(1)} custom-call(bf16[128,4096]{1,0:T(8,128)(2,1)S(1)} %multiply_convert_fusion.x_ref, bf16[3,4096,1024]{2,1,0:T(8,128)(2,1)} %bitcast.67), custom_call_target="tpu_custom_call" | custom-call | flops 3221225472 | bytes 27787264 | tf_op jit(solution)/shard_map/pallas_call | solution.py:229
  70.1 0.5 subtract_convert_fusion.1
  71.4 1.2 pad_maximum_fusion
  72.5 2.0 %all-to-all-done.3 = bf16[16,256,128]{2,1,0:T(8,128)(2,1)S(1)} async-done(((bf16[16,256,128]{2,1,0:T(8,128)(2,1)}), bf16[16,256,128]{2,1,0:T(8,128)(2,1)S(1)}, u32[]{:S(2)}, u32[]{:S(2)}) %all-to-all-start.3) | async-done | bytes 1048608 | tf_op jit(solution)/shard_map/all_to_all | solution.py:274
  74.6 1.0 copy-done
  75.5 4.3 %all-to-all-start.2 = ((bf16[16,320,128]{2,1,0:T(8,128)(2,1)}), bf16[16,320,128]{2,1,0:T(8,128)(2,1)S(1)}, u32[]{:S(2)}, u32[]{:S(2)}) async-start(bf16[16,320,128]{2,1,0:T(8,128)(2,1)} %pad_maximum_fusion), calls=%async_computation.2 | async-start | bytes 2621440 | tf_op jit(solution)/shard_map/all_to_all | solution.py:347
  79.9 0.5 add.90.qpos_ref
  80.3 1.3 %fusion.3 = (bf16[16,128,128]{2,1,0:T(8,128)(2,1)S(1)}, bf16[16,128,128]{2,1,0:T(8,128)(2,1)S(1)}) fusion(bf16[16,256,128]{2,1,0:T(8,128)(2,1)} %copy-done), kind=kLoop, calls=%fused_computation.25 | loop fusion | bytes 2097152 | tf_op jit(solution)/shard_map/slice | solution.py:278
  81.6 16.8 %all-to-all-done.2 = bf16[16,320,128]{2,1,0:T(8,128)(2,1)S(1)} async-done(((bf16[16,320,128]{2,1,0:T(8,128)(2,1)}), bf16[16,320,128]{2,1,0:T(8,128)(2,1)S(1)}, u32[]{:S(2)}, u32[]{:S(2)}) %all-to-all-start.2) | async-done | bytes 1310752 | tf_op jit(solution)/shard_map/all_to_all | solution.py:347
  98.5 4.0 %shard_map.130 = (f32[1024,128]{1,0:T(8,128)S(1)}, f32[1024,128]{1,0:T(8,128)S(1)}, f32[1024,128]{1,0:T(8,128)S(1)}) custom-call(bf16[1024,128]{1,0:T(8,128)(2,1)S(1)} %bitcast.62, bf16[2048,128]{1,0:T(8,128)(2,1)S(1)} %bitcast.66, bf16[2048,128]{1,0:T(8,128)(2,1)S(1)} %bitcast.65), custom_call_target="tpu_custom_call" | custom-call | flops 1610612736 | bytes 2883584 | tf_op jit(solution)/shard_map/pallas_call | solution.py:181
  102.6 4.0 %shard_map.131 = bf16[1024,128]{1,0:T(8,128)(2,1)S(1)} custom-call(bf16[1024,128]{1,0:T(8,128)(2,1)S(1)} %bitcast.63, bf16[2048,128]{1,0:T(8,128)(2,1)S(1)} %bitcast.61, bf16[2048,128]{1,0:T(8,128)(2,1)S(1)} %bitcast.60, s32[1024,1]{1,0:T(8,128)S(1)} %add.90.qpos_ref, f32[1024,128]{1,0:T(8,128)S(1)} %get-tuple-element.16.max_ref, ...), custom_call_target="tpu_custom_call" | custom-call | tf_op jit(solution)/shard_map/pallas_call | solution.py:204
  106.6 10.5 %all_to_all.26 = bf16[16,64,128]{2,1,0:T(8,128)(2,1)S(1)} all-to-all(bf16[16,64,128]{2,1,0:T(8,128)(2,1)S(1)} %bitcast.64), channel_id=1, replica_groups=mesh['dp'=2,'context'=16,'tensor'=4] {'context'}, dimensions={0} | all-to-all | bytes 524288 | tf_op jit(solution)/shard_map/all_to_all | solution.py:364
  117.3 0.8 copy.37
  (38 shorter events, 3.3 us)
Async XLA Ops:
  0.8 5.4 %collective-permute-start = (bf16[2,3,1024]{2,0,1:T(2,128)(2,1)S(1)}, bf16[2,3,1024]{2,0,1:T(2,128)(2,1)S(1)}, u32[]{:S(2)}, u32[]{:S(2)}) collective-permute-start(bf16[2,3,1024]{2,0,1:T(2,128)(2,1)S(1)} %slice.40), channel_id=1, source_target_pairs={{0,4},{4,8},{8,12},{12,16},{16,20},{20,24},{24,28},{28,32},{32,36}... | collective-permute-start | bytes 36872 | tf_op jit(solution)/shard_map/ppermute | solution.py:21
  6.2 0.6 copy-start.4
  30.3 9.5 %copy-start.1 = (bf16[128,1024]{1,0:T(8,128)(2,1)S(1)}, bf16[128,1024]{1,0:T(8,128)(2,1)}, u32[]{:S(2)}) copy-start(bf16[128,1024]{1,0:T(8,128)(2,1)} %param.24) | copy-start | bytes 786436
  35.1 4.9 %copy-start.2 = (bf16[128,1024]{1,0:T(8,128)(2,1)S(1)}, bf16[128,1024]{1,0:T(8,128)(2,1)}, u32[]{:S(2)}) copy-start(bf16[128,1024]{1,0:T(8,128)(2,1)} %param.25) | copy-start | bytes 786436
  35.1 17.6 %all-to-all-start.1 = ((bf16[4,128,1024]{2,1,0:T(8,128)(2,1)}), bf16[4,128,1024]{2,1,0:T(8,128)(2,1)S(1)}, u32[]{:S(2)}, u32[]{:S(2)}) async-start(bf16[4,128,1024]{2,1,0:T(8,128)(2,1)} %shard_map.128), calls=%async_computation.1 | async-start | bytes 2097152 | tf_op jit(solution)/shard_map/all_to_all | solution.py:324
  52.7 21.9 %all-to-all-start.3 = ((bf16[16,256,128]{2,1,0:T(8,128)(2,1)}), bf16[16,256,128]{2,1,0:T(8,128)(2,1)S(1)}, u32[]{:S(2)}, u32[]{:S(2)}) async-start(bf16[16,256,128]{2,1,0:T(8,128)(2,1)} %pad_maximum_fusion.1), calls=%async_computation.3 | async-start | bytes 2097152 | tf_op jit(solution)/shard_map/all_to_all | solution.py:274
  59.0 0.7 copy-start.3
  74.6 1.0 copy-start
  75.5 22.9 %all-to-all-start.2 = ((bf16[16,320,128]{2,1,0:T(8,128)(2,1)}), bf16[16,320,128]{2,1,0:T(8,128)(2,1)S(1)}, u32[]{:S(2)}, u32[]{:S(2)}) async-start(bf16[16,320,128]{2,1,0:T(8,128)(2,1)} %pad_maximum_fusion), calls=%async_computation.2 | async-start | bytes 2621440 | tf_op jit(solution)/shard_map/all_to_all | solution.py:347

commit v15 on v14

--- a/solution.py
+++ b/solution.py
@@ -197,7 +197,7 @@
     )(queries, keys, values)
 
 
-def attend_new(queries, keys, values, query_pos, pieces, spread, block=512):
+def attend_new(queries, keys, values, query_pos, pieces, spread, block=256):
     rows, width = queries.shape
     key_rows = keys.shape[0]
     row_spec = pl.BlockSpec((block, width), lambda i: (i, 0))

time: 119 us -> 119 us (level)
  no operation moved by 1% of the time
where the time goes in v15:
time: 119 us; the launch traced here: 118 us
  waiting for transfers between devices  30.7 us (26%)
  Pallas kernels  29.9 us (25%)
  blocking collectives  27 us (23%)
  starting transfers between devices  19.1 us (16%)
  local copies, waits for them, and re-layouts  6.7 us (6%)
  other arithmetic  4.22 us (4%)
    all_to_all x1, waiting for transfers between devices, shards(): lax.all_to_all(jnp.concatenate([query_parts, by_head(new_keys), by_head(n...  16.8 us
    all_to_all x1, blocking collectives, shards(): finals = lax.all_to_all(finals_out, 'context', 0, 0, tiled=True)  16.5 us
    pallas_call x2, Pallas kernels, channel_blocks(): pl.pallas_call(kernel, grid_spec=grid_spec, out_shape=outputs)  11.7 us
    all_to_all x1, waiting for transfers between devices, shards(): gathered = lax.all_to_all(hidden_out, 'tensor', 0, 0, tiled=True)  11 us
    all_to_all x1, blocking collectives, shards(): back = lax.all_to_all(mine, 'context', 0, 0, tiled=True)  10.5 us
    pallas_call x1, Pallas kernels, project(): pl.pallas_call(project_kernel, grid=(groups, width // block), in_specs=[p...  9.69 us
    all_to_all x1, starting transfers between devices, shards(): lax.all_to_all(jnp.concatenate([by_head(cache_keys), by_head(cache_values...  6.07 us
    ppermute x1, starting transfers between devices, shifted(): return lax.ppermute(x, axis, pairs)  4.58 us
  transfers between devices with their start and end apart: 4, of which 4 were waited for; matrix products, arithmetic and copies ran while one was open for 6% of the time, Pallas kernels for 8%

profile of v15, /device:TPU:1, one launch (start us, length us, event | category | flops | bytes accessed | tf_op | source)
XLA Modules:
  0.0 118.5 jit_solution(10603900553910979234)
XLA Ops:
  0.0 0.8 slice.40
  0.8 4.6 %collective-permute-start = (bf16[2,3,1024]{2,0,1:T(2,128)(2,1)S(1)}, bf16[2,3,1024]{2,0,1:T(2,128)(2,1)S(1)}, u32[]{:S(2)}, u32[]{:S(2)}) collective-permute-start(bf16[2,3,1024]{2,0,1:T(2,128)(2,1)S(1)} %slice.40), channel_id=1, source_target_pairs={{0,4},{4,8},{8,12},{12,16},{16,20},{20,24},{24,28},{28,32},{32,36}... | collective-permute-start | bytes 36872 | tf_op jit(solution)/shard_map/ppermute | solution.py:21
  5.4 0.8 collective-permute-done
  6.2 0.6 copy-done.4
  6.8 7.0 %shard_map.127 = (bf16[128,1024]{1,0:T(8,128)(2,1)}, f32[128,1024]{1,0:T(8,128)}, f32[128,1024]{1,0:T(8,128)}, bf16[16,16,1024]{2,1,0:T(8,128)(2,1)}) custom-call(s32[1]{0:T(128)} %bitcast.idx_ref, bf16[3,128,1024]{2,1,0:T(8,128)(2,1)} %bitcast.82, bf16[3,2,1024]{2,1,0:T(2,128)(2,1)} %bitcast.86, bf16[3,2,1024]{2,1,0:T(2,128)(2,1)} %bitcast.85, ...), custom_call_target="tpu_custom_call" | custom-call | tf_op jit(solution)/shard_map/pallas_call | solution.py:122
  13.8 16.5 %all_to_all.25.fin_ref = bf16[16,16,1024]{2,1,0:T(8,128)(2,1)} all-to-all(bf16[16,16,1024]{2,1,0:T(8,128)(2,1)} %get-tuple-element.13), channel_id=1, replica_groups=mesh['dp'=2,'context'=16,'tensor'=4] {'context'}, dimensions={0} | all-to-all | bytes 1048576 | tf_op jit(solution)/shard_map/all_to_all | solution.py:306
  30.3 4.7 %shard_map.128 = bf16[4,128,1024]{2,1,0:T(8,128)(2,1)} custom-call(s32[1]{0:T(128)} %bitcast.idx_ref, f32[128,1024]{1,0:T(8,128)} %get-tuple-element.12.local_ref, f32[16,1024]{1,0:T(8,128)} %rate_ref.3, f32[16,1024]{1,0:T(8,128)} %res_ref.3, bf16[16,16,1024]{2,1,0:T(8,128)(2,1)} %all_to_all.25.fin_ref, f32[16,1024]{1,0:T(8,128)} %hs_ref.1, ...), custom_call_target="tpu_custom_call" | custom-call | tf_op jit(solution)/shard_map/pallas_call | solution.py:122
  35.1 4.1 %all-to-all-start.1 = ((bf16[4,128,1024]{2,1,0:T(8,128)(2,1)}), bf16[4,128,1024]{2,1,0:T(8,128)(2,1)S(1)}, u32[]{:S(2)}, u32[]{:S(2)}) async-start(bf16[4,128,1024]{2,1,0:T(8,128)(2,1)} %shard_map.128), calls=%async_computation.1 | async-start | bytes 2097152 | tf_op jit(solution)/shard_map/all_to_all | solution.py:324
  40.3 1.1 pad_maximum_fusion.1
  41.7 11.0 %all-to-all-done.1 = bf16[4,128,1024]{2,1,0:T(8,128)(2,1)S(1)} async-done(((bf16[4,128,1024]{2,1,0:T(8,128)(2,1)}), bf16[4,128,1024]{2,1,0:T(8,128)(2,1)S(1)}, u32[]{:S(2)}, u32[]{:S(2)}) %all-to-all-start.1) | async-done | bytes 1048608 | tf_op jit(solution)/shard_map/all_to_all | solution.py:324
  52.7 6.1 %all-to-all-start.3 = ((bf16[16,256,128]{2,1,0:T(8,128)(2,1)}), bf16[16,256,128]{2,1,0:T(8,128)(2,1)S(1)}, u32[]{:S(2)}, u32[]{:S(2)}) async-start(bf16[16,256,128]{2,1,0:T(8,128)(2,1)} %pad_maximum_fusion.1), calls=%async_computation.3 | async-start | bytes 2097152 | tf_op jit(solution)/shard_map/all_to_all | solution.py:274
  60.0 9.7 %shard_map.129 = f32[3,128,1024]{2,1,0:T(8,128)S(1)} custom-call(bf16[128,4096]{1,0:T(8,128)(2,1)S(1)} %multiply_convert_fusion.x_ref, bf16[3,4096,1024]{2,1,0:T(8,128)(2,1)} %bitcast.67), custom_call_target="tpu_custom_call" | custom-call | flops 3221225472 | bytes 27787264 | tf_op jit(solution)/shard_map/pallas_call | solution.py:229
  70.1 0.5 subtract_convert_fusion.1
  71.4 1.2 pad_maximum_fusion
  72.5 2.0 %all-to-all-done.3 = bf16[16,256,128]{2,1,0:T(8,128)(2,1)S(1)} async-done(((bf16[16,256,128]{2,1,0:T(8,128)(2,1)}), bf16[16,256,128]{2,1,0:T(8,128)(2,1)S(1)}, u32[]{:S(2)}, u32[]{:S(2)}) %all-to-all-start.3) | async-done | bytes 1048608 | tf_op jit(solution)/shard_map/all_to_all | solution.py:274
  74.6 1.0 copy-done
  75.5 4.3 %all-to-all-start.2 = ((bf16[16,320,128]{2,1,0:T(8,128)(2,1)}), bf16[16,320,128]{2,1,0:T(8,128)(2,1)S(1)}, u32[]{:S(2)}, u32[]{:S(2)}) async-start(bf16[16,320,128]{2,1,0:T(8,128)(2,1)} %pad_maximum_fusion), calls=%async_computation.2 | async-start | bytes 2621440 | tf_op jit(solution)/shard_map/all_to_all | solution.py:347
  79.9 0.5 add.90.qpos_ref
  80.3 1.3 %fusion.3 = (bf16[16,128,128]{2,1,0:T(8,128)(2,1)S(1)}, bf16[16,128,128]{2,1,0:T(8,128)(2,1)S(1)}) fusion(bf16[16,256,128]{2,1,0:T(8,128)(2,1)} %copy-done), kind=kLoop, calls=%fused_computation.25 | loop fusion | bytes 2097152 | tf_op jit(solution)/shard_map/slice | solution.py:278
  81.6 16.8 %all-to-all-done.2 = bf16[16,320,128]{2,1,0:T(8,128)(2,1)S(1)} async-done(((bf16[16,320,128]{2,1,0:T(8,128)(2,1)}), bf16[16,320,128]{2,1,0:T(8,128)(2,1)S(1)}, u32[]{:S(2)}, u32[]{:S(2)}) %all-to-all-start.2) | async-done | bytes 1310752 | tf_op jit(solution)/shard_map/all_to_all | solution.py:347
  98.5 4.0 %shard_map.130 = (f32[1024,128]{1,0:T(8,128)S(1)}, f32[1024,128]{1,0:T(8,128)S(1)}, f32[1024,128]{1,0:T(8,128)S(1)}) custom-call(bf16[1024,128]{1,0:T(8,128)(2,1)S(1)} %bitcast.62, bf16[2048,128]{1,0:T(8,128)(2,1)S(1)} %bitcast.66, bf16[2048,128]{1,0:T(8,128)(2,1)S(1)} %bitcast.65), custom_call_target="tpu_custom_call" | custom-call | flops 1610612736 | bytes 2883584 | tf_op jit(solution)/shard_map/pallas_call | solution.py:181
  102.6 4.5 %shard_map.131 = bf16[1024,128]{1,0:T(8,128)(2,1)S(1)} custom-call(bf16[1024,128]{1,0:T(8,128)(2,1)S(1)} %bitcast.63, bf16[2048,128]{1,0:T(8,128)(2,1)S(1)} %bitcast.61, bf16[2048,128]{1,0:T(8,128)(2,1)S(1)} %bitcast.60, s32[1024,1]{1,0:T(8,128)S(1)} %add.90.qpos_ref, f32[1024,128]{1,0:T(8,128)S(1)} %get-tuple-element.16.max_ref, ...), custom_call_target="tpu_custom_call" | custom-call | tf_op jit(solution)/shard_map/pallas_call | solution.py:204
  107.1 10.5 %all_to_all.26 = bf16[16,64,128]{2,1,0:T(8,128)(2,1)S(1)} all-to-all(bf16[16,64,128]{2,1,0:T(8,128)(2,1)S(1)} %bitcast.64), channel_id=1, replica_groups=mesh['dp'=2,'context'=16,'tensor'=4] {'context'}, dimensions={0} | all-to-all | bytes 524288 | tf_op jit(solution)/shard_map/all_to_all | solution.py:364
  117.7 0.8 copy.37
  (38 shorter events, 3.3 us)
Async XLA Ops:
  0.8 5.4 %collective-permute-start = (bf16[2,3,1024]{2,0,1:T(2,128)(2,1)S(1)}, bf16[2,3,1024]{2,0,1:T(2,128)(2,1)S(1)}, u32[]{:S(2)}, u32[]{:S(2)}) collective-permute-start(bf16[2,3,1024]{2,0,1:T(2,128)(2,1)S(1)} %slice.40), channel_id=1, source_target_pairs={{0,4},{4,8},{8,12},{12,16},{16,20},{20,24},{24,28},{28,32},{32,36}... | collective-permute-start | bytes 36872 | tf_op jit(solution)/shard_map/ppermute | solution.py:21
  6.2 0.6 copy-start.4
  30.3 9.5 %copy-start.1 = (bf16[128,1024]{1,0:T(8,128)(2,1)S(1)}, bf16[128,1024]{1,0:T(8,128)(2,1)}, u32[]{:S(2)}) copy-start(bf16[128,1024]{1,0:T(8,128)(2,1)} %param.24) | copy-start | bytes 786436
  35.1 4.9 %copy-start.2 = (bf16[128,1024]{1,0:T(8,128)(2,1)S(1)}, bf16[128,1024]{1,0:T(8,128)(2,1)}, u32[]{:S(2)}) copy-start(bf16[128,1024]{1,0:T(8,128)(2,1)} %param.25) | copy-start | bytes 786436
  35.1 17.6 %all-to-all-start.1 = ((bf16[4,128,1024]{2,1,0:T(8,128)(2,1)}), bf16[4,128,1024]{2,1,0:T(8,128)(2,1)S(1)}, u32[]{:S(2)}, u32[]{:S(2)}) async-start(bf16[4,128,1024]{2,1,0:T(8,128)(2,1)} %shard_map.128), calls=%async_computation.1 | async-start | bytes 2097152 | tf_op jit(solution)/shard_map/all_to_all | solution.py:324
  52.7 21.9 %all-to-all-start.3 = ((bf16[16,256,128]{2,1,0:T(8,128)(2,1)}), bf16[16,256,128]{2,1,0:T(8,128)(2,1)S(1)}, u32[]{:S(2)}, u32[]{:S(2)}) async-start(bf16[16,256,128]{2,1,0:T(8,128)(2,1)} %pad_maximum_fusion.1), calls=%async_computation.3 | async-start | bytes 2097152 | tf_op jit(solution)/shard_map/all_to_all | solution.py:274
  59.0 0.7 copy-start.3
  74.6 1.0 copy-start
  75.5 22.9 %all-to-all-start.2 = ((bf16[16,320,128]{2,1,0:T(8,128)(2,1)}), bf16[16,320,128]{2,1,0:T(8,128)(2,1)S(1)}, u32[]{:S(2)}, u32[]{:S(2)}) async-start(bf16[16,320,128]{2,1,0:T(8,128)(2,1)} %pad_maximum_fusion), calls=%async_computation.2 | async-start | bytes 2621440 | tf_op jit(solution)/shard_map/all_to_all | solution.py:347

commit v16 on v14

--- a/solution.py
+++ b/solution.py
@@ -319,7 +319,7 @@
             skip_weight[None, :],
         ],
         [jax.ShapeDtypeStruct((ways, row_count, channels), jnp.bfloat16)],
-        block,
+        2 * block,
     )
     gathered = lax.all_to_all(hidden_out, "tensor", 0, 0, tiled=True)
     gathered = gathered.transpose(1, 0, 2).reshape(row_count, ways * channels)

time: 119 us -> 118 us (level)
  no operation moved by 1% of the time
where the time goes in v16:
time: 118 us
  waiting for transfers between devices  30.7 us (26%)
  Pallas kernels  28.9 us (24%)
  blocking collectives  27 us (23%)
  starting transfers between devices  19.1 us (16%)
  local copies, waits for them, and re-layouts  6.7 us (6%)
  other arithmetic  4.22 us (4%)
    all_to_all x1, waiting for transfers between devices, shards(): lax.all_to_all(jnp.concatenate([query_parts, by_head(new_keys), by_head(n...  16.8 us
    all_to_all x1, blocking collectives, shards(): finals = lax.all_to_all(finals_out, 'context', 0, 0, tiled=True)  16.5 us
    pallas_call x2, Pallas kernels, channel_blocks(): pl.pallas_call(kernel, grid_spec=grid_spec, out_shape=outputs)  11.2 us
    all_to_all x1, waiting for transfers between devices, shards(): gathered = lax.all_to_all(hidden_out, 'tensor', 0, 0, tiled=True)  11 us
    all_to_all x1, blocking collectives, shards(): back = lax.all_to_all(mine, 'context', 0, 0, tiled=True)  10.5 us
    pallas_call x1, Pallas kernels, project(): pl.pallas_call(project_kernel, grid=(groups, width // block), in_specs=[p...  9.69 us
    all_to_all x1, starting transfers between devices, shards(): lax.all_to_all(jnp.concatenate([by_head(cache_keys), by_head(cache_values...  6.07 us
    ppermute x1, starting transfers between devices, shifted(): return lax.ppermute(x, axis, pairs)  4.58 us
  transfers between devices with their start and end apart: 4, of which 4 were waited for; matrix products, arithmetic and copies ran while one was open for 6% of the time, Pallas kernels for 8%

profile of v16, /device:TPU:1, one launch (start us, length us, event | category | flops | bytes accessed | tf_op | source)
XLA Modules:
  0.0 117.5 jit_solution(4300247420260079965)
XLA Ops:
  0.0 0.8 slice.40
  0.8 4.6 %collective-permute-start = (bf16[2,3,1024]{2,0,1:T(2,128)(2,1)S(1)}, bf16[2,3,1024]{2,0,1:T(2,128)(2,1)S(1)}, u32[]{:S(2)}, u32[]{:S(2)}) collective-permute-start(bf16[2,3,1024]{2,0,1:T(2,128)(2,1)S(1)} %slice.40), channel_id=1, source_target_pairs={{0,4},{4,8},{8,12},{12,16},{16,20},{20,24},{24,28},{28,32},{32,36}... | collective-permute-start | bytes 36872 | tf_op jit(solution)/shard_map/ppermute | solution.py:21
  5.4 0.8 collective-permute-done
  6.2 0.6 copy-done.4
  6.8 7.0 %shard_map.127 = (bf16[128,1024]{1,0:T(8,128)(2,1)}, f32[128,1024]{1,0:T(8,128)}, f32[128,1024]{1,0:T(8,128)}, bf16[16,16,1024]{2,1,0:T(8,128)(2,1)}) custom-call(s32[1]{0:T(128)} %bitcast.idx_ref, bf16[3,128,1024]{2,1,0:T(8,128)(2,1)} %bitcast.82, bf16[3,2,1024]{2,1,0:T(2,128)(2,1)} %bitcast.86, bf16[3,2,1024]{2,1,0:T(2,128)(2,1)} %bitcast.85, ...), custom_call_target="tpu_custom_call" | custom-call | tf_op jit(solution)/shard_map/pallas_call | solution.py:122
  13.8 16.5 %all_to_all.25.fin_ref = bf16[16,16,1024]{2,1,0:T(8,128)(2,1)} all-to-all(bf16[16,16,1024]{2,1,0:T(8,128)(2,1)} %get-tuple-element.13), channel_id=1, replica_groups=mesh['dp'=2,'context'=16,'tensor'=4] {'context'}, dimensions={0} | all-to-all | bytes 1048576 | tf_op jit(solution)/shard_map/all_to_all | solution.py:306
  30.3 4.2 %shard_map.128 = bf16[4,128,1024]{2,1,0:T(8,128)(2,1)} custom-call(s32[1]{0:T(128)} %bitcast.idx_ref, f32[128,1024]{1,0:T(8,128)} %get-tuple-element.12.local_ref, f32[16,1024]{1,0:T(8,128)} %rate_ref.3, f32[16,1024]{1,0:T(8,128)} %res_ref.3, bf16[16,16,1024]{2,1,0:T(8,128)(2,1)} %all_to_all.25.fin_ref, f32[16,1024]{1,0:T(8,128)} %hs_ref.1, ...), custom_call_target="tpu_custom_call" | custom-call | tf_op jit(solution)/shard_map/pallas_call | solution.py:122
  34.5 4.1 %all-to-all-start.1 = ((bf16[4,128,1024]{2,1,0:T(8,128)(2,1)}), bf16[4,128,1024]{2,1,0:T(8,128)(2,1)S(1)}, u32[]{:S(2)}, u32[]{:S(2)}) async-start(bf16[4,128,1024]{2,1,0:T(8,128)(2,1)} %shard_map.128), calls=%async_computation.1 | async-start | bytes 2097152 | tf_op jit(solution)/shard_map/all_to_all | solution.py:324
  39.8 1.1 pad_maximum_fusion.1
  41.2 11.0 %all-to-all-done.1 = bf16[4,128,1024]{2,1,0:T(8,128)(2,1)S(1)} async-done(((bf16[4,128,1024]{2,1,0:T(8,128)(2,1)}), bf16[4,128,1024]{2,1,0:T(8,128)(2,1)S(1)}, u32[]{:S(2)}, u32[]{:S(2)}) %all-to-all-start.1) | async-done | bytes 1048608 | tf_op jit(solution)/shard_map/all_to_all | solution.py:324
  52.2 6.1 %all-to-all-start.3 = ((bf16[16,256,128]{2,1,0:T(8,128)(2,1)}), bf16[16,256,128]{2,1,0:T(8,128)(2,1)S(1)}, u32[]{:S(2)}, u32[]{:S(2)}) async-start(bf16[16,256,128]{2,1,0:T(8,128)(2,1)} %pad_maximum_fusion.1), calls=%async_computation.3 | async-start | bytes 2097152 | tf_op jit(solution)/shard_map/all_to_all | solution.py:274
  59.5 9.7 %shard_map.129 = f32[3,128,1024]{2,1,0:T(8,128)S(1)} custom-call(bf16[128,4096]{1,0:T(8,128)(2,1)S(1)} %multiply_convert_fusion.x_ref, bf16[3,4096,1024]{2,1,0:T(8,128)(2,1)} %bitcast.67), custom_call_target="tpu_custom_call" | custom-call | flops 3221225472 | bytes 27787264 | tf_op jit(solution)/shard_map/pallas_call | solution.py:229
  69.6 0.5 subtract_convert_fusion.1
  70.8 1.2 pad_maximum_fusion
  72.0 2.0 %all-to-all-done.3 = bf16[16,256,128]{2,1,0:T(8,128)(2,1)S(1)} async-done(((bf16[16,256,128]{2,1,0:T(8,128)(2,1)}), bf16[16,256,128]{2,1,0:T(8,128)(2,1)S(1)}, u32[]{:S(2)}, u32[]{:S(2)}) %all-to-all-start.3) | async-done | bytes 1048608 | tf_op jit(solution)/shard_map/all_to_all | solution.py:274
  74.0 1.0 copy-done
  75.0 4.3 %all-to-all-start.2 = ((bf16[16,320,128]{2,1,0:T(8,128)(2,1)}), bf16[16,320,128]{2,1,0:T(8,128)(2,1)S(1)}, u32[]{:S(2)}, u32[]{:S(2)}) async-start(bf16[16,320,128]{2,1,0:T(8,128)(2,1)} %pad_maximum_fusion), calls=%async_computation.2 | async-start | bytes 2621440 | tf_op jit(solution)/shard_map/all_to_all | solution.py:347
  79.4 0.5 add.90.qpos_ref
  79.8 1.3 %fusion.3 = (bf16[16,128,128]{2,1,0:T(8,128)(2,1)S(1)}, bf16[16,128,128]{2,1,0:T(8,128)(2,1)S(1)}) fusion(bf16[16,256,128]{2,1,0:T(8,128)(2,1)} %copy-done), kind=kLoop, calls=%fused_computation.25 | loop fusion | bytes 2097152 | tf_op jit(solution)/shard_map/slice | solution.py:278
  81.1 16.8 %all-to-all-done.2 = bf16[16,320,128]{2,1,0:T(8,128)(2,1)S(1)} async-done(((bf16[16,320,128]{2,1,0:T(8,128)(2,1)}), bf16[16,320,128]{2,1,0:T(8,128)(2,1)S(1)}, u32[]{:S(2)}, u32[]{:S(2)}) %all-to-all-start.2) | async-done | bytes 1310752 | tf_op jit(solution)/shard_map/all_to_all | solution.py:347
  98.0 4.0 %shard_map.130 = (f32[1024,128]{1,0:T(8,128)S(1)}, f32[1024,128]{1,0:T(8,128)S(1)}, f32[1024,128]{1,0:T(8,128)S(1)}) custom-call(bf16[1024,128]{1,0:T(8,128)(2,1)S(1)} %bitcast.62, bf16[2048,128]{1,0:T(8,128)(2,1)S(1)} %bitcast.66, bf16[2048,128]{1,0:T(8,128)(2,1)S(1)} %bitcast.65), custom_call_target="tpu_custom_call" | custom-call | flops 1610612736 | bytes 2883584 | tf_op jit(solution)/shard_map/pallas_call | solution.py:181
  102.1 4.0 %shard_map.131 = bf16[1024,128]{1,0:T(8,128)(2,1)S(1)} custom-call(bf16[1024,128]{1,0:T(8,128)(2,1)S(1)} %bitcast.63, bf16[2048,128]{1,0:T(8,128)(2,1)S(1)} %bitcast.61, bf16[2048,128]{1,0:T(8,128)(2,1)S(1)} %bitcast.60, s32[1024,1]{1,0:T(8,128)S(1)} %add.90.qpos_ref, f32[1024,128]{1,0:T(8,128)S(1)} %get-tuple-element.16.max_ref, ...), custom_call_target="tpu_custom_call" | custom-call | tf_op jit(solution)/shard_map/pallas_call | solution.py:204
  106.1 10.5 %all_to_all.26 = bf16[16,64,128]{2,1,0:T(8,128)(2,1)S(1)} all-to-all(bf16[16,64,128]{2,1,0:T(8,128)(2,1)S(1)} %bitcast.64), channel_id=1, replica_groups=mesh['dp'=2,'context'=16,'tensor'=4] {'context'}, dimensions={0} | all-to-all | bytes 524288 | tf_op jit(solution)/shard_map/all_to_all | solution.py:364
  116.8 0.8 copy.37
  (38 shorter events, 3.3 us)
Async XLA Ops:
  0.8 5.4 %collective-permute-start = (bf16[2,3,1024]{2,0,1:T(2,128)(2,1)S(1)}, bf16[2,3,1024]{2,0,1:T(2,128)(2,1)S(1)}, u32[]{:S(2)}, u32[]{:S(2)}) collective-permute-start(bf16[2,3,1024]{2,0,1:T(2,128)(2,1)S(1)} %slice.40), channel_id=1, source_target_pairs={{0,4},{4,8},{8,12},{12,16},{16,20},{20,24},{24,28},{28,32},{32,36}... | collective-permute-start | bytes 36872 | tf_op jit(solution)/shard_map/ppermute | solution.py:21
  6.2 0.6 copy-start.4
  30.3 9.0 %copy-start.1 = (bf16[128,1024]{1,0:T(8,128)(2,1)S(1)}, bf16[128,1024]{1,0:T(8,128)(2,1)}, u32[]{:S(2)}) copy-start(bf16[128,1024]{1,0:T(8,128)(2,1)} %param.24) | copy-start | bytes 786436
  34.5 4.9 %copy-start.2 = (bf16[128,1024]{1,0:T(8,128)(2,1)S(1)}, bf16[128,1024]{1,0:T(8,128)(2,1)}, u32[]{:S(2)}) copy-start(bf16[128,1024]{1,0:T(8,128)(2,1)} %param.25) | copy-start | bytes 786436
  34.5 17.6 %all-to-all-start.1 = ((bf16[4,128,1024]{2,1,0:T(8,128)(2,1)}), bf16[4,128,1024]{2,1,0:T(8,128)(2,1)S(1)}, u32[]{:S(2)}, u32[]{:S(2)}) async-start(bf16[4,128,1024]{2,1,0:T(8,128)(2,1)} %shard_map.128), calls=%async_computation.1 | async-start | bytes 2097152 | tf_op jit(solution)/shard_map/all_to_all | solution.py:324
  52.2 21.9 %all-to-all-start.3 = ((bf16[16,256,128]{2,1,0:T(8,128)(2,1)}), bf16[16,256,128]{2,1,0:T(8,128)(2,1)S(1)}, u32[]{:S(2)}, u32[]{:S(2)}) async-start(bf16[16,256,128]{2,1,0:T(8,128)(2,1)} %pad_maximum_fusion.1), calls=%async_computation.3 | async-start | bytes 2097152 | tf_op jit(solution)/shard_map/all_to_all | solution.py:274
  58.5 0.7 copy-start.3
  74.0 1.0 copy-start
  75.0 22.9 %all-to-all-start.2 = ((bf16[16,320,128]{2,1,0:T(8,128)(2,1)}), bf16[16,320,128]{2,1,0:T(8,128)(2,1)S(1)}, u32[]{:S(2)}, u32[]{:S(2)}) async-start(bf16[16,320,128]{2,1,0:T(8,128)(2,1)} %pad_maximum_fusion), calls=%async_computation.2 | async-start | bytes 2621440 | tf_op jit(solution)/shard_map/all_to_all | solution.py:347

commit v17 on v16

--- a/solution.py
+++ b/solution.py
@@ -173,7 +173,7 @@
             block_with(keys)
 
 
-def attend_cache(queries, keys, values, block=512):
+def attend_cache(queries, keys, values, block=1024):
     rows, width = queries.shape
     key_rows = keys.shape[0]
     piece = jax.ShapeDtypeStruct((rows, width), jnp.float32)

time: 118 us -> 118 us (level)
  no operation moved by 1% of the time
where the time goes in v17:
time: 118 us; the launch traced here: 117 us
  waiting for transfers between devices  30.7 us (26%)
  Pallas kernels  28.6 us (24%)
  blocking collectives  27 us (23%)
  starting transfers between devices  19.1 us (16%)
  local copies, waits for them, and re-layouts  6.7 us (6%)
  other arithmetic  4.22 us (4%)
    all_to_all x1, waiting for transfers between devices, shards(): lax.all_to_all(jnp.concatenate([query_parts, by_head(new_keys), by_head(n...  16.8 us
    all_to_all x1, blocking collectives, shards(): finals = lax.all_to_all(finals_out, 'context', 0, 0, tiled=True)  16.5 us
    pallas_call x2, Pallas kernels, channel_blocks(): pl.pallas_call(kernel, grid_spec=grid_spec, out_shape=outputs)  11.2 us
    all_to_all x1, waiting for transfers between devices, shards(): gathered = lax.all_to_all(hidden_out, 'tensor', 0, 0, tiled=True)  11 us
    all_to_all x1, blocking collectives, shards(): back = lax.all_to_all(mine, 'context', 0, 0, tiled=True)  10.5 us
    pallas_call x1, Pallas kernels, project(): pl.pallas_call(project_kernel, grid=(groups, width // block), in_specs=[p...  9.69 us
    all_to_all x1, starting transfers between devices, shards(): lax.all_to_all(jnp.concatenate([by_head(cache_keys), by_head(cache_values...  6.07 us
    ppermute x1, starting transfers between devices, shifted(): return lax.ppermute(x, axis, pairs)  4.58 us
  transfers between devices with their start and end apart: 4, of which 4 were waited for; matrix products, arithmetic and copies ran while one was open for 6% of the time, Pallas kernels for 8%

profile of v17, /device:TPU:1, one launch (start us, length us, event | category | flops | bytes accessed | tf_op | source)
XLA Modules:
  0.0 117.2 jit_solution(6736698633585779405)
XLA Ops:
  0.0 0.8 slice.40
  0.8 4.6 %collective-permute-start = (bf16[2,3,1024]{2,0,1:T(2,128)(2,1)S(1)}, bf16[2,3,1024]{2,0,1:T(2,128)(2,1)S(1)}, u32[]{:S(2)}, u32[]{:S(2)}) collective-permute-start(bf16[2,3,1024]{2,0,1:T(2,128)(2,1)S(1)} %slice.40), channel_id=1, source_target_pairs={{0,4},{4,8},{8,12},{12,16},{16,20},{20,24},{24,28},{28,32},{32,36}... | collective-permute-start | bytes 36872 | tf_op jit(solution)/shard_map/ppermute | solution.py:21
  5.4 0.8 collective-permute-done
  6.2 0.6 copy-done.4
  6.8 7.0 %shard_map.127 = (bf16[128,1024]{1,0:T(8,128)(2,1)}, f32[128,1024]{1,0:T(8,128)}, f32[128,1024]{1,0:T(8,128)}, bf16[16,16,1024]{2,1,0:T(8,128)(2,1)}) custom-call(s32[1]{0:T(128)} %bitcast.idx_ref, bf16[3,128,1024]{2,1,0:T(8,128)(2,1)} %bitcast.82, bf16[3,2,1024]{2,1,0:T(2,128)(2,1)} %bitcast.86, bf16[3,2,1024]{2,1,0:T(2,128)(2,1)} %bitcast.85, ...), custom_call_target="tpu_custom_call" | custom-call | tf_op jit(solution)/shard_map/pallas_call | solution.py:122
  13.8 16.5 %all_to_all.25.fin_ref = bf16[16,16,1024]{2,1,0:T(8,128)(2,1)} all-to-all(bf16[16,16,1024]{2,1,0:T(8,128)(2,1)} %get-tuple-element.13), channel_id=1, replica_groups=mesh['dp'=2,'context'=16,'tensor'=4] {'context'}, dimensions={0} | all-to-all | bytes 1048576 | tf_op jit(solution)/shard_map/all_to_all | solution.py:306
  30.3 4.2 %shard_map.128 = bf16[4,128,1024]{2,1,0:T(8,128)(2,1)} custom-call(s32[1]{0:T(128)} %bitcast.idx_ref, f32[128,1024]{1,0:T(8,128)} %get-tuple-element.12.local_ref, f32[16,1024]{1,0:T(8,128)} %rate_ref.3, f32[16,1024]{1,0:T(8,128)} %res_ref.3, bf16[16,16,1024]{2,1,0:T(8,128)(2,1)} %all_to_all.25.fin_ref, f32[16,1024]{1,0:T(8,128)} %hs_ref.1, ...), custom_call_target="tpu_custom_call" | custom-call | tf_op jit(solution)/shard_map/pallas_call | solution.py:122
  34.5 4.1 %all-to-all-start.1 = ((bf16[4,128,1024]{2,1,0:T(8,128)(2,1)}), bf16[4,128,1024]{2,1,0:T(8,128)(2,1)S(1)}, u32[]{:S(2)}, u32[]{:S(2)}) async-start(bf16[4,128,1024]{2,1,0:T(8,128)(2,1)} %shard_map.128), calls=%async_computation.1 | async-start | bytes 2097152 | tf_op jit(solution)/shard_map/all_to_all | solution.py:324
  39.8 1.1 pad_maximum_fusion.1
  41.2 11.0 %all-to-all-done.1 = bf16[4,128,1024]{2,1,0:T(8,128)(2,1)S(1)} async-done(((bf16[4,128,1024]{2,1,0:T(8,128)(2,1)}), bf16[4,128,1024]{2,1,0:T(8,128)(2,1)S(1)}, u32[]{:S(2)}, u32[]{:S(2)}) %all-to-all-start.1) | async-done | bytes 1048608 | tf_op jit(solution)/shard_map/all_to_all | solution.py:324
  52.2 6.1 %all-to-all-start.3 = ((bf16[16,256,128]{2,1,0:T(8,128)(2,1)}), bf16[16,256,128]{2,1,0:T(8,128)(2,1)S(1)}, u32[]{:S(2)}, u32[]{:S(2)}) async-start(bf16[16,256,128]{2,1,0:T(8,128)(2,1)} %pad_maximum_fusion.1), calls=%async_computation.3 | async-start | bytes 2097152 | tf_op jit(solution)/shard_map/all_to_all | solution.py:274
  59.5 9.7 %shard_map.129 = f32[3,128,1024]{2,1,0:T(8,128)S(1)} custom-call(bf16[128,4096]{1,0:T(8,128)(2,1)S(1)} %multiply_convert_fusion.x_ref, bf16[3,4096,1024]{2,1,0:T(8,128)(2,1)} %bitcast.67), custom_call_target="tpu_custom_call" | custom-call | flops 3221225472 | bytes 27787264 | tf_op jit(solution)/shard_map/pallas_call | solution.py:229
  69.6 0.5 subtract_convert_fusion.1
  70.8 1.2 pad_maximum_fusion
  72.0 2.0 %all-to-all-done.3 = bf16[16,256,128]{2,1,0:T(8,128)(2,1)S(1)} async-done(((bf16[16,256,128]{2,1,0:T(8,128)(2,1)}), bf16[16,256,128]{2,1,0:T(8,128)(2,1)S(1)}, u32[]{:S(2)}, u32[]{:S(2)}) %all-to-all-start.3) | async-done | bytes 1048608 | tf_op jit(solution)/shard_map/all_to_all | solution.py:274
  74.0 1.0 copy-done
  75.0 4.3 %all-to-all-start.2 = ((bf16[16,320,128]{2,1,0:T(8,128)(2,1)}), bf16[16,320,128]{2,1,0:T(8,128)(2,1)S(1)}, u32[]{:S(2)}, u32[]{:S(2)}) async-start(bf16[16,320,128]{2,1,0:T(8,128)(2,1)} %pad_maximum_fusion), calls=%async_computation.2 | async-start | bytes 2621440 | tf_op jit(solution)/shard_map/all_to_all | solution.py:347
  79.4 0.5 add.90.qpos_ref
  79.8 1.3 %fusion.3 = (bf16[16,128,128]{2,1,0:T(8,128)(2,1)S(1)}, bf16[16,128,128]{2,1,0:T(8,128)(2,1)S(1)}) fusion(bf16[16,256,128]{2,1,0:T(8,128)(2,1)} %copy-done), kind=kLoop, calls=%fused_computation.25 | loop fusion | bytes 2097152 | tf_op jit(solution)/shard_map/slice | solution.py:278
  81.1 16.8 %all-to-all-done.2 = bf16[16,320,128]{2,1,0:T(8,128)(2,1)S(1)} async-done(((bf16[16,320,128]{2,1,0:T(8,128)(2,1)}), bf16[16,320,128]{2,1,0:T(8,128)(2,1)S(1)}, u32[]{:S(2)}, u32[]{:S(2)}) %all-to-all-start.2) | async-done | bytes 1310752 | tf_op jit(solution)/shard_map/all_to_all | solution.py:347
  98.0 3.7 %shard_map.130 = (f32[1024,128]{1,0:T(8,128)S(1)}, f32[1024,128]{1,0:T(8,128)S(1)}, f32[1024,128]{1,0:T(8,128)S(1)}) custom-call(bf16[1024,128]{1,0:T(8,128)(2,1)S(1)} %bitcast.62, bf16[2048,128]{1,0:T(8,128)(2,1)S(1)} %bitcast.66, bf16[2048,128]{1,0:T(8,128)(2,1)S(1)} %bitcast.65), custom_call_target="tpu_custom_call" | custom-call | flops 1610612736 | bytes 2883584 | tf_op jit(solution)/shard_map/pallas_call | solution.py:181
  101.8 4.0 %shard_map.131 = bf16[1024,128]{1,0:T(8,128)(2,1)S(1)} custom-call(bf16[1024,128]{1,0:T(8,128)(2,1)S(1)} %bitcast.63, bf16[2048,128]{1,0:T(8,128)(2,1)S(1)} %bitcast.61, bf16[2048,128]{1,0:T(8,128)(2,1)S(1)} %bitcast.60, s32[1024,1]{1,0:T(8,128)S(1)} %add.90.qpos_ref, f32[1024,128]{1,0:T(8,128)S(1)} %get-tuple-element.16.max_ref, ...), custom_call_target="tpu_custom_call" | custom-call | tf_op jit(solution)/shard_map/pallas_call | solution.py:204
  105.8 10.5 %all_to_all.26 = bf16[16,64,128]{2,1,0:T(8,128)(2,1)S(1)} all-to-all(bf16[16,64,128]{2,1,0:T(8,128)(2,1)S(1)} %bitcast.64), channel_id=1, replica_groups=mesh['dp'=2,'context'=16,'tensor'=4] {'context'}, dimensions={0} | all-to-all | bytes 524288 | tf_op jit(solution)/shard_map/all_to_all | solution.py:364
  116.4 0.8 copy.37
  (38 shorter events, 3.4 us)
Async XLA Ops:
  0.8 5.4 %collective-permute-start = (bf16[2,3,1024]{2,0,1:T(2,128)(2,1)S(1)}, bf16[2,3,1024]{2,0,1:T(2,128)(2,1)S(1)}, u32[]{:S(2)}, u32[]{:S(2)}) collective-permute-start(bf16[2,3,1024]{2,0,1:T(2,128)(2,1)S(1)} %slice.40), channel_id=1, source_target_pairs={{0,4},{4,8},{8,12},{12,16},{16,20},{20,24},{24,28},{28,32},{32,36}... | collective-permute-start | bytes 36872 | tf_op jit(solution)/shard_map/ppermute | solution.py:21
  6.2 0.6 copy-start.4
  30.3 9.0 %copy-start.1 = (bf16[128,1024]{1,0:T(8,128)(2,1)S(1)}, bf16[128,1024]{1,0:T(8,128)(2,1)}, u32[]{:S(2)}) copy-start(bf16[128,1024]{1,0:T(8,128)(2,1)} %param.24) | copy-start | bytes 786436
  34.5 4.9 %copy-start.2 = (bf16[128,1024]{1,0:T(8,128)(2,1)S(1)}, bf16[128,1024]{1,0:T(8,128)(2,1)}, u32[]{:S(2)}) copy-start(bf16[128,1024]{1,0:T(8,128)(2,1)} %param.25) | copy-start | bytes 786436
  34.5 17.6 %all-to-all-start.1 = ((bf16[4,128,1024]{2,1,0:T(8,128)(2,1)}), bf16[4,128,1024]{2,1,0:T(8,128)(2,1)S(1)}, u32[]{:S(2)}, u32[]{:S(2)}) async-start(bf16[4,128,1024]{2,1,0:T(8,128)(2,1)} %shard_map.128), calls=%async_computation.1 | async-start | bytes 2097152 | tf_op jit(solution)/shard_map/all_to_all | solution.py:324
  52.2 21.9 %all-to-all-start.3 = ((bf16[16,256,128]{2,1,0:T(8,128)(2,1)}), bf16[16,256,128]{2,1,0:T(8,128)(2,1)S(1)}, u32[]{:S(2)}, u32[]{:S(2)}) async-start(bf16[16,256,128]{2,1,0:T(8,128)(2,1)} %pad_maximum_fusion.1), calls=%async_computation.3 | async-start | bytes 2097152 | tf_op jit(solution)/shard_map/all_to_all | solution.py:274
  58.5 0.7 copy-start.3
  74.0 1.0 copy-start
  75.0 22.9 %all-to-all-start.2 = ((bf16[16,320,128]{2,1,0:T(8,128)(2,1)}), bf16[16,320,128]{2,1,0:T(8,128)(2,1)S(1)}, u32[]{:S(2)}, u32[]{:S(2)}) async-start(bf16[16,320,128]{2,1,0:T(8,128)(2,1)} %pad_maximum_fusion), calls=%async_computation.2 | async-start | bytes 2621440 | tf_op jit(solution)/shard_map/all_to_all | solution.py:347

commit v18 on v17

--- a/solution.py
+++ b/solution.py
@@ -319,7 +319,7 @@
             skip_weight[None, :],
         ],
         [jax.ShapeDtypeStruct((ways, row_count, channels), jnp.bfloat16)],
-        2 * block,
+        4 * block,
     )
     gathered = lax.all_to_all(hidden_out, "tensor", 0, 0, tiled=True)
     gathered = gathered.transpose(1, 0, 2).reshape(row_count, ways * channels)

time: 118 us -> 118 us (level)
  no operation moved by 1% of the time
where the time goes in v18:
time: 118 us
  waiting for transfers between devices  30.7 us (26%)
  Pallas kernels  29 us (25%)
  blocking collectives  27 us (23%)
  starting transfers between devices  19.1 us (16%)
  local copies, waits for them, and re-layouts  6.7 us (6%)
  other arithmetic  4.22 us (4%)
    all_to_all x1, waiting for transfers between devices, shards(): lax.all_to_all(jnp.concatenate([query_parts, by_head(new_keys), by_head(n...  16.8 us
    all_to_all x1, blocking collectives, shards(): finals = lax.all_to_all(finals_out, 'context', 0, 0, tiled=True)  16.5 us
    pallas_call x2, Pallas kernels, channel_blocks(): pl.pallas_call(kernel, grid_spec=grid_spec, out_shape=outputs)  11.6 us
    all_to_all x1, waiting for transfers between devices, shards(): gathered = lax.all_to_all(hidden_out, 'tensor', 0, 0, tiled=True)  11 us
    all_to_all x1, blocking collectives, shards(): back = lax.all_to_all(mine, 'context', 0, 0, tiled=True)  10.5 us
    pallas_call x1, Pallas kernels, project(): pl.pallas_call(project_kernel, grid=(groups, width // block), in_specs=[p...  9.69 us
    all_to_all x1, starting transfers between devices, shards(): lax.all_to_all(jnp.concatenate([by_head(cache_keys), by_head(cache_values...  6.07 us
    ppermute x1, starting transfers between devices, shifted(): return lax.ppermute(x, axis, pairs)  4.58 us
  transfers between devices with their start and end apart: 4, of which 4 were waited for; matrix products, arithmetic and copies ran while one was open for 6% of the time, Pallas kernels for 8%

profile of v18, /device:TPU:1, one launch (start us, length us, event | category | flops | bytes accessed | tf_op | source)
XLA Modules:
  0.0 117.6 jit_solution(2514797014971250943)
XLA Ops:
  0.0 0.8 slice.40
  0.8 4.6 %collective-permute-start = (bf16[2,3,1024]{2,0,1:T(2,128)(2,1)S(1)}, bf16[2,3,1024]{2,0,1:T(2,128)(2,1)S(1)}, u32[]{:S(2)}, u32[]{:S(2)}) collective-permute-start(bf16[2,3,1024]{2,0,1:T(2,128)(2,1)S(1)} %slice.40), channel_id=1, source_target_pairs={{0,4},{4,8},{8,12},{12,16},{16,20},{20,24},{24,28},{28,32},{32,36}... | collective-permute-start | bytes 36872 | tf_op jit(solution)/shard_map/ppermute | solution.py:21
  5.4 0.8 collective-permute-done
  6.2 0.6 copy-done.4
  6.8 7.0 %shard_map.127 = (bf16[128,1024]{1,0:T(8,128)(2,1)}, f32[128,1024]{1,0:T(8,128)}, f32[128,1024]{1,0:T(8,128)}, bf16[16,16,1024]{2,1,0:T(8,128)(2,1)}) custom-call(s32[1]{0:T(128)} %bitcast.idx_ref, bf16[3,128,1024]{2,1,0:T(8,128)(2,1)} %bitcast.82, bf16[3,2,1024]{2,1,0:T(2,128)(2,1)} %bitcast.86, bf16[3,2,1024]{2,1,0:T(2,128)(2,1)} %bitcast.85, ...), custom_call_target="tpu_custom_call" | custom-call | tf_op jit(solution)/shard_map/pallas_call | solution.py:122
  13.8 16.5 %all_to_all.25.fin_ref = bf16[16,16,1024]{2,1,0:T(8,128)(2,1)} all-to-all(bf16[16,16,1024]{2,1,0:T(8,128)(2,1)} %get-tuple-element.13), channel_id=1, replica_groups=mesh['dp'=2,'context'=16,'tensor'=4] {'context'}, dimensions={0} | all-to-all | bytes 1048576 | tf_op jit(solution)/shard_map/all_to_all | solution.py:306
  30.3 4.6 %shard_map.128 = bf16[4,128,1024]{2,1,0:T(8,128)(2,1)} custom-call(s32[1]{0:T(128)} %bitcast.idx_ref, f32[128,1024]{1,0:T(8,128)} %get-tuple-element.12.local_ref, f32[16,1024]{1,0:T(8,128)} %rate_ref.3, f32[16,1024]{1,0:T(8,128)} %res_ref.3, bf16[16,16,1024]{2,1,0:T(8,128)(2,1)} %all_to_all.25.fin_ref, f32[16,1024]{1,0:T(8,128)} %hs_ref.1, ...), custom_call_target="tpu_custom_call" | custom-call | tf_op jit(solution)/shard_map/pallas_call | solution.py:122
  34.9 4.1 %all-to-all-start.1 = ((bf16[4,128,1024]{2,1,0:T(8,128)(2,1)}), bf16[4,128,1024]{2,1,0:T(8,128)(2,1)S(1)}, u32[]{:S(2)}, u32[]{:S(2)}) async-start(bf16[4,128,1024]{2,1,0:T(8,128)(2,1)} %shard_map.128), calls=%async_computation.1 | async-start | bytes 2097152 | tf_op jit(solution)/shard_map/all_to_all | solution.py:324
  40.1 1.1 pad_maximum_fusion.1
  41.5 11.0 %all-to-all-done.1 = bf16[4,128,1024]{2,1,0:T(8,128)(2,1)S(1)} async-done(((bf16[4,128,1024]{2,1,0:T(8,128)(2,1)}), bf16[4,128,1024]{2,1,0:T(8,128)(2,1)S(1)}, u32[]{:S(2)}, u32[]{:S(2)}) %all-to-all-start.1) | async-done | bytes 1048608 | tf_op jit(solution)/shard_map/all_to_all | solution.py:324
  52.5 6.1 %all-to-all-start.3 = ((bf16[16,256,128]{2,1,0:T(8,128)(2,1)}), bf16[16,256,128]{2,1,0:T(8,128)(2,1)S(1)}, u32[]{:S(2)}, u32[]{:S(2)}) async-start(bf16[16,256,128]{2,1,0:T(8,128)(2,1)} %pad_maximum_fusion.1), calls=%async_computation.3 | async-start | bytes 2097152 | tf_op jit(solution)/shard_map/all_to_all | solution.py:274
  59.9 9.7 %shard_map.129 = f32[3,128,1024]{2,1,0:T(8,128)S(1)} custom-call(bf16[128,4096]{1,0:T(8,128)(2,1)S(1)} %multiply_convert_fusion.x_ref, bf16[3,4096,1024]{2,1,0:T(8,128)(2,1)} %bitcast.67), custom_call_target="tpu_custom_call" | custom-call | flops 3221225472 | bytes 27787264 | tf_op jit(solution)/shard_map/pallas_call | solution.py:229
  70.0 0.5 subtract_convert_fusion.1
  71.2 1.2 pad_maximum_fusion
  72.4 2.0 %all-to-all-done.3 = bf16[16,256,128]{2,1,0:T(8,128)(2,1)S(1)} async-done(((bf16[16,256,128]{2,1,0:T(8,128)(2,1)}), bf16[16,256,128]{2,1,0:T(8,128)(2,1)S(1)}, u32[]{:S(2)}, u32[]{:S(2)}) %all-to-all-start.3) | async-done | bytes 1048608 | tf_op jit(solution)/shard_map/all_to_all | solution.py:274
  74.4 1.0 copy-done
  75.4 4.3 %all-to-all-start.2 = ((bf16[16,320,128]{2,1,0:T(8,128)(2,1)}), bf16[16,320,128]{2,1,0:T(8,128)(2,1)S(1)}, u32[]{:S(2)}, u32[]{:S(2)}) async-start(bf16[16,320,128]{2,1,0:T(8,128)(2,1)} %pad_maximum_fusion), calls=%async_computation.2 | async-start | bytes 2621440 | tf_op jit(solution)/shard_map/all_to_all | solution.py:347
  79.7 0.5 add.90.qpos_ref
  80.2 1.3 %fusion.3 = (bf16[16,128,128]{2,1,0:T(8,128)(2,1)S(1)}, bf16[16,128,128]{2,1,0:T(8,128)(2,1)S(1)}) fusion(bf16[16,256,128]{2,1,0:T(8,128)(2,1)} %copy-done), kind=kLoop, calls=%fused_computation.25 | loop fusion | bytes 2097152 | tf_op jit(solution)/shard_map/slice | solution.py:278
  81.5 16.8 %all-to-all-done.2 = bf16[16,320,128]{2,1,0:T(8,128)(2,1)S(1)} async-done(((bf16[16,320,128]{2,1,0:T(8,128)(2,1)}), bf16[16,320,128]{2,1,0:T(8,128)(2,1)S(1)}, u32[]{:S(2)}, u32[]{:S(2)}) %all-to-all-start.2) | async-done | bytes 1310752 | tf_op jit(solution)/shard_map/all_to_all | solution.py:347
  98.3 3.7 %shard_map.130 = (f32[1024,128]{1,0:T(8,128)S(1)}, f32[1024,128]{1,0:T(8,128)S(1)}, f32[1024,128]{1,0:T(8,128)S(1)}) custom-call(bf16[1024,128]{1,0:T(8,128)(2,1)S(1)} %bitcast.62, bf16[2048,128]{1,0:T(8,128)(2,1)S(1)} %bitcast.66, bf16[2048,128]{1,0:T(8,128)(2,1)S(1)} %bitcast.65), custom_call_target="tpu_custom_call" | custom-call | flops 1610612736 | bytes 2883584 | tf_op jit(solution)/shard_map/pallas_call | solution.py:181
  102.1 4.0 %shard_map.131 = bf16[1024,128]{1,0:T(8,128)(2,1)S(1)} custom-call(bf16[1024,128]{1,0:T(8,128)(2,1)S(1)} %bitcast.63, bf16[2048,128]{1,0:T(8,128)(2,1)S(1)} %bitcast.61, bf16[2048,128]{1,0:T(8,128)(2,1)S(1)} %bitcast.60, s32[1024,1]{1,0:T(8,128)S(1)} %add.90.qpos_ref, f32[1024,128]{1,0:T(8,128)S(1)} %get-tuple-element.16.max_ref, ...), custom_call_target="tpu_custom_call" | custom-call | tf_op jit(solution)/shard_map/pallas_call | solution.py:204
  106.2 10.5 %all_to_all.26 = bf16[16,64,128]{2,1,0:T(8,128)(2,1)S(1)} all-to-all(bf16[16,64,128]{2,1,0:T(8,128)(2,1)S(1)} %bitcast.64), channel_id=1, replica_groups=mesh['dp'=2,'context'=16,'tensor'=4] {'context'}, dimensions={0} | all-to-all | bytes 524288 | tf_op jit(solution)/shard_map/all_to_all | solution.py:364
  116.8 0.8 copy.37
  (38 shorter events, 3.4 us)
Async XLA Ops:
  0.8 5.4 %collective-permute-start = (bf16[2,3,1024]{2,0,1:T(2,128)(2,1)S(1)}, bf16[2,3,1024]{2,0,1:T(2,128)(2,1)S(1)}, u32[]{:S(2)}, u32[]{:S(2)}) collective-permute-start(bf16[2,3,1024]{2,0,1:T(2,128)(2,1)S(1)} %slice.40), channel_id=1, source_target_pairs={{0,4},{4,8},{8,12},{12,16},{16,20},{20,24},{24,28},{28,32},{32,36}... | collective-permute-start | bytes 36872 | tf_op jit(solution)/shard_map/ppermute | solution.py:21
  6.2 0.6 copy-start.4
  30.3 9.4 %copy-start.1 = (bf16[128,1024]{1,0:T(8,128)(2,1)S(1)}, bf16[128,1024]{1,0:T(8,128)(2,1)}, u32[]{:S(2)}) copy-start(bf16[128,1024]{1,0:T(8,128)(2,1)} %param.24) | copy-start | bytes 786436
  34.9 4.9 %copy-start.2 = (bf16[128,1024]{1,0:T(8,128)(2,1)S(1)}, bf16[128,1024]{1,0:T(8,128)(2,1)}, u32[]{:S(2)}) copy-start(bf16[128,1024]{1,0:T(8,128)(2,1)} %param.25) | copy-start | bytes 786436
  34.9 17.6 %all-to-all-start.1 = ((bf16[4,128,1024]{2,1,0:T(8,128)(2,1)}), bf16[4,128,1024]{2,1,0:T(8,128)(2,1)S(1)}, u32[]{:S(2)}, u32[]{:S(2)}) async-start(bf16[4,128,1024]{2,1,0:T(8,128)(2,1)} %shard_map.128), calls=%async_computation.1 | async-start | bytes 2097152 | tf_op jit(solution)/shard_map/all_to_all | solution.py:324
  52.5 21.9 %all-to-all-start.3 = ((bf16[16,256,128]{2,1,0:T(8,128)(2,1)}), bf16[16,256,128]{2,1,0:T(8,128)(2,1)S(1)}, u32[]{:S(2)}, u32[]{:S(2)}) async-start(bf16[16,256,128]{2,1,0:T(8,128)(2,1)} %pad_maximum_fusion.1), calls=%async_computation.3 | async-start | bytes 2097152 | tf_op jit(solution)/shard_map/all_to_all | solution.py:274
  58.8 0.7 copy-start.3
  74.4 1.0 copy-start
  75.4 22.9 %all-to-all-start.2 = ((bf16[16,320,128]{2,1,0:T(8,128)(2,1)}), bf16[16,320,128]{2,1,0:T(8,128)(2,1)S(1)}, u32[]{:S(2)}, u32[]{:S(2)}) async-start(bf16[16,320,128]{2,1,0:T(8,128)(2,1)} %pad_maximum_fusion), calls=%async_computation.2 | async-start | bytes 2621440 | tf_op jit(solution)/shard_map/all_to_all | solution.py:347
